TPU v7x, 128 devices: a whole 4x4x4 slice. The times are simulated.
128 devices in a mesh: seq: 16 (over y, x), batch: 8 (over z, core).
Axes of the slice: x: 4, y: 4, z: 4, core: 2. Of those that a mesh axis runs over, the one named last changes fastest.
Arguments:
- ssm_input: bfloat16 [32768, 4096], P(('batch', 'seq')), parts along dimension 0, may hold values from -6 to 6
- gate_input: bfloat16 [32768, 4096], P(('batch', 'seq')), parts along dimension 0, may hold values from -6 to 6
- b_rows: bfloat16 [32768, 128], P(('batch', 'seq')), parts along dimension 0, may hold values from -6 to 6
- c_rows: bfloat16 [32768, 128], P(('batch', 'seq')), parts along dimension 0, may hold values from -6 to 6
- step_raw: float32 [32768, 64], P(('batch', 'seq')), parts along dimension 0, may hold values from -14 to 2
- step_bias: float32 [64], replicated, may hold values from -0.5 to 0.5
- rate_log: float32 [64], replicated, may hold values from -1.5 to 4
- skip_gain: float32 [64], replicated, may hold values from 0.5 to 2
- norm_gain: float32 [4096], replicated, may hold values from 0.5 to 1.5
- w_out: bfloat16 [4096, 4096], P(None, 'seq'), may hold values from -0.09375 to 0.09375
- residual: bfloat16 [32768, 4096], P(('batch', 'seq')), parts along dimension 0, may hold values from -6 to 6
- moe_gain: float32 [4096], replicated, may hold values from 0.5 to 1.5
- router: bfloat16 [4096, 16], replicated, may hold values from -0.09375 to 0.09375
- expert_ids: int32 [32768, 2], P(('batch', 'seq')), parts along dimension 0, may hold values from 0 to 15, all different within a row; in each aligned block of 256 rows (0 to 255, 256 to 511, ...) at most 48 rows name the same one
- w_gate: bfloat16 [16, 4096, 384], P('seq'), may hold values from -0.09375 to 0.09375
- w_up: bfloat16 [16, 4096, 384], P('seq'), may hold values from -0.09375 to 0.09375
- w_down: bfloat16 [16, 384, 4096], P('seq'), may hold values from -0.3125 to 0.3125
Outputs:
- layer_out: bfloat16 [32768, 4096], P(('batch', 'seq')), parts along dimension 0
There are 8 independent parts, one for each index of `batch`. A program takes and returns all parts, laid end to end along the dimension named above; an argument that names none is the same for every part. Nothing has to cross between parts.
Inputs may be any that keep to these rules, and one draw needn't show every extreme that they name: `expert_ids`: the 2 ids of a token differ. In the rows of one device (256 rows, aligned blocks), no expert is named by more than 48 rows, a bound that some block reaches.
All inputs are finite; a program needn't handle non-finite values.
Results may differ from a plain program's by a relative error of at most 0.008.
Values may be sent and summed in bfloat16 or wider, within the bound.
No kernel may reach another device: no remote copies, remote signals or barrier semaphores. Data moves between devices by JAX's collectives and lax.ppermute only.
A program may use at most 192 MiB of HBM per device.

v0:
```python
import jax
import jax.numpy as jnp
from jax import lax
from jax.sharding import PartitionSpec as P

GROUP = 256


def group_pass(carried, pieces):
    inputs, b_block, c_block, steps_h, logs_h = pieces
    running = jnp.cumsum(logs_h, axis=0)
    length = logs_h.shape[0]
    scores = jnp.dot(c_block, b_block.T, preferred_element_type=jnp.float32)
    causal = jnp.arange(length)[:, None] >= jnp.arange(length)[None, :]
    spread = running[:, None, :] - running[None, :, :]
    decays = jnp.exp(jnp.where(causal[:, :, None], spread, -jnp.inf))
    mixing = (scores[:, :, None] * decays * steps_h[None, :, :]).astype(jnp.bfloat16)
    intra = jnp.einsum("tsh,shp->thp", mixing, inputs, preferred_element_type=jnp.float32)
    c_wide = c_block.astype(jnp.float32)
    from_state = jnp.exp(running)[:, :, None] * jnp.einsum(
        "tn,hpn->thp", c_wide, carried, precision=lax.Precision.HIGHEST
    )
    departing_state = jnp.exp(running[-1][None, :] - running) * steps_h
    block_in = (departing_state[:, :, None] * b_block.astype(jnp.float32)[:, None, :]).astype(
        jnp.bfloat16
    )
    update = jnp.einsum("shn,shp->hpn", block_in, inputs, preferred_element_type=jnp.float32)
    new_carried = jnp.exp(running[-1])[:, None, None] * carried + update
    return (new_carried, intra + from_state)


def shards(
    ssm_input,
    gate_input,
    b_rows,
    c_rows,
    step_raw,
    step_bias,
    rate_log,
    skip_gain,
    norm_gain,
    w_out,
    residual,
    moe_gain,
    router,
    expert_ids,
    w_gate,
    w_up,
    w_down,
):
    tokens_here = ssm_input.shape[0]
    inner = ssm_input.shape[1]
    heads = rate_log.shape[0]
    head_width = inner // heads
    state_width = b_rows.shape[1]
    blocks = tokens_here // GROUP
    step_sizes = jax.nn.softplus(step_raw + step_bias[None, :])
    log_decay = -step_sizes * jnp.exp(rate_log)[None, :]
    inputs = ssm_input.reshape(tokens_here, heads, head_width)
    pieces = (
        inputs.reshape(blocks, GROUP, heads, head_width),
        b_rows.reshape(blocks, GROUP, state_width),
        c_rows.reshape(blocks, GROUP, state_width),
        step_sizes.reshape(blocks, GROUP, heads),
        log_decay.reshape(blocks, GROUP, heads),
    )
    start = jnp.zeros((heads, head_width, state_width), jnp.float32)
    segment_state, outputs = lax.scan(group_pass, start, pieces)
    slab_log = jnp.cumsum(log_decay, axis=0)
    slab_total = slab_log[-1]
    all_logs, every_state_list = (
        lax.all_gather(slab_total[None], "seq", axis=0, tiled=True),
        lax.all_gather(segment_state[None], "seq", axis=0, tiled=True),
    )
    position = lax.axis_index("seq")
    through = jnp.cumsum(all_logs, axis=0)
    before_me = lax.dynamic_index_in_dim(through - all_logs, position, 0, keepdims=False)
    earlier = (jnp.arange(all_logs.shape[0]) < position)[:, None]
    weights = jnp.exp(jnp.where(earlier, before_me[None, :] - through, -jnp.inf))
    entering = jnp.einsum(
        "jh,jhpn->hpn", weights, every_state_list, precision=lax.Precision.HIGHEST
    )
    c_wide = c_rows.astype(jnp.float32)
    arriving = jnp.exp(slab_log)[:, :, None] * jnp.einsum(
        "tn,hpn->thp", c_wide, entering, precision=lax.Precision.HIGHEST
    )
    ssm_out = (
        outputs.reshape(tokens_here, heads, head_width)
        + arriving
        + skip_gain[None, :, None] * inputs.astype(jnp.float32)
    )
    gated = ssm_out.reshape(tokens_here, inner) * jax.nn.silu(gate_input.astype(jnp.float32))
    normed = (
        gated
        * lax.rsqrt(jnp.mean(gated * gated, axis=1, keepdims=True) + 1e-05)
        * norm_gain[None, :]
    ).astype(jnp.bfloat16)
    columns = jnp.dot(
        lax.all_gather(normed, "seq", axis=0, tiled=True), w_out, preferred_element_type=jnp.float32
    ).astype(jnp.bfloat16)
    mixer_out = lax.all_to_all(columns, "seq", split_axis=0, concat_axis=1, tiled=True)
    hidden = (residual.astype(jnp.float32) + mixer_out.astype(jnp.float32)).astype(jnp.bfloat16)
    hidden_wide = hidden.astype(jnp.float32)
    moe_input = (
        hidden_wide
        * lax.rsqrt(jnp.mean(hidden_wide * hidden_wide, axis=1, keepdims=True) + 1e-05)
        * moe_gain[None, :]
    ).astype(jnp.bfloat16)
    logits = jnp.dot(moe_input, router, preferred_element_type=jnp.float32)
    chosen = jnp.take_along_axis(logits, expert_ids, axis=1)
    powers = jnp.exp(chosen)
    combine = powers / jnp.sum(powers, axis=1, keepdims=True)
    experts_all = lax.axis_size("seq")
    fanout = expert_ids.shape[1]
    capacity = tokens_here * fanout * 3 // (2 * experts_all)
    width = moe_input.shape[1]
    flat_ids = expert_ids.reshape(-1)
    one_hot = (flat_ids[:, None] == jnp.arange(experts_all, dtype=jnp.int32)[None, :]).astype(
        jnp.int32
    )
    running_count = jnp.cumsum(one_hot, axis=0)
    slot_of = jnp.sum(running_count * one_hot, axis=1) - 1
    target = flat_ids * capacity + slot_of
    repeated = jnp.repeat(moe_input, fanout, axis=0)
    departing_state = (
        jnp.zeros((experts_all * capacity, width), jnp.bfloat16).at[target].set(repeated)
    )
    departing_state = departing_state.reshape(experts_all, capacity, width)
    batch = lax.all_to_all(departing_state, "seq", split_axis=0, concat_axis=0, tiled=True)
    flat_rows = batch.reshape(-1, width)
    gate_part = jnp.dot(flat_rows, w_gate[0], preferred_element_type=jnp.float32)
    up_part = jnp.dot(flat_rows, w_up[0], preferred_element_type=jnp.float32)
    expert_hidden = (jax.nn.silu(gate_part) * up_part).astype(jnp.bfloat16)
    result = jnp.dot(expert_hidden, w_down[0], preferred_element_type=jnp.float32).astype(
        jnp.bfloat16
    )
    finished = result.reshape(batch.shape)
    returned = lax.all_to_all(finished, "seq", split_axis=0, concat_axis=0, tiled=True).reshape(
        experts_all * capacity, width
    )
    fetched = returned[target].astype(jnp.float32).reshape(tokens_here, fanout, width)
    total = hidden_wide + jnp.sum(combine[:, :, None] * fetched, axis=1)
    return total.astype(jnp.bfloat16)


def solution(mesh):
    in_specs = (
        P(("batch", "seq"), None),
        P(("batch", "seq"), None),
        P(("batch", "seq"), None),
        P(("batch", "seq"), None),
        P(("batch", "seq"), None),
        P(),
        P(),
        P(),
        P(),
        P(None, "seq"),
        P(("batch", "seq"), None),
        P(),
        P(),
        P(("batch", "seq"), None),
        P("seq", None, None),
        P("seq", None, None),
        P("seq", None, None),
    )
    out_specs = P(("batch", "seq"), None)
    return jax.shard_map(shards, mesh=mesh, in_specs=in_specs, out_specs=out_specs, check_vma=False)
```

profile of v0, /device:TPU:0, one launch (start us, length us, event | category | flops | bytes accessed | tf_op | source)
XLA Modules:
  0.0 798.5 jit_solution(825056761227957821)
XLA Ops:
  6.5 0.8 exp.45
  7.4 1.1 multiply_bitcast_fusion
  8.5 0.6 reduce-window.16
  9.1 0.2 slice_reduce_fusion
  9.3 0.1 bitcast_bitcast_fusion
  9.4 0.2 slice_reduce_fusion.2
  9.6 0.7 fusion.48
  10.4 4.1 copy.55
  14.5 5.1 add_bitcast_fusion
  19.6 21.3 %all-gather.1 = f32[16,1,64]{2,1,0:T(1,128)S(1)} all-gather(f32[1,1,64]{2,1,0:T(1,128)S(1)} %bitcast.127), channel_id=1, replica_groups=mesh['seq'=16,'batch'=8] {'seq'}, dimensions={0}, use_global_device_ids=true | all-gather | bytes 4352 | tf_op jit(solution)/shard_map/all_gather | solution.py:72
  41.0 0.1 exponential_bitcast_fusion
  41.1 0.7 copy.65
  41.8 0.7 iota_compare_fusion
  42.4 0.2 fusion.51
  42.6 3.8 fusion.36
  46.4 172.6 %all-gather.7.cloned.1.call-done = f32[1024,64,128]{2,1,0:T(8,128)} async-done(((f32[64,64,128]{2,1,0:T(8,128)}), f32[1024,64,128]{2,1,0:T(8,128)}) %all-gather.7.cloned.1.call-update) | async-done | bytes 33554448 | tf_op jit(solution)/shard_map/all_gather | solution.py:73
  219.1 45.7 %fusion = f32[64,1,64,128]{3,1,2,0:T(1,128)S(1)} fusion(f32[16,64,1,1]{0,2,3,1:T(1,128)S(1)} %copy-done.15, f32[16,64,64,128]{3,2,1,0:T(8,128)} %bitcast.110), kind=kOutput, calls=%fused_computation.3 | convolution fusion | flops 100663296 | bytes 35655680 | tf_op jit(solution)/shard_map/jh,jhpn->hpn/dot_general | solution.py:80
  264.8 1.8 fusion.38
  266.7 0.3 copy-done.8
  267.0 0.7 copy-done.10
  267.7 6.5 fusion.19
  274.2 5.7 copy.56
  279.9 4.5 multiply_reduce_fusion.1
  284.4 0.2 copy-done.7
  284.6 3.1 multiply_convert_fusion.4
  287.7 196.7 %all-gather.5.cloned.1.call-done = bf16[4096,4096]{1,0:T(8,128)(2,1)} async-done(((bf16[256,4096]{1,0:T(8,128)(2,1)}), bf16[4096,4096]{1,0:T(8,128)(2,1)}) %all-gather.5.cloned.1.call-update) | async-done | bytes 33554448 | tf_op jit(solution)/shard_map/all_gather | solution.py:99
  484.4 16.8 %convolution_convert_fusion.1 = bf16[4096,256]{1,0:T(8,128)(2,1)} fusion(bf16[4096,4096]{1,0:T(8,128)(2,1)} %all-gather.5.cloned.1.call-done, bf16[4096,256]{1,0:T(8,128)(2,1)} %param.26), kind=kOutput, calls=%fused_computation.21 | convolution fusion | flops 8590983168 | bytes 37748736 | tf_op jit(solution)/shard_map/dot_general | solution.py:98
  501.2 5.9 all-to-all-start
  507.1 0.1 copy.62
  507.3 0.1 eq.29
  507.4 0.1 eq.25
  507.6 1.2 reduce-window.24
  508.7 0.2 slice_reduce_fusion.1
  509.0 0.1 copy.61
  509.2 0.1 mul.206
  509.3 0.1 fusion.42
  509.4 29.1 %all-to-all-done = bf16[16,256,256]{2,1,0:T(8,128)(2,1)} async-done(((bf16[16,256,256]{2,1,0:T(8,128)(2,1)}), bf16[16,256,256]{2,1,0:T(8,128)(2,1)}, u32[]{:S(2)}, u32[]{:S(2)}) %all-to-all-start) | async-done | bytes 2097184 | tf_op jit(solution)/shard_map/all_to_all | solution.py:101
  538.5 2.0 convert_bitcast_fusion
  540.6 0.5 copy.70
  541.0 1.1 copy-done.9
  542.2 0.8 fusion.13
  543.0 1.3 copy-done.3
  544.3 0.6 fusion.15
  545.0 1.3 copy-done.5
  546.3 4.7 broadcast_in_dim.95
  551.0 7.2 reshape.210
  558.2 11.4 %scatter_custom_fusion = bf16[768,4096]{1,0:T(8,128)(2,1)} fusion(s32[512]{0:T(512)S(1)} %bitcast.124, bf16[512,4096]{1,0:T(8,128)(2,1)} %reshape.210, bf16[]{:T(256)} %constant.80.clone.1), kind=kCustom, calls=%fused_computation.47 | custom fusion | bytes 6291968 | tf_op jit(solution)/shard_map/scatter | solution.py:126
  569.6 77.2 %all_to_all.23 = bf16[16,48,4096]{2,1,0:T(8,128)(2,1)S(1)} all-to-all(bf16[16,48,4096]{2,1,0:T(8,128)(2,1)} %bitcast.111), channel_id=1, replica_groups=mesh['seq'=16,'batch'=8] {'seq'}, dimensions={0} | all-to-all | bytes 12582912 | tf_op jit(solution)/shard_map/all_to_all | solution.py:129
  646.8 3.4 fusion.26
  650.2 3.5 fusion.33
  653.7 5.4 convolution_convert_fusion
  659.1 4.8 all-to-all-start.2
  663.8 0.1 copy.58
  664.0 0.1 reshape.200
  664.2 0.6 fusion.52
  664.8 4.6 gather_fusion.1
  669.4 0.1 reshape.203
  669.5 0.1 copy.59
  669.7 0.1 copy.60
  669.8 84.3 %all-to-all-done.2 = bf16[16,48,4096]{2,1,0:T(8,128)(2,1)} async-done(((bf16[16,48,4096]{2,1,0:T(8,128)(2,1)}), bf16[16,48,4096]{2,1,0:T(8,128)(2,1)}, u32[]{:S(2)}, u32[]{:S(2)}) %all-to-all-start.2) | async-done | bytes 6291488 | tf_op jit(solution)/shard_map/all_to_all | solution.py:138
  754.1 12.2 %gather_fusion = bf16[512,4096]{1,0:T(8,128)(2,1)} fusion(bf16[768,4096]{1,0:T(8,128)(2,1)} %bitcast.27, s32[1024]{0:T(1024)S(1)} %pad_clamp_fusion), kind=kCustom, calls=%fused_computation | custom fusion | bytes 8390656 | tf_op jit(solution)/shard_map/gather | solution.py:141
  766.2 9.7 %reshape.191 = f32[256,2,4096]{2,1,0:T(2,128)} reshape(bf16[512,4096]{1,0:T(8,128)(2,1)} %gather_fusion) | data formatting | bytes 12582912 | tf_op jit(solution)/shard_map/convert_element_type | solution.py:141
  775.9 13.6 %multiply_reduce_fusion = f32[256,4096]{1,0:T(8,128)S(1)} fusion(f32[256,2,4096]{2,1,0:T(2,128)} %reshape.191, f32[256,2]{1,0:T(8,128)S(1)} %copy.60), kind=kLoop, calls=%fused_computation.7 | loop fusion | flops 3145728 | bytes 12584960 | tf_op jit(solution)/shard_map/reduce_sum | solution.py:142
  789.5 2.0 fusion.16
  (72 shorter events, 0.4 us)
Async XLA Ops:
  6.5 647.1 %copy-start = (bf16[1,384,4096]{2,1,0:T(8,128)(2,1)S(1)}, bf16[1,384,4096]{2,1,0:T(8,128)(2,1)}, u32[]{:S(2)}) copy-start(bf16[1,384,4096]{2,1,0:T(8,128)(2,1)} %param.33) | copy-start | bytes 9437188
  6.5 7.9 copy-start.12
  6.5 212.5 %all-gather.7.cloned.1.call-start = ((), (), s32[]{:S(2)}) async-start(), calls=%async_computation.4 | async-start | bytes 35651584 | tf_op jit(solution)/shard_map/all_gather | solution.py:73
  8.5 11.1 %copy-start.13 = (f32[256,64]{0,1:T(8,128)}, f32[256,64]{0,1:T(8,128)S(1)}, u32[]{:S(2)}) copy-start(f32[256,64]{0,1:T(8,128)S(1)} %get-tuple-element.32) | copy-start | bytes 196612
  9.4 10.1 %copy-start.16 = (f32[256,64]{0,1:T(8,128)}, f32[256,64]{0,1:T(8,128)S(1)}, u32[]{:S(2)}) copy-start(f32[256,64]{0,1:T(8,128)S(1)} %bitcast_bitcast_fusion) | copy-start | bytes 196612
  14.4 28.0 %copy-start.11 = (bf16[256,128]{1,0:T(8,128)(2,1)S(1)}, bf16[256,128]{1,0:T(8,128)(2,1)}, u32[]{:S(2)}) copy-start(bf16[256,128]{1,0:T(8,128)(2,1)} %param.20) | copy-start | bytes 196612
  19.6 464.8 %all-gather.5.cloned.1.call-start = ((), (), s32[]{:S(2)}) async-start(), calls=%async_computation.3 | async-start | bytes 35651584 | tf_op jit(solution)/shard_map/all_gather | solution.py:99
  42.6 176.5 %copy-start.15 = (f32[16,64,1,1]{0,2,3,1:T(1,128)S(1)}, f32[16,64,1,1]{0,2,3,1:T(1,128)}, u32[]{:S(2)}) copy-start(f32[16,64,1,1]{0,2,3,1:T(1,128)} %copy.65) | copy-start | bytes 12292
  219.1 47.6 %copy-start.17 = (f32[256,64]{0,1:T(8,128)S(1)}, f32[256,64]{0,1:T(8,128)}, u32[]{:S(2)}) copy-start(f32[256,64]{0,1:T(8,128)} %copy-done.16) | copy-start | bytes 196612
  219.1 47.6 %copy-start.19 = (pred[256,256]{1,0:T(8,128)(4,1)S(1)}, pred[256,256]{1,0:T(8,128)(4,1)}, u32[]{:S(2)}) copy-start(pred[256,256]{1,0:T(8,128)(4,1)} %iota_compare_fusion) | copy-start | bytes 196612
  219.1 47.6 %copy-start.20 = (f32[256,64]{0,1:T(8,128)S(1)}, f32[256,64]{0,1:T(8,128)}, u32[]{:S(2)}) copy-start(f32[256,64]{0,1:T(8,128)} %get-tuple-element.34) | copy-start | bytes 196612
  264.8 2.2 copy-start.8
  264.8 2.9 copy-start.10
  264.8 2.9 copy-start.14
  264.8 2.8 copy-start.26
  274.2 10.2 %copy-start.22 = (f32[4096]{0:T(1024)S(1)}, f32[4096]{0:T(1024)}, u32[]{:S(2)}) copy-start(f32[4096]{0:T(1024)} %param.25) | copy-start | bytes 49156
  279.9 4.5 copy-start.2
  279.9 4.7 copy-start.7
  501.2 5.9 copy-start.21
  501.2 37.3 %all-to-all-start = ((bf16[16,256,256]{2,1,0:T(8,128)(2,1)}), bf16[16,256,256]{2,1,0:T(8,128)(2,1)}, u32[]{:S(2)}, u32[]{:S(2)}) async-start(bf16[16,256,256]{2,1,0:T(8,128)(2,1)} %bitcast.120), calls=%async_computation | async-start | bytes 4194304 | tf_op jit(solution)/shard_map/all_to_all | solution.py:101
  540.6 1.6 copy-start.9
  542.1 2.2 copy-start.23
  543.0 1.3 copy-start.3
  545.0 1.3 copy-start.5
  569.6 77.2 %copy-start.24 = (bf16[1,4096,384]{2,1,0:T(8,128)(2,1)S(1)}, bf16[1,4096,384]{2,1,0:T(8,128)(2,1)}, u32[]{:S(2)}) copy-start(bf16[1,4096,384]{2,1,0:T(8,128)(2,1)} %param.31) | copy-start | bytes 9437188
  646.8 3.4 copy-start.25
  659.1 5.1 copy-start.6
  659.1 5.1 copy-start.18
  659.1 95.0 %all-to-all-start.2 = ((bf16[16,48,4096]{2,1,0:T(8,128)(2,1)}), bf16[16,48,4096]{2,1,0:T(8,128)(2,1)}, u32[]{:S(2)}, u32[]{:S(2)}) async-start(bf16[16,48,4096]{2,1,0:T(8,128)(2,1)} %bitcast.114), calls=%async_computation.2 | async-start | bytes 12582912 | tf_op jit(solution)/shard_map/all_to_all | solution.py:138
  775.9 13.6 %copy-start.4 = (bf16[256,4096]{1,0:T(8,128)(2,1)S(1)}, bf16[256,4096]{1,0:T(8,128)(2,1)}, u32[]{:S(2)}) copy-start(bf16[256,4096]{1,0:T(8,128)(2,1)} %copy-done.3) | copy-start | bytes 6291460
  775.9 15.6 %copy-start.1 = (bf16[1,384,4096]{2,1,0:T(8,128)(2,1)S(1)}, bf16[1,384,4096]{2,1,0:T(8,128)(2,1)}, u32[]{:S(2)}) copy-start(bf16[1,384,4096]{2,1,0:T(8,128)(2,1)} %param.33) | copy-start | bytes 9437188
Sparse Core Ops, SparseCore 0:
  19.7 199.3 all-gather.6
  287.8 196.5 all-gather.4
where the time goes:
time: 803 us; the launch traced here: 799 us
  waiting for transfers between devices  483 us (60%)
  blocking collectives  98.5 us (12%)
  matrix products  92.8 us (12%)
  local copies, waits for them, and re-layouts  68.3 us (9%)
  other arithmetic  31.4 us (4%)
  between operations  14 us (2%)
  starting transfers between devices  10.7 us (1%)
    all_gather x1, waiting for transfers between devices, shards(): lax.all_gather(normed, 'seq', axis=0, tiled=True)  197 us
    all_gather x1, waiting for transfers between devices, shards(): lax.all_gather(segment_state[None], 'seq', axis=0, tiled=True)  173 us
    all_to_all x1, waiting for transfers between devices, shards(): lax.all_to_all(finished, 'seq', split_axis=0, concat_axis=0, tiled=True)  84.3 us
    all_to_all x1, blocking collectives, shards(): lax.all_to_all(departing_state, 'seq', split_axis=0, concat_axis=0, tiled...  77.2 us
    dot_general x1, matrix products, shards(): jnp.einsum('jh,jhpn->hpn', weights, every_state_list, precision=lax.Preci...  45.7 us
    all_to_all x1, waiting for transfers between devices, shards(): lax.all_to_all(columns, 'seq', split_axis=0, concat_axis=1, tiled=True)  29.1 us
    all_gather x1, blocking collectives, shards(): lax.all_gather(slab_total[None], 'seq', axis=0, tiled=True)  21.3 us
    dot_general x1, matrix products, shards(): jnp.dot(lax.all_gather(normed, 'seq', axis=0, tiled=True), w_out, preferr...  16.8 us
  transfers between devices with their start and end apart: 4, of which 4 were waited for; matrix products, arithmetic and copies ran while one was open for 2% of the time, Pallas kernels for 0%

commit v1 on v0

--- a/solution.py
+++ b/solution.py
@@ -68,17 +68,25 @@
     segment_state, outputs = lax.scan(group_pass, start, pieces)
     slab_log = jnp.cumsum(log_decay, axis=0)
     slab_total = slab_log[-1]
-    all_logs, every_state_list = (
-        lax.all_gather(slab_total[None], "seq", axis=0, tiled=True),
-        lax.all_gather(segment_state[None], "seq", axis=0, tiled=True),
+    n_seq = lax.axis_size("seq")
+    per_chunk = heads // n_seq
+    flat_state = segment_state.reshape(heads, head_width * state_width)
+    packed = jnp.concatenate(
+        [flat_state, jnp.broadcast_to(slab_total[:, None], (heads, 128))], axis=1
+    ).reshape(n_seq, per_chunk, head_width * state_width + 128)
+    received = lax.all_to_all(packed, "seq", 0, 0, tiled=True)
+    slab_states = received[:, :, : head_width * state_width]
+    slab_totals = received[:, :, head_width * state_width]
+
+    def chain(entering_here, piece):
+        state_j, total_j = piece
+        return jnp.exp(total_j)[:, None] * entering_here + state_j, entering_here
+
+    _, entering_each = lax.scan(
+        chain, jnp.zeros((per_chunk, head_width * state_width), jnp.float32), (slab_states, slab_totals)
     )
-    position = lax.axis_index("seq")
-    through = jnp.cumsum(all_logs, axis=0)
-    before_me = lax.dynamic_index_in_dim(through - all_logs, position, 0, keepdims=False)
-    earlier = (jnp.arange(all_logs.shape[0]) < position)[:, None]
-    weights = jnp.exp(jnp.where(earlier, before_me[None, :] - through, -jnp.inf))
-    entering = jnp.einsum(
-        "jh,jhpn->hpn", weights, every_state_list, precision=lax.Precision.HIGHEST
+    entering = lax.all_to_all(entering_each, "seq", 0, 0, tiled=True).reshape(
+        heads, head_width, state_width
     )
     c_wide = c_rows.astype(jnp.float32)
     arriving = jnp.exp(slab_log)[:, :, None] * jnp.einsum(
@@ -95,10 +103,8 @@
         * lax.rsqrt(jnp.mean(gated * gated, axis=1, keepdims=True) + 1e-05)
         * norm_gain[None, :]
     ).astype(jnp.bfloat16)
-    columns = jnp.dot(
-        lax.all_gather(normed, "seq", axis=0, tiled=True), w_out, preferred_element_type=jnp.float32
-    ).astype(jnp.bfloat16)
-    mixer_out = lax.all_to_all(columns, "seq", split_axis=0, concat_axis=1, tiled=True)
+    w_full = lax.all_gather(w_out, "seq", axis=1, tiled=True)
+    mixer_out = jnp.dot(normed, w_full, preferred_element_type=jnp.float32).astype(jnp.bfloat16)
     hidden = (residual.astype(jnp.float32) + mixer_out.astype(jnp.float32)).astype(jnp.bfloat16)
     hidden_wide = hidden.astype(jnp.float32)
     moe_input = (

time: 803 us -> 554 us (0.69)
  waiting for transfers between devices: 483 us -> 252 us
  matrix products: 92.8 us -> 53.2 us
  other arithmetic: 31.4 us -> 57.2 us
  blocking collectives: 98.5 us -> 78.4 us
    all_gather x2 -> x1, waiting for transfers between devices: 369 us -> 89.5 us  [shards(): w_full = lax.all_gather(w_out, 'seq', axis=1, tiled=True)]
    all_to_all x1 -> x2, waiting for transfers between devices: 29.1 us -> 77.5 us  [the longest x1 40.7 us: shards(): lax.all_to_all(entering_each, 'seq', 0, 0, tiled=True)]
    dot_general x2 -> x1, matrix products: 62.5 us -> 19.4 us  [shards(): jnp.dot(normed, w_full, preferred_element_type=jnp.float32)]
    all_gather x1 -> x0, blocking collectives: 21.3 us -> none  [shards(): lax.all_gather(slab_total[None], 'seq', axis=0, tiled=True)]
    add x0 -> x16, other arithmetic: none -> 16.3 us  [chain(): return (jnp.exp(total_j)[:, None] * entering_here + state_j, entering_here)]
    dynamic_update_slice x0 -> x16, other arithmetic: none -> 11 us  [shards(): lax.scan(chain, jnp.zeros((per_chunk, head_width * state_width), jnp.floa...]
  transfers between devices with their start and end apart: 4 -> 4, of which waited for: 4 -> 4; matrix products, arithmetic and copies ran while one was open for 2% -> 13% of each run, Pallas kernels for 0% -> 0%
where the time goes in v1:
time: 554 us; the launch traced here: 548 us
  waiting for transfers between devices  252 us (45%)
  blocking collectives  78.4 us (14%)
  local copies, waits for them, and re-layouts  74.9 us (14%)
  other arithmetic  57.2 us (10%)
  matrix products  53.2 us (10%)
  starting transfers between devices  18.5 us (3%)
  between operations  14.1 us (3%)
    all_gather x1, waiting for transfers between devices, shards(): w_full = lax.all_gather(w_out, 'seq', axis=1, tiled=True)  89.5 us
    all_to_all x1, waiting for transfers between devices, shards(): lax.all_to_all(finished, 'seq', split_axis=0, concat_axis=0, tiled=True)  84 us
    all_to_all x1, blocking collectives, shards(): lax.all_to_all(departing_state, 'seq', split_axis=0, concat_axis=0, tiled...  78.4 us
    all_to_all x1, waiting for transfers between devices, shards(): lax.all_to_all(entering_each, 'seq', 0, 0, tiled=True)  40.7 us
    all_to_all x1, waiting for transfers between devices, shards(): received = lax.all_to_all(packed, 'seq', 0, 0, tiled=True)  36.7 us
    dot_general x1, matrix products, shards(): jnp.dot(normed, w_full, preferred_element_type=jnp.float32)  19.4 us
    add x16, other arithmetic, chain(): return (jnp.exp(total_j)[:, None] * entering_here + state_j, entering_here)  16.3 us
    reduce_sum x1, other arithmetic, shards(): total = hidden_wide + jnp.sum(combine[:, :, None] * fetched, axis=1)  13.6 us
  transfers between devices with their start and end apart: 4, of which 4 were waited for; matrix products, arithmetic and copies ran while one was open for 13% of the time, Pallas kernels for 0%

profile of v1, /device:TPU:0, one launch (start us, length us, event | category | flops | bytes accessed | tf_op | source)
XLA Modules:
  0.0 548.3 jit_solution(11514367973339552408)
XLA Ops:
  6.5 0.8 exp.52
  7.4 1.1 multiply_bitcast_fusion
  9.7 0.7 fusion.52
  10.4 4.1 copy.41
  14.5 5.1 add_bitcast_fusion
  19.6 3.1 concatenate.6
  22.8 3.5 pad_maximum_fusion
  26.3 7.2 %all-to-all-start = ((f32[16,4,8320]{2,1,0:T(4,128)}), f32[16,4,8320]{2,1,0:T(4,128)}, u32[]{:S(2)}, u32[]{:S(2)}) async-start(f32[16,4,8320]{2,1,0:T(4,128)} %pad_maximum_fusion), calls=%async_computation | async-start | bytes 4259840 | tf_op jit(solution)/shard_map/all_to_all | solution.py:77
  34.2 36.7 %all-to-all-done = f32[16,4,8320]{2,1,0:T(4,128)} async-done(((f32[16,4,8320]{2,1,0:T(4,128)}), f32[16,4,8320]{2,1,0:T(4,128)}, u32[]{:S(2)}, u32[]{:S(2)}) %all-to-all-start) | async-done | bytes 2129952 | tf_op jit(solution)/shard_map/all_to_all | solution.py:77
  71.0 0.8 slice.39
  71.9 3.2 slice.40
  75.1 27.7 %while.3 = (s32[]{:T(128)}, f32[4,8192]{1,0:T(4,128)S(1)}, f32[16,4,8192]{2,1,0:T(4,128)}, f32[16,4]{1,0:T(8,128)S(1)}, f32[16,4,8192]{2,1,0:T(4,128)}, /*index=5*/s32[]{:T(128)}, s32[]{:T(128)}) while((s32[]{:T(128)}, f32[4,8192]{1,0:T(4,128)S(1)}, f32[16,4,8192]{2,1,0:T(4,128)}, f32[16,4]{1,0:T(8,128)S(1)}, ...), condition=%wide.region_3.4_spmd.clone, body=%wide.region_2.3_spmd.clone.sunk | while | flops 131075 | bytes 656016 | solution.py:85
  75.8 1.0 bitcast_add_fusion.2
  76.8 0.7 bitcast_dynamic-update-slice_fusion.2
  77.5 1.0 bitcast_add_fusion.2
  78.6 0.7 bitcast_dynamic-update-slice_fusion.2
  79.3 1.0 bitcast_add_fusion.2
  80.3 0.7 bitcast_dynamic-update-slice_fusion.2
  81.0 1.0 bitcast_add_fusion.2
  82.0 0.7 bitcast_dynamic-update-slice_fusion.2
  82.7 1.0 bitcast_add_fusion.2
  83.7 0.7 bitcast_dynamic-update-slice_fusion.2
  84.4 1.0 bitcast_add_fusion.2
  85.5 0.7 bitcast_dynamic-update-slice_fusion.2
  86.2 1.0 bitcast_add_fusion.2
  87.2 0.7 bitcast_dynamic-update-slice_fusion.2
  87.9 1.0 bitcast_add_fusion.2
  88.9 0.7 bitcast_dynamic-update-slice_fusion.2
  89.6 1.0 bitcast_add_fusion.2
  91.4 1.0 bitcast_add_fusion.2
  93.1 1.0 bitcast_add_fusion.2
  94.8 1.0 bitcast_add_fusion.2
  96.6 1.0 bitcast_add_fusion.2
  98.3 1.0 bitcast_add_fusion.2
  100.0 1.0 bitcast_add_fusion.2
  101.8 1.0 bitcast_add_fusion.2
  102.8 6.3 %all-to-all-start.1 = ((f32[16,4,8192]{2,1,0:T(4,128)}), f32[16,4,8192]{2,1,0:T(4,128)}, u32[]{:S(2)}, u32[]{:S(2)}) async-start(f32[16,4,8192]{2,1,0:T(4,128)} %get-tuple-element.56), calls=%async_computation.1 | async-start | bytes 4194304 | tf_op jit(solution)/shard_map/all_to_all | solution.py:88
  109.5 1.2 reduce-window.24
  111.4 0.9 fusion.56
  112.3 3.8 fusion.41
  116.1 40.7 %all-to-all-done.1 = f32[16,4,8192]{2,1,0:T(4,128)} async-done(((f32[16,4,8192]{2,1,0:T(4,128)}), f32[16,4,8192]{2,1,0:T(4,128)}, u32[]{:S(2)}, u32[]{:S(2)}) %all-to-all-start.1) | async-done | bytes 2097184 | tf_op jit(solution)/shard_map/all_to_all | solution.py:88
  156.9 3.7 reshape.193
  160.5 3.5 fusion.43
  164.2 7.5 %fusion.22 = f32[256,64,64]{0,2,1:T(8,128)} fusion(f32[64,64,256]{2,1,0:T(8,128)S(1)} %fusion.43, f32[64,64,256]{2,1,0:T(8,128)S(1)} %copy-done.5, bf16[256,64,64]{0,2,1:T(8,128)(2,1)S(1)} %bitcast.113, f32[256,64]{0,1:T(8,128)S(1)} %get-tuple-element.103, f32[256,64]{0,1:T(8,128)S(1)} %copy-done.10, f32[256,256]{1,0:T(8,128)} %fusion.56, ...), kind=kOutput, calls=%fused_computation.39 | convolution fusion | flops 565182464 | bytes 15204608 | tf_op jit(solution)/shard_map/while/body/eval_jaxpr/tsh,shp->thp/dot_general | solution.py:18
  171.7 5.6 %copy.44 = f32[256,4096]{1,0:T(8,128)} copy(f32[256,4096]{0,1:T(8,128)} %bitcast.111) | data formatting | bytes 8388608 | tf_op jit(solution)/shard_map/reshape | solution.py:100
  177.3 4.7 multiply_reduce_fusion.1
  182.0 89.5 %all-gather.2.cloned.1.call-done = bf16[4096,4096]{1,0:T(8,128)(2,1)} async-done(((bf16[4096,256]{1,0:T(8,128)(2,1)}), bf16[4096,4096]{1,0:T(8,128)(2,1)}) %all-gather.2.cloned.1.call-update) | async-done | bytes 33554448 | tf_op jit(solution)/shard_map/all_gather | solution.py:106
  271.5 19.4 %fusion.16 = (f32[256]{0:T(256)S(1)}, bf16[256,4096]{1,0:T(8,128)(2,1)}) fusion(bf16[4096,4096]{1,0:T(8,128)(2,1)} %all-gather.2.cloned.1.call-done, f32[4096]{0:T(1024)S(1)} %copy-done.17, f32[256]{0:T(256)S(1)} %add_rsqrt_fusion.1, f32[256,4096]{1,0:T(8,128)} %copy.44, bf16[256,4096]{1,0:T(8,128)(2,1)} %param.20, bf16[256,4096]{1,0:T(8,128)(2,1)} %param.29), kind=kOutput, calls=%fused_computation.32 | convolution fusion | flops 8607760384 | bytes 44058624 | tf_op jit(solution)/shard_map/dot_general | solution.py:107
  290.8 2.2 fusion.18
  293.1 1.4 copy-done.2
  294.4 4.7 broadcast_in_dim.97
  299.1 7.2 %reshape.221 = bf16[512,4096]{1,0:T(8,128)(2,1)} reshape(bf16[256,2,4096]{2,1,0:T(2,128)(2,1)} %broadcast_in_dim.97) | data formatting | bytes 8388608 | tf_op jit(solution)/shard_map/reshape | solution.py:130
  306.3 11.6 %scatter_custom_fusion = bf16[768,4096]{1,0:T(8,128)(2,1)} fusion(s32[512]{0:T(512)S(1)} %bitcast.115, bf16[512,4096]{1,0:T(8,128)(2,1)} %reshape.221, bf16[]{:T(256)} %constant.79.clone.1), kind=kCustom, calls=%fused_computation.51 | custom fusion | bytes 6291968 | tf_op jit(solution)/shard_map/scatter | solution.py:132
  317.9 78.4 %all_to_all.20 = bf16[16,48,4096]{2,1,0:T(8,128)(2,1)S(1)} all-to-all(bf16[16,48,4096]{2,1,0:T(8,128)(2,1)} %bitcast.107), channel_id=1, replica_groups=mesh['seq'=16,'batch'=8] {'seq'}, dimensions={0} | all-to-all | bytes 12582912 | tf_op jit(solution)/shard_map/all_to_all | solution.py:135
  396.4 3.4 fusion.29
  399.8 3.5 fusion.38
  403.3 5.4 convolution_convert_fusion
  408.7 5.0 all-to-all-start.3
  414.7 4.6 gather_fusion.1
  419.7 84.0 %all-to-all-done.3 = bf16[16,48,4096]{2,1,0:T(8,128)(2,1)} async-done(((bf16[16,48,4096]{2,1,0:T(8,128)(2,1)}), bf16[16,48,4096]{2,1,0:T(8,128)(2,1)}, u32[]{:S(2)}, u32[]{:S(2)}) %all-to-all-start.3) | async-done | bytes 6291488 | tf_op jit(solution)/shard_map/all_to_all | solution.py:144
  503.8 12.2 %gather_fusion = bf16[512,4096]{1,0:T(8,128)(2,1)} fusion(bf16[768,4096]{1,0:T(8,128)(2,1)} %bitcast.20, s32[1024]{0:T(1024)S(1)} %pad_clamp_fusion), kind=kCustom, calls=%fused_computation | custom fusion | bytes 8390656 | tf_op jit(solution)/shard_map/gather | solution.py:147
  515.9 9.6 %reshape.202 = f32[256,2,4096]{2,1,0:T(2,128)} reshape(bf16[512,4096]{1,0:T(8,128)(2,1)} %gather_fusion) | data formatting | bytes 12582912 | tf_op jit(solution)/shard_map/convert_element_type | solution.py:147
  525.6 13.6 %multiply_reduce_fusion = f32[256,4096]{1,0:T(8,128)S(1)} fusion(f32[256,2,4096]{2,1,0:T(2,128)} %reshape.202, f32[256,2]{1,0:T(8,128)S(1)} %copy.47), kind=kLoop, calls=%fused_computation.10 | loop fusion | flops 3145728 | bytes 12584960 | tf_op jit(solution)/shard_map/reduce_sum | solution.py:148
  539.2 2.0 fusion.19
  (104 shorter events, 10.3 us)
Async XLA Ops:
  6.5 396.7 %copy-start = (bf16[1,384,4096]{2,1,0:T(8,128)(2,1)S(1)}, bf16[1,384,4096]{2,1,0:T(8,128)(2,1)}, u32[]{:S(2)}) copy-start(bf16[1,384,4096]{2,1,0:T(8,128)(2,1)} %param.35) | copy-start | bytes 9437188
  6.5 8.0 %copy-start.8 = (bf16[256,128]{1,0:T(8,128)(2,1)S(1)}, bf16[256,128]{1,0:T(8,128)(2,1)}, u32[]{:S(2)}) copy-start(bf16[256,128]{1,0:T(8,128)(2,1)} %param.21) | copy-start | bytes 196612
  9.4 10.2 %copy-start.9 = (f32[256,64]{0,1:T(8,128)}, f32[256,64]{0,1:T(8,128)S(1)}, u32[]{:S(2)}) copy-start(f32[256,64]{0,1:T(8,128)S(1)} %bitcast_bitcast_fusion) | copy-start | bytes 196612
  26.3 44.7 %all-to-all-start = ((f32[16,4,8320]{2,1,0:T(4,128)}), f32[16,4,8320]{2,1,0:T(4,128)}, u32[]{:S(2)}, u32[]{:S(2)}) async-start(f32[16,4,8320]{2,1,0:T(4,128)} %pad_maximum_fusion), calls=%async_computation | async-start | bytes 4259840 | tf_op jit(solution)/shard_map/all_to_all | solution.py:77
  33.5 238.0 %all-gather.2.cloned.1.call-start = ((), (), s32[]{:S(2)}) async-start(), calls=%async_computation.4 | async-start | bytes 35651584 | tf_op jit(solution)/shard_map/all_gather | solution.py:106
  75.1 34.0 %copy-start.13 = (s32[256,2]{0,1:T(2,128)S(1)}, s32[256,2]{0,1:T(2,128)}, u32[]{:S(2)}) copy-start(s32[256,2]{0,1:T(2,128)} %param.32) | copy-start | bytes 6148
  75.1 36.3 %copy-start.7 = (bf16[256,128]{1,0:T(8,128)(2,1)S(1)}, bf16[256,128]{1,0:T(8,128)(2,1)}, u32[]{:S(2)}) copy-start(bf16[256,128]{1,0:T(8,128)(2,1)} %param.22) | copy-start | bytes 196612
  102.8 54.1 %all-to-all-start.1 = ((f32[16,4,8192]{2,1,0:T(4,128)}), f32[16,4,8192]{2,1,0:T(4,128)}, u32[]{:S(2)}, u32[]{:S(2)}) async-start(f32[16,4,8192]{2,1,0:T(4,128)} %get-tuple-element.56), calls=%async_computation.1 | async-start | bytes 4194304 | tf_op jit(solution)/shard_map/all_to_all | solution.py:88
  156.9 7.3 %copy-start.12 = (f32[256,64]{0,1:T(8,128)S(1)}, f32[256,64]{0,1:T(8,128)}, u32[]{:S(2)}) copy-start(f32[256,64]{0,1:T(8,128)} %get-tuple-element.104) | copy-start | bytes 196612
  160.5 3.6 copy-start.5
  160.5 3.6 copy-start.6
  160.5 3.6 copy-start.10
  160.5 3.6 copy-start.18
  177.3 94.1 %copy-start.17 = (f32[4096]{0:T(1024)S(1)}, f32[4096]{0:T(1024)}, u32[]{:S(2)}) copy-start(f32[4096]{0:T(1024)} %param.27) | copy-start | bytes 49156
  182.0 108.8 %copy-start.14 = (f32[4096]{0:T(1024)S(1)}, f32[4096]{0:T(1024)}, u32[]{:S(2)}) copy-start(f32[4096]{0:T(1024)} %param.30) | copy-start | bytes 49156
  293.1 1.4 copy-start.2
  317.9 78.5 %copy-start.15 = (bf16[1,4096,384]{2,1,0:T(8,128)(2,1)S(1)}, bf16[1,4096,384]{2,1,0:T(8,128)(2,1)}, u32[]{:S(2)}) copy-start(bf16[1,4096,384]{2,1,0:T(8,128)(2,1)} %param.33) | copy-start | bytes 9437188
  396.4 3.4 copy-start.16
  408.7 5.3 copy-start.3
  408.7 5.4 copy-start.11
  408.7 95.0 %all-to-all-start.3 = ((bf16[16,48,4096]{2,1,0:T(8,128)(2,1)}), bf16[16,48,4096]{2,1,0:T(8,128)(2,1)}, u32[]{:S(2)}, u32[]{:S(2)}) async-start(bf16[16,48,4096]{2,1,0:T(8,128)(2,1)} %bitcast.108), calls=%async_computation.3 | async-start | bytes 12582912 | tf_op jit(solution)/shard_map/all_to_all | solution.py:144
  525.5 13.6 %copy-start.4 = (bf16[256,4096]{1,0:T(8,128)(2,1)S(1)}, bf16[256,4096]{1,0:T(8,128)(2,1)}, u32[]{:S(2)}) copy-start(bf16[256,4096]{1,0:T(8,128)(2,1)} %get-tuple-element.107) | copy-start | bytes 6291460
  525.6 15.6 %copy-start.1 = (bf16[1,384,4096]{2,1,0:T(8,128)(2,1)S(1)}, bf16[1,384,4096]{2,1,0:T(8,128)(2,1)}, u32[]{:S(2)}) copy-start(bf16[1,384,4096]{2,1,0:T(8,128)(2,1)} %param.35) | copy-start | bytes 9437188
Sparse Core Ops, SparseCore 0:
  36.4 235.0 all-gather.1

commit v2 on v1

--- a/solution.py
+++ b/solution.py
@@ -78,13 +78,12 @@
     slab_states = received[:, :, : head_width * state_width]
     slab_totals = received[:, :, head_width * state_width]
 
-    def chain(entering_here, piece):
-        state_j, total_j = piece
-        return jnp.exp(total_j)[:, None] * entering_here + state_j, entering_here
-
-    _, entering_each = lax.scan(
-        chain, jnp.zeros((per_chunk, head_width * state_width), jnp.float32), (slab_states, slab_totals)
-    )
+    entering_here = jnp.zeros((per_chunk, head_width * state_width), jnp.float32)
+    entering_list = []
+    for j in range(n_seq):
+        entering_list.append(entering_here)
+        entering_here = jnp.exp(slab_totals[j])[:, None] * entering_here + slab_states[j]
+    entering_each = jnp.stack(entering_list)
     entering = lax.all_to_all(entering_each, "seq", 0, 0, tiled=True).reshape(
         heads, head_width, state_width
     )
@@ -103,8 +102,29 @@
         * lax.rsqrt(jnp.mean(gated * gated, axis=1, keepdims=True) + 1e-05)
         * norm_gain[None, :]
     ).astype(jnp.bfloat16)
-    w_full = lax.all_gather(w_out, "seq", axis=1, tiled=True)
-    mixer_out = jnp.dot(normed, w_full, preferred_element_type=jnp.float32).astype(jnp.bfloat16)
+    n_batch = lax.axis_size("batch")
+    core = lax.axis_index("batch") % 2
+    shard_cols = w_out.shape[1]
+    half = shard_cols // 2
+    w_half = lax.all_gather(
+        lax.dynamic_slice_in_dim(w_out, core * half, half, axis=1), "seq", axis=1, tiled=True
+    )
+    partners = [(b, b ^ 1) for b in range(n_batch)]
+    normed_partner = lax.ppermute(normed, "batch", partners)
+    own_half = jnp.dot(normed, w_half, preferred_element_type=jnp.float32).astype(jnp.bfloat16)
+    partner_half = jnp.dot(normed_partner, w_half, preferred_element_type=jnp.float32).astype(
+        jnp.bfloat16
+    )
+    other_half = lax.ppermute(partner_half, "batch", partners)
+    first_half = jnp.where(core == 0, own_half, other_half)
+    second_half = jnp.where(core == 0, other_half, own_half)
+    mixer_out = jnp.stack(
+        [
+            first_half.reshape(tokens_here, n_seq, half),
+            second_half.reshape(tokens_here, n_seq, half),
+        ],
+        axis=2,
+    ).reshape(tokens_here, n_seq * shard_cols)
     hidden = (residual.astype(jnp.float32) + mixer_out.astype(jnp.float32)).astype(jnp.bfloat16)
     hidden_wide = hidden.astype(jnp.float32)
     moe_input = (
@@ -127,10 +147,15 @@
     running_count = jnp.cumsum(one_hot, axis=0)
     slot_of = jnp.sum(running_count * one_hot, axis=1) - 1
     target = flat_ids * capacity + slot_of
-    repeated = jnp.repeat(moe_input, fanout, axis=0)
-    departing_state = (
-        jnp.zeros((experts_all * capacity, width), jnp.bfloat16).at[target].set(repeated)
-    )
+    slots = experts_all * capacity
+    target_pairs = target.reshape(tokens_here, fanout)
+    slot_ids = jnp.arange(slots, dtype=jnp.int32)
+    placing = jnp.zeros((slots, tokens_here), jnp.bool_)
+    for k in range(fanout):
+        placing = placing | (slot_ids[:, None] == target_pairs[None, :, k])
+    departing_state = jnp.dot(
+        placing.astype(jnp.bfloat16), moe_input, preferred_element_type=jnp.float32
+    ).astype(jnp.bfloat16)
     departing_state = departing_state.reshape(experts_all, capacity, width)
     batch = lax.all_to_all(departing_state, "seq", split_axis=0, concat_axis=0, tiled=True)
     flat_rows = batch.reshape(-1, width)
@@ -144,8 +169,11 @@
     returned = lax.all_to_all(finished, "seq", split_axis=0, concat_axis=0, tiled=True).reshape(
         experts_all * capacity, width
     )
-    fetched = returned[target].astype(jnp.float32).reshape(tokens_here, fanout, width)
-    total = hidden_wide + jnp.sum(combine[:, :, None] * fetched, axis=1)
+    total = hidden_wide
+    for k in range(fanout):
+        picking = (target_pairs[:, k][:, None] == slot_ids[None, :]).astype(jnp.bfloat16)
+        fetched = jnp.dot(picking, returned, preferred_element_type=jnp.float32)
+        total = total + combine[:, k][:, None] * fetched
     return total.astype(jnp.bfloat16)
 
 

time: 554 us -> 439 us (0.79)
  waiting for transfers between devices: 252 us -> 170 us
  local copies, waits for them, and re-layouts: 74.9 us -> 40.1 us
  matrix products: 53.2 us -> 65.4 us
  other arithmetic: 57.2 us -> 46.8 us
    all_gather x1, waiting for transfers between devices: 89.5 us -> 12.5 us  [shards(): lax.all_gather(lax.dynamic_slice_in_dim(w_out, core * half, half, axis=1)...]
    unnamed x2 -> x16, other arithmetic: 1.12 us -> 25.3 us
    add x16 -> x1, other arithmetic: 16.3 us -> 0.01 us  [shards(): target = flat_ids * capacity + slot_of]
    gather x1 -> x0, local copies, waits for them, and re-layouts: 12.2 us -> none  [shards(): returned[target].astype(jnp.float32).reshape(tokens_here, fanout, width)]
    scatter x1 -> x0, local copies, waits for them, and re-layouts: 11.6 us -> none  [shards(): jnp.zeros((experts_all * capacity, width), jnp.bfloat16).at[target]]
    dot_general x1 -> x5, matrix products: 19.4 us -> 30.8 us  [the longest x2 11.4 us: shards(): fetched = jnp.dot(picking, returned, preferred_element_type=jnp.float32)]
    dynamic_update_slice x16 -> x0, other arithmetic: 11 us -> none  [shards(): lax.scan(chain, jnp.zeros((per_chunk, head_width * state_width), jnp.floa...]
    reduce_sum x1, other arithmetic: 13.6 us -> 3.71 us  [shards(): jnp.mean(hidden_wide * hidden_wide, axis=1, keepdims=True) + 1e-05]
  transfers between devices with their start and end apart: 4 -> 6, of which waited for: 4 -> 5; matrix products, arithmetic and copies ran while one was open for 13% -> 18% of each run, Pallas kernels for 0% -> 0%
where the time goes in v2:
time: 439 us; the launch traced here: 434 us
  waiting for transfers between devices  170 us (39%)
  blocking collectives  79.6 us (18%)
  matrix products  65.4 us (15%)
  other arithmetic  46.8 us (11%)
  local copies, waits for them, and re-layouts  40.1 us (9%)
  starting transfers between devices  17.7 us (4%)
  between operations  14 us (3%)
    all_to_all x1, waiting for transfers between devices, shards(): lax.all_to_all(finished, 'seq', split_axis=0, concat_axis=0, tiled=True)  85.1 us
    all_to_all x1, blocking collectives, shards(): lax.all_to_all(departing_state, 'seq', split_axis=0, concat_axis=0, tiled...  79.6 us
    all_to_all x1, waiting for transfers between devices, shards(): lax.all_to_all(entering_each, 'seq', 0, 0, tiled=True)  38.7 us
    all_to_all x1, waiting for transfers between devices, shards(): received = lax.all_to_all(packed, 'seq', 0, 0, tiled=True)  31.5 us
    unnamed x16, other arithmetic  25.3 us
    all_gather x1, waiting for transfers between devices, shards(): lax.all_gather(lax.dynamic_slice_in_dim(w_out, core * half, half, axis=1)...  12.5 us
    convert_element_type x2, local copies, waits for them, and re-layouts, shards(): mixer_out.astype(jnp.float32)  11.6 us
    dot_general x2, matrix products, shards(): fetched = jnp.dot(picking, returned, preferred_element_type=jnp.float32)  11.4 us
  transfers between devices with their start and end apart: 6, of which 5 were waited for; matrix products, arithmetic and copies ran while one was open for 18% of the time, Pallas kernels for 0%

profile of v2, /device:TPU:0, one launch (start us, length us, event | category | flops | bytes accessed | tf_op | source)
XLA Modules:
  0.0 433.8 jit_solution(6942577916162186558)
XLA Ops:
  6.5 0.8 exp.188
  7.3 1.1 multiply_bitcast_fusion
  8.5 0.6 reduce-window.16
  9.4 0.6 copy-done.10
  10.3 0.7 fusion.71
  11.0 4.1 copy.143
  15.1 5.1 %add_bitcast_fusion = f32[64,64,128]{2,1,0:T(8,128)} fusion(bf16[256,64,64]{0,2,1:T(8,128)(2,1)} %bitcast.117, f32[256,128]{1,0:T(8,128)S(1)} %convert_element_type.70, f32[256,64]{0,1:T(8,128)S(1)} %get-tuple-element.65, f32[64]{0:T(128)S(1)} %exponential_multiply_fusion.1), kind=kOutput, calls=%fused_computation.48 | convolution fusion | flops 273154048 | bytes 4391168 | tf_op jit(solution)/shard_map/while/body/eval_jaxpr/shn,shp->hpn/dot_general | solution.py:27
  20.2 3.1 concatenate.6
  23.4 3.4 pad_maximum_fusion
  26.8 7.2 %all-to-all-start = ((f32[16,4,8320]{2,1,0:T(4,128)}), f32[16,4,8320]{2,1,0:T(4,128)}, u32[]{:S(2)}, u32[]{:S(2)}) async-start(f32[16,4,8320]{2,1,0:T(4,128)} %pad_maximum_fusion), calls=%async_computation | async-start | bytes 4259840 | tf_op jit(solution)/shard_map/all_to_all | solution.py:77
  34.1 2.3 constant_dynamic-slice_fusion
  36.4 0.7 broadcast_dynamic-update-slice_fusion
  37.1 31.5 %all-to-all-done = f32[16,4,8320]{2,1,0:T(4,128)} async-done(((f32[16,4,8320]{2,1,0:T(4,128)}), f32[16,4,8320]{2,1,0:T(4,128)}, u32[]{:S(2)}, u32[]{:S(2)}) %all-to-all-start) | async-done | bytes 2129952 | tf_op jit(solution)/shard_map/all_to_all | solution.py:77
  68.6 1.1 fusion.53
  69.7 1.7 fusion.45
  71.4 1.7 constant_dynamic-update-slice_fusion.12
  73.1 1.8 constant_dynamic-update-slice_fusion.11
  74.9 1.9 constant_dynamic-update-slice_fusion.10
  76.8 1.7 constant_dynamic-update-slice_fusion.9
  78.5 1.8 constant_dynamic-update-slice_fusion.8
  80.2 1.7 constant_dynamic-update-slice_fusion.7
  81.9 1.7 constant_dynamic-update-slice_fusion.6
  83.6 1.7 constant_dynamic-update-slice_fusion.5
  85.3 1.7 constant_dynamic-update-slice_fusion.4
  87.0 1.7 constant_dynamic-update-slice_fusion.3
  88.7 1.7 constant_dynamic-update-slice_fusion.2
  90.4 1.7 constant_dynamic-update-slice_fusion.1
  92.1 1.8 constant_dynamic-update-slice_fusion
  93.8 1.7 fusion.44
  95.5 5.3 %all-to-all-start.1 = ((f32[16,4,8192]{2,1,0:T(4,128)}), f32[16,4,8192]{2,1,0:T(4,128)}, u32[]{:S(2)}, u32[]{:S(2)}) async-start(f32[16,4,8192]{2,1,0:T(4,128)} %fusion.44), calls=%async_computation.1 | async-start | bytes 4194304 | tf_op jit(solution)/shard_map/all_to_all | solution.py:87
  100.8 0.7 iota_compare_fusion.7
  101.6 3.7 fusion.33
  105.4 38.7 %all-to-all-done.1 = f32[16,4,8192]{2,1,0:T(4,128)} async-done(((f32[16,4,8192]{2,1,0:T(4,128)}), f32[16,4,8192]{2,1,0:T(4,128)}, u32[]{:S(2)}, u32[]{:S(2)}) %all-to-all-start.1) | async-done | bytes 2097184 | tf_op jit(solution)/shard_map/all_to_all | solution.py:87
  144.0 3.7 reshape.1062
  147.8 3.6 fusion.46
  151.6 7.4 %fusion.18 = f32[256,64,64]{0,2,1:T(8,128)} fusion(f32[64,64,256]{2,1,0:T(8,128)S(1)} %fusion.46, f32[64,64,256]{2,1,0:T(8,128)S(1)} %copy-done.4, bf16[256,64,64]{0,2,1:T(8,128)(2,1)S(1)} %bitcast.118, f32[256,64]{0,1:T(8,128)S(1)} %copy-done.9, f32[256,64]{0,1:T(8,128)S(1)} %copy-done.11, f32[256,256]{1,0:T(8,128)S(1)} %fusion.76, ...), kind=kOutput, calls=%fused_computation.31 | convolution fusion | flops 565182464 | bytes 15204608 | tf_op jit(solution)/shard_map/while/body/eval_jaxpr/tsh,shp->thp/dot_general | solution.py:18
  159.0 5.6 %copy.144 = f32[256,4096]{1,0:T(8,128)} copy(f32[256,4096]{0,1:T(8,128)} %bitcast.114) | data formatting | bytes 8388608 | tf_op jit(solution)/shard_map/reshape | solution.py:99
  164.6 4.7 %multiply_reduce_fusion = f32[256]{0:T(256)S(1)} fusion(f32[256,4096]{1,0:T(8,128)} %copy.144, bf16[256,4096]{1,0:T(8,128)(2,1)} %param.18), kind=kLoop, calls=%fused_computation.36 | loop fusion | flops 8388352 | bytes 6292480 | tf_op jit(solution)/shard_map/reduce_sum | solution.py:102
  169.3 0.4 copy-done.3
  169.7 3.1 multiply_convert_fusion.4
  172.8 0.4 collective-permute-start
  173.7 1.2 reduce-window.24
  174.8 0.2 slice_reduce_fusion.1
  175.4 2.3 collective-permute-done
  177.7 12.5 %all-gather.2.cloned.1.call-done = bf16[4096,2048]{1,0:T(8,128)(2,1)} async-done(((bf16[4096,128]{1,0:T(8,128)(2,1)}), bf16[4096,2048]{1,0:T(8,128)(2,1)}) %all-gather.2.cloned.1.call-update) | async-done | bytes 16777232 | tf_op jit(solution)/shard_map/all_gather | solution.py:109
  190.2 11.0 %convolution_convert_fusion.2 = bf16[256,2048]{1,0:T(8,128)(2,1)S(1)} fusion(bf16[256,4096]{1,0:T(8,128)(2,1)} %collective-permute-done, bf16[4096,2048]{1,0:T(8,128)(2,1)} %all-gather.2.cloned.1.call-done), kind=kOutput, calls=%fused_computation.44 | convolution fusion | flops 4295491584 | bytes 19922944 | tf_op jit(solution)/shard_map/dot_general | solution.py:115
  201.3 6.3 %convolution_convert_fusion.3 = bf16[256,2048]{1,0:T(8,128)(2,1)S(1)} fusion(bf16[256,4096]{1,0:T(8,128)(2,1)} %multiply_convert_fusion.4, bf16[4096,2048]{1,0:T(8,128)(2,1)S(1)} %copy-done.15), kind=kOutput, calls=%fused_computation.45 | convolution fusion | flops 4295491584 | bytes 19922944 | tf_op jit(solution)/shard_map/dot_general | solution.py:114
  207.8 0.2 copy.155
  208.0 0.2 copy.156
  208.2 0.3 maximum_convert_fusion
  208.5 5.2 %copy.145 = f32[256,16,2,128]{3,2,1,0:T(2,128)} copy(f32[256,16,2,128]{3,1,0,2:T(8,128)S(1)} %maximum_convert_fusion) | data formatting | bytes 8388608 | tf_op jit(solution)/shard_map/convert_element_type | solution.py:128
  213.7 6.4 %reshape.1070 = f32[256,4096]{1,0:T(8,128)} reshape(f32[256,16,2,128]{3,2,1,0:T(2,128)} %copy.145) | data formatting | bytes 8388608 | tf_op jit(solution)/shard_map/convert_element_type | solution.py:128
  220.2 3.7 fusion.13
  223.9 2.0 convolution_convert_fusion
  226.0 79.6 %all_to_all.20 = bf16[16,48,4096]{2,1,0:T(8,128)(2,1)S(1)} all-to-all(bf16[16,48,4096]{2,1,0:T(8,128)(2,1)S(1)} %bitcast.110), channel_id=1, replica_groups=mesh['seq'=16,'batch'=8] {'seq'}, dimensions={0} | all-to-all | bytes 12582912 | tf_op jit(solution)/shard_map/all_to_all | solution.py:160
  305.6 3.4 fusion.25
  309.0 3.5 fusion.30
  312.5 5.4 %convolution_convert_fusion.1 = bf16[768,4096]{1,0:T(8,128)(2,1)} fusion(bf16[768,384]{1,0:T(8,128)(2,1)S(1)} %fusion.30, bf16[1,384,4096]{2,1,0:T(8,128)(2,1)S(1)} %copy-done), kind=kOutput, calls=%fused_computation.11 | convolution fusion | flops 2419064832 | bytes 10027008 | tf_op jit(solution)/shard_map/dot_general | solution.py:165
  317.9 4.8 %all-to-all-start.3 = ((bf16[16,48,4096]{2,1,0:T(8,128)(2,1)}), bf16[16,48,4096]{2,1,0:T(8,128)(2,1)}, u32[]{:S(2)}, u32[]{:S(2)}) async-start(bf16[16,48,4096]{2,1,0:T(8,128)(2,1)} %bitcast.111), calls=%async_computation.3 | async-start | bytes 12582912 | tf_op jit(solution)/shard_map/all_to_all | solution.py:169
  323.0 2.3 fusion.38
  325.3 4.6 %gather_fusion = f32[512]{0:T(512)S(1)} fusion(f32[256,16]{0,1:T(8,128)S(1)} %fusion.38, s32[512]{0:T(512)S(1)} %reshape.1071), kind=kCustom, calls=%fused_computation | custom fusion | bytes 8192 | tf_op jit(solution)/shard_map/jit(take_along_axis)/gather | solution.py:136
  330.2 85.1 %all-to-all-done.3 = bf16[16,48,4096]{2,1,0:T(8,128)(2,1)} async-done(((bf16[16,48,4096]{2,1,0:T(8,128)(2,1)}), bf16[16,48,4096]{2,1,0:T(8,128)(2,1)}, u32[]{:S(2)}, u32[]{:S(2)}) %all-to-all-start.3) | async-done | bytes 6291488 | tf_op jit(solution)/shard_map/all_to_all | solution.py:169
  415.3 5.3 %convert_add_fusion = f32[256,4096]{1,0:T(8,128)S(1)} fusion(bf16[256,4096]{1,0:T(8,128)(2,1)} %copy-done.2, bf16[768,4096]{1,0:T(8,128)(2,1)} %bitcast.20, f32[256]{0:T(256)S(1)} %bitcast.124, s32[256]{0:T(256)S(1)} %bitcast.121), kind=kOutput, calls=%fused_computation.12 | convolution fusion | flops 1613955072 | bytes 12584960 | tf_op jit(solution)/shard_map/dot_general | solution.py:175
  420.6 6.1 %fusion.8 = bf16[256,4096]{1,0:T(8,128)(2,1)} fusion(f32[256,4096]{1,0:T(8,128)S(1)} %convert_add_fusion, bf16[768,4096]{1,0:T(8,128)(2,1)} %bitcast.20, f32[256]{0:T(256)S(1)} %bitcast.125, s32[256]{0:T(256)S(1)} %bitcast.123), kind=kOutput, calls=%fused_computation.20 | convolution fusion | flops 1613955072 | bytes 12584960 | tf_op jit(solution)/shard_map/dot_general | solution.py:175
  (76 shorter events, 2.7 us)
Async XLA Ops:
  6.5 305.9 %copy-start = (bf16[1,384,4096]{2,1,0:T(8,128)(2,1)S(1)}, bf16[1,384,4096]{2,1,0:T(8,128)(2,1)}, u32[]{:S(2)}) copy-start(bf16[1,384,4096]{2,1,0:T(8,128)(2,1)} %param.33) | copy-start | bytes 9437188
  8.5 6.7 %copy-start.8 = (f32[256,64]{0,1:T(8,128)}, f32[256,64]{0,1:T(8,128)S(1)}, u32[]{:S(2)}) copy-start(f32[256,64]{0,1:T(8,128)S(1)} %get-tuple-element.61) | copy-start | bytes 196612
  9.4 0.6 copy-start.10
  11.0 4.1 copy-start.7
  26.8 41.8 %all-to-all-start = ((f32[16,4,8320]{2,1,0:T(4,128)}), f32[16,4,8320]{2,1,0:T(4,128)}, u32[]{:S(2)}, u32[]{:S(2)}) async-start(f32[16,4,8320]{2,1,0:T(4,128)} %pad_maximum_fusion), calls=%async_computation | async-start | bytes 4259840 | tf_op jit(solution)/shard_map/all_to_all | solution.py:77
  34.0 156.1 %all-gather.2.cloned.1.call-start = ((), (), s32[]{:S(2)}) async-start(), calls=%async_computation.4 | async-start | bytes 17825792 | tf_op jit(solution)/shard_map/all_gather | solution.py:109
  95.5 5.9 %copy-start.6 = (bf16[256,128]{1,0:T(8,128)(2,1)S(1)}, bf16[256,128]{1,0:T(8,128)(2,1)}, u32[]{:S(2)}) copy-start(bf16[256,128]{1,0:T(8,128)(2,1)} %param.20) | copy-start | bytes 196612
  95.5 48.5 %all-to-all-start.1 = ((f32[16,4,8192]{2,1,0:T(4,128)}), f32[16,4,8192]{2,1,0:T(4,128)}, u32[]{:S(2)}, u32[]{:S(2)}) async-start(f32[16,4,8192]{2,1,0:T(4,128)} %fusion.44), calls=%async_computation.1 | async-start | bytes 4194304 | tf_op jit(solution)/shard_map/all_to_all | solution.py:87
  144.0 7.4 %copy-start.11 = (f32[256,64]{0,1:T(8,128)S(1)}, f32[256,64]{0,1:T(8,128)}, u32[]{:S(2)}) copy-start(f32[256,64]{0,1:T(8,128)} %copy-done.10) | copy-start | bytes 196612
  147.8 3.7 copy-start.4
  147.8 3.8 copy-start.5
  147.8 3.8 copy-start.9
  147.8 3.8 copy-start.19
  159.0 10.3 %copy-start.13 = (f32[4096]{0:T(1024)S(1)}, f32[4096]{0:T(1024)}, u32[]{:S(2)}) copy-start(f32[4096]{0:T(1024)} %param.25) | copy-start | bytes 49156
  164.6 4.7 %copy-start.1 = (f32[256,4096]{1,0:T(8,128)S(1)}, f32[256,4096]{1,0:T(8,128)}, u32[]{:S(2)}) copy-start(f32[256,4096]{1,0:T(8,128)} %copy.144) | copy-start | bytes 12582916
  164.6 5.1 %copy-start.3 = (bf16[256,4096]{1,0:T(8,128)(2,1)S(1)}, bf16[256,4096]{1,0:T(8,128)(2,1)}, u32[]{:S(2)}) copy-start(bf16[256,4096]{1,0:T(8,128)(2,1)} %param.18) | copy-start | bytes 6291460
  169.7 3.5 copy-start.12
  172.8 4.9 %collective-permute-start = (bf16[256,4096]{1,0:T(8,128)(2,1)}, bf16[256,4096]{1,0:T(8,128)(2,1)}, u32[]{:S(2)}, u32[]{:S(2)}) collective-permute-start(bf16[256,4096]{1,0:T(8,128)(2,1)} %multiply_convert_fusion.4), channel_id=1, source_target_pairs={{0,1},{1,0},{2,3},{3,2},{4,5},{5,4},{6,7},{7,6},{8,9},{9,8},{10,11... | collective-permute-start | bytes 6291464 | tf_op jit(solution)/shard_map/ppermute | solution.py:113
  190.2 11.2 %copy-start.15 = (bf16[4096,2048]{1,0:T(8,128)(2,1)S(1)}, bf16[4096,2048]{1,0:T(8,128)(2,1)}, u32[]{:S(2)}) copy-start(bf16[4096,2048]{1,0:T(8,128)(2,1)} %all-gather.2.cloned.1.call-done) | copy-start | bytes 50331652
  201.2 6.4 %collective-permute-start.1 = (bf16[256,2048]{1,0:T(8,128)(2,1)S(1)}, bf16[256,2048]{1,0:T(8,128)(2,1)S(1)}, u32[]{:S(2)}, u32[]{:S(2)}) collective-permute-start(bf16[256,2048]{1,0:T(8,128)(2,1)S(1)} %convolution_convert_fusion.2), channel_id=1, source_target_pairs={{0,1},{1,0},{2,3},{3,2},{4,5},{5,4},{6,7},{7,6},{8,9},{9,8},{10,11... | collective-permute-start | bytes 3145736 | tf_op jit(solution)/shard_map/ppermute | solution.py:118
  220.2 3.7 copy-start.14
  223.9 2.1 copy-start.2
  225.9 79.6 %copy-start.16 = (bf16[1,4096,384]{2,1,0:T(8,128)(2,1)S(1)}, bf16[1,4096,384]{2,1,0:T(8,128)(2,1)}, u32[]{:S(2)}) copy-start(bf16[1,4096,384]{2,1,0:T(8,128)(2,1)} %param.31) | copy-start | bytes 9437188
  305.6 3.4 copy-start.17
  317.9 5.1 %copy-start.18 = (bf16[4096,16]{0,1:T(8,128)(2,1)S(1)}, bf16[4096,16]{0,1:T(8,128)(2,1)}, u32[]{:S(2)}) copy-start(bf16[4096,16]{0,1:T(8,128)(2,1)} %param.29) | copy-start | bytes 393220
  317.9 97.4 %all-to-all-start.3 = ((bf16[16,48,4096]{2,1,0:T(8,128)(2,1)}), bf16[16,48,4096]{2,1,0:T(8,128)(2,1)}, u32[]{:S(2)}, u32[]{:S(2)}) async-start(bf16[16,48,4096]{2,1,0:T(8,128)(2,1)} %bitcast.111), calls=%async_computation.3 | async-start | bytes 12582912 | tf_op jit(solution)/shard_map/all_to_all | solution.py:169
Sparse Core Ops, SparseCore 0:
  36.9 153.1 all-gather.1

commit v3 on v2

--- a/solution.py
+++ b/solution.py
@@ -71,19 +71,22 @@
     n_seq = lax.axis_size("seq")
     per_chunk = heads // n_seq
     flat_state = segment_state.reshape(heads, head_width * state_width)
-    packed = jnp.concatenate(
-        [flat_state, jnp.broadcast_to(slab_total[:, None], (heads, 128))], axis=1
-    ).reshape(n_seq, per_chunk, head_width * state_width + 128)
+    with jax.named_scope("state_pack"):
+        packed = jnp.concatenate(
+            [flat_state, jnp.broadcast_to(slab_total[:, None], (heads, 128))], axis=1
+        ).reshape(n_seq, per_chunk, head_width * state_width + 128)
     received = lax.all_to_all(packed, "seq", 0, 0, tiled=True)
     slab_states = received[:, :, : head_width * state_width]
     slab_totals = received[:, :, head_width * state_width]
 
-    entering_here = jnp.zeros((per_chunk, head_width * state_width), jnp.float32)
-    entering_list = []
-    for j in range(n_seq):
-        entering_list.append(entering_here)
-        entering_here = jnp.exp(slab_totals[j])[:, None] * entering_here + slab_states[j]
-    entering_each = jnp.stack(entering_list)
+    order = jnp.arange(n_seq)
+    between = (order[None, None, :] > order[None, :, None]) & (order[None, None, :] < order[:, None, None])
+    span = jnp.sum(jnp.where(between[:, :, :, None], slab_totals[None, None, :, :], 0.0), axis=2)
+    earlier = (order[:, None] > order[None, :])[:, :, None]
+    carry_weights = jnp.where(earlier, jnp.exp(span), 0.0)
+    entering_each = jnp.einsum(
+        "ijh,jhx->ihx", carry_weights, slab_states, precision=lax.Precision.HIGHEST
+    )
     entering = lax.all_to_all(entering_each, "seq", 0, 0, tiled=True).reshape(
         heads, head_width, state_width
     )
@@ -104,27 +107,20 @@
     ).astype(jnp.bfloat16)
     n_batch = lax.axis_size("batch")
     core = lax.axis_index("batch") % 2
-    shard_cols = w_out.shape[1]
-    half = shard_cols // 2
-    w_half = lax.all_gather(
-        lax.dynamic_slice_in_dim(w_out, core * half, half, axis=1), "seq", axis=1, tiled=True
+    depth = w_out.shape[0] // 2
+    with jax.named_scope("wgather"):
+        w_rows = lax.all_gather(
+            lax.dynamic_slice_in_dim(w_out, core * depth, depth, axis=0), "seq", axis=1, tiled=True
+        )
+    partners = [(b, b ^ 1) for b in range(n_batch)]
+    own_rows = lax.dynamic_slice_in_dim(normed, core * depth, depth, axis=1)
+    partner_rows = lax.ppermute(
+        lax.dynamic_slice_in_dim(normed, (1 - core) * depth, depth, axis=1), "batch", partners
     )
-    partners = [(b, b ^ 1) for b in range(n_batch)]
-    normed_partner = lax.ppermute(normed, "batch", partners)
-    own_half = jnp.dot(normed, w_half, preferred_element_type=jnp.float32).astype(jnp.bfloat16)
-    partner_half = jnp.dot(normed_partner, w_half, preferred_element_type=jnp.float32).astype(
-        jnp.bfloat16
-    )
-    other_half = lax.ppermute(partner_half, "batch", partners)
-    first_half = jnp.where(core == 0, own_half, other_half)
-    second_half = jnp.where(core == 0, other_half, own_half)
-    mixer_out = jnp.stack(
-        [
-            first_half.reshape(tokens_here, n_seq, half),
-            second_half.reshape(tokens_here, n_seq, half),
-        ],
-        axis=2,
-    ).reshape(tokens_here, n_seq * shard_cols)
+    own_part = jnp.dot(own_rows, w_rows, preferred_element_type=jnp.float32)
+    partner_part = jnp.dot(partner_rows, w_rows, preferred_element_type=jnp.float32)
+    other_part = lax.ppermute(partner_part, "batch", partners)
+    mixer_out = (own_part + other_part).astype(jnp.bfloat16)
     hidden = (residual.astype(jnp.float32) + mixer_out.astype(jnp.float32)).astype(jnp.bfloat16)
     hidden_wide = hidden.astype(jnp.float32)
     moe_input = (

time: 439 us -> 420 us (0.957)
  other arithmetic: 46.8 us -> 17.7 us
  waiting for transfers between devices: 170 us -> 177 us
  matrix products: 65.4 us -> 72.3 us
  local copies, waits for them, and re-layouts: 40.1 us -> 33.5 us
    unnamed x16 -> x1, other arithmetic: 25.3 us -> 0.95 us
    convert_element_type x2 -> x0, local copies, waits for them, and re-layouts: 11.6 us -> none  [shards(): mixer_out.astype(jnp.float32)]
    dot_general x2 -> x3, matrix products: 17.3 us -> 24.2 us  [the longest x1 12.5 us: shards(): jnp.dot(partner_rows, w_rows, preferred_element_type=jnp.float32)]
    all_to_all x1, waiting for transfers between devices: 31.5 us -> 37.9 us  [shards(): received = lax.all_to_all(packed, 'seq', 0, 0, tiled=True)]
  transfers between devices with their start and end apart: 6 -> 6, of which waited for: 5 -> 5; matrix products, arithmetic and copies ran while one was open for 18% -> 19% of each run, Pallas kernels for 0% -> 0%
where the time goes in v3:
time: 420 us; the launch traced here: 413 us
  waiting for transfers between devices  177 us (42%)
  blocking collectives  80.7 us (19%)
  matrix products  72.3 us (17%)
  local copies, waits for them, and re-layouts  33.5 us (8%)
  other arithmetic  17.7 us (4%)
  starting transfers between devices  16.8 us (4%)
  between operations  14.3 us (3%)
    all_to_all x1, waiting for transfers between devices, shards(): lax.all_to_all(finished, 'seq', split_axis=0, concat_axis=0, tiled=True)  85.2 us
    all_to_all x1, blocking collectives, shards(): lax.all_to_all(departing_state, 'seq', split_axis=0, concat_axis=0, tiled...  80.7 us
    all_to_all x1, waiting for transfers between devices, shards(): lax.all_to_all(entering_each, 'seq', 0, 0, tiled=True)  38.4 us
    all_to_all x1, waiting for transfers between devices, shards(): received = lax.all_to_all(packed, 'seq', 0, 0, tiled=True)  37.9 us
    all_gather x1, waiting for transfers between devices, shards(): lax.all_gather(lax.dynamic_slice_in_dim(w_out, core * depth, depth, axis=...  13.2 us
    dot_general x1, matrix products, shards(): jnp.dot(partner_rows, w_rows, preferred_element_type=jnp.float32)  12.5 us
    dot_general x2, matrix products, shards(): fetched = jnp.dot(picking, returned, preferred_element_type=jnp.float32)  11.4 us
    dot_general x1, matrix products, shards(): own_part = jnp.dot(own_rows, w_rows, preferred_element_type=jnp.float32)  8.58 us
  transfers between devices with their start and end apart: 6, of which 5 were waited for; matrix products, arithmetic and copies ran while one was open for 19% of the time, Pallas kernels for 0%

profile of v3, /device:TPU:0, one launch (start us, length us, event | category | flops | bytes accessed | tf_op | source)
XLA Modules:
  0.0 412.9 jit_solution(8856688508422826162)
XLA Ops:
  6.5 2.5 constant_dynamic-slice_fusion.1
  9.1 0.7 exp.43
  9.7 1.0 multiply_bitcast_fusion
  10.7 0.6 reduce-window.16
  11.3 0.2 slice_reduce_fusion
  11.5 4.1 copy.98
  15.6 0.1 bitcast_bitcast_fusion
  15.7 0.2 slice_reduce_fusion.2
  15.9 0.1 broadcast_in_dim.117
  16.0 0.7 fusion.58
  16.7 5.1 %add_bitcast_fusion = f32[64,64,128]{2,1,0:T(8,128)} fusion(bf16[256,64,64]{0,2,1:T(8,128)(2,1)} %bitcast.107, f32[256,128]{1,0:T(8,128)S(1)} %convert_element_type.64, f32[256,64]{0,1:T(8,128)S(1)} %get-tuple-element.36, f32[64]{0:T(128)S(1)} %exponential_multiply_fusion.1), kind=kOutput, calls=%fused_computation.48 | convolution fusion | flops 273154048 | bytes 4391168 | tf_op jit(solution)/shard_map/while/body/eval_jaxpr/shn,shp->hpn/dot_general | solution.py:27
  21.9 3.2 concatenate.6
  25.1 0.1 broadcast_in_dim.118
  25.1 3.5 pad_maximum_fusion
  28.6 7.2 %all-to-all-start = ((f32[16,4,8320]{2,1,0:T(4,128)}), f32[16,4,8320]{2,1,0:T(4,128)}, u32[]{:S(2)}, u32[]{:S(2)}) async-start(f32[16,4,8320]{2,1,0:T(4,128)} %pad_maximum_fusion), calls=%async_computation | async-start | bytes 4259840 | tf_op jit(solution)/shard_map/all_to_all | solution.py:78
  35.8 37.9 %all-to-all-done = f32[16,4,8320]{2,1,0:T(4,128)} async-done(((f32[16,4,8320]{2,1,0:T(4,128)}), f32[16,4,8320]{2,1,0:T(4,128)}, u32[]{:S(2)}, u32[]{:S(2)}) %all-to-all-start) | async-done | bytes 2129952 | tf_op jit(solution)/shard_map/all_to_all | solution.py:78
  73.8 0.8 slice.56
  74.6 0.1 copy.100
  74.7 1.7 slice.55
  76.4 0.2 select_reduce_fusion
  76.7 3.1 convolution_bitcast_fusion
  79.8 2.7 copy.102
  82.5 4.6 %all-to-all-start.1 = ((f32[16,4,8192]{2,1,0:T(4,128)}), f32[16,4,8192]{2,1,0:T(4,128)}, u32[]{:S(2)}, u32[]{:S(2)}) async-start(f32[16,4,8192]{2,1,0:T(4,128)} %copy.102), calls=%async_computation.1 | async-start | bytes 4194304 | tf_op jit(solution)/shard_map/all_to_all | solution.py:90
  87.1 0.6 iota_compare_fusion.7
  87.8 0.2 fusion.63
  88.0 3.7 fusion.36
  91.7 38.4 %all-to-all-done.1 = f32[16,4,8192]{2,1,0:T(4,128)} async-done(((f32[16,4,8192]{2,1,0:T(4,128)}), f32[16,4,8192]{2,1,0:T(4,128)}, u32[]{:S(2)}, u32[]{:S(2)}) %all-to-all-start.1) | async-done | bytes 2097184 | tf_op jit(solution)/shard_map/all_to_all | solution.py:90
  130.1 3.8 reshape.185
  133.8 3.6 fusion.47
  137.5 7.5 %fusion.18 = f32[256,64,64]{0,2,1:T(8,128)} fusion(f32[64,64,256]{2,1,0:T(8,128)S(1)} %fusion.47, f32[64,64,256]{2,1,0:T(8,128)S(1)} %copy-done.5, bf16[256,64,64]{0,2,1:T(8,128)(2,1)S(1)} %bitcast.108, f32[256,64]{0,1:T(8,128)S(1)} %copy-done.11, f32[256,64]{0,1:T(8,128)S(1)} %copy-done.13, f32[256,256]{1,0:T(8,128)S(1)} %fusion.63, ...), kind=kOutput, calls=%fused_computation.32 | convolution fusion | flops 565182464 | bytes 15204608 | tf_op jit(solution)/shard_map/while/body/eval_jaxpr/tsh,shp->thp/dot_general | solution.py:18
  145.0 5.7 %copy.103 = f32[256,4096]{1,0:T(8,128)} copy(f32[256,4096]{0,1:T(8,128)} %bitcast.106) | data formatting | bytes 8388608 | tf_op jit(solution)/shard_map/reshape | solution.py:102
  150.6 4.7 %multiply_reduce_fusion = f32[256]{0:T(256)S(1)} fusion(f32[256,4096]{1,0:T(8,128)} %copy.103, bf16[256,4096]{1,0:T(8,128)(2,1)} %param.18), kind=kLoop, calls=%fused_computation.38 | loop fusion | flops 8388352 | bytes 6292480 | tf_op jit(solution)/shard_map/reduce_sum | solution.py:105
  155.4 0.4 copy-done.3
  155.8 1.7 multiply_convert_fusion.4
  157.5 1.3 copy-done.4
  158.9 0.3 collective-permute-start
  159.2 2.8 collective-permute-done
  162.0 13.2 %all-gather.2.cloned.1.call-done = bf16[2048,4096]{1,0:T(8,128)(2,1)} async-done(((bf16[2048,256]{1,0:T(8,128)(2,1)}), bf16[2048,4096]{1,0:T(8,128)(2,1)}) %all-gather.2.cloned.1.call-update) | async-done | bytes 16777232 | tf_op jit(solution)/shard_map/wgather/all_gather | solution.py:112
  175.1 12.5 %fusion.64 = f32[256,4096]{1,0:T(8,128)} fusion(bf16[256,2048]{1,0:T(8,128)(2,1)} %collective-permute-done, bf16[2048,4096]{1,0:T(8,128)(2,1)} %all-gather.2.cloned.1.call-done), kind=kOutput, calls=%fused_computation.112 | convolution fusion | flops 4294967296 | bytes 22020096 | tf_op jit(solution)/shard_map/dot_general | solution.py:121
  187.7 0.1 copy.106
  187.8 0.1 eq.87
  188.0 0.1 eq.83
  188.1 1.2 reduce-window.24
  189.3 0.2 slice_reduce_fusion.1
  189.5 0.1 fusion.51
  189.7 0.1 sub.48
  189.8 0.1 copy.109
  189.9 8.6 %fusion.34 = f32[256,4096]{1,0:T(8,128)S(1)} fusion(bf16[2048,4096]{1,0:T(8,128)(2,1)} %all-gather.2.cloned.1.call-done, bf16[256,4096]{1,0:T(8,128)(2,1)} %copy-done.4, s32[]{:T(128)S(6)} %select_n.44), kind=kOutput, calls=%fused_computation.51 | convolution fusion | flops 4294967296 | bytes 22020100 | tf_op jit(solution)/shard_map/dot_general | solution.py:120
  198.5 3.1 fusion.13
  201.7 2.0 convolution_convert_fusion
  203.7 80.7 %all_to_all.20 = bf16[16,48,4096]{2,1,0:T(8,128)(2,1)S(1)} all-to-all(bf16[16,48,4096]{2,1,0:T(8,128)(2,1)S(1)} %bitcast.102), channel_id=1, replica_groups=mesh['seq'=16,'batch'=8] {'seq'}, dimensions={0} | all-to-all | bytes 12582912 | tf_op jit(solution)/shard_map/all_to_all | solution.py:156
  284.4 3.4 fusion.25
  287.8 3.5 fusion.31
  291.3 5.4 %convolution_convert_fusion.1 = bf16[768,4096]{1,0:T(8,128)(2,1)} fusion(bf16[768,384]{1,0:T(8,128)(2,1)S(1)} %fusion.31, bf16[1,384,4096]{2,1,0:T(8,128)(2,1)S(1)} %copy-done), kind=kOutput, calls=%fused_computation.12 | convolution fusion | flops 2419064832 | bytes 10027008 | tf_op jit(solution)/shard_map/dot_general | solution.py:161
  296.7 4.8 %all-to-all-start.3 = ((bf16[16,48,4096]{2,1,0:T(8,128)(2,1)}), bf16[16,48,4096]{2,1,0:T(8,128)(2,1)}, u32[]{:S(2)}, u32[]{:S(2)}) async-start(bf16[16,48,4096]{2,1,0:T(8,128)(2,1)} %bitcast.103), calls=%async_computation.3 | async-start | bytes 12582912 | tf_op jit(solution)/shard_map/all_to_all | solution.py:165
  301.5 0.1 copy.104
  301.6 0.1 reshape.193
  301.8 2.3 fusion.41
  304.1 4.6 %gather_fusion = f32[512]{0:T(512)S(1)} fusion(f32[256,16]{0,1:T(8,128)S(1)} %fusion.41, s32[512]{0:T(512)S(1)} %reshape.193), kind=kCustom, calls=%fused_computation | custom fusion | bytes 8192 | tf_op jit(solution)/shard_map/jit(take_along_axis)/gather | solution.py:132
  308.7 0.1 reshape.196
  308.8 0.1 copy.105
  309.0 85.2 %all-to-all-done.3 = bf16[16,48,4096]{2,1,0:T(8,128)(2,1)} async-done(((bf16[16,48,4096]{2,1,0:T(8,128)(2,1)}), bf16[16,48,4096]{2,1,0:T(8,128)(2,1)}, u32[]{:S(2)}, u32[]{:S(2)}) %all-to-all-start.3) | async-done | bytes 6291488 | tf_op jit(solution)/shard_map/all_to_all | solution.py:165
  394.1 5.3 %convert_add_fusion = f32[256,4096]{1,0:T(8,128)S(1)} fusion(bf16[256,4096]{1,0:T(8,128)(2,1)} %copy-done.2, bf16[768,4096]{1,0:T(8,128)(2,1)} %bitcast.22, f32[256]{0:T(256)S(1)} %bitcast.115, s32[256]{0:T(256)S(1)} %bitcast.111), kind=kOutput, calls=%fused_computation.13 | convolution fusion | flops 1613955072 | bytes 12584960 | tf_op jit(solution)/shard_map/dot_general | solution.py:171
  399.4 6.1 %fusion.8 = bf16[256,4096]{1,0:T(8,128)(2,1)} fusion(f32[256,4096]{1,0:T(8,128)S(1)} %convert_add_fusion, bf16[768,4096]{1,0:T(8,128)(2,1)} %bitcast.22, f32[256]{0:T(256)S(1)} %bitcast.116, s32[256]{0:T(256)S(1)} %bitcast.113), kind=kOutput, calls=%fused_computation.21 | convolution fusion | flops 1613955072 | bytes 12584960 | tf_op jit(solution)/shard_map/dot_general | solution.py:171
  (66 shorter events, 0.4 us)
Async XLA Ops:
  6.5 284.7 %copy-start = (bf16[1,384,4096]{2,1,0:T(8,128)(2,1)S(1)}, bf16[1,384,4096]{2,1,0:T(8,128)(2,1)}, u32[]{:S(2)}) copy-start(bf16[1,384,4096]{2,1,0:T(8,128)(2,1)} %param.33) | copy-start | bytes 9437188
  6.5 9.1 %copy-start.9 = (bf16[256,128]{1,0:T(8,128)(2,1)S(1)}, bf16[256,128]{1,0:T(8,128)(2,1)}, u32[]{:S(2)}) copy-start(bf16[256,128]{1,0:T(8,128)(2,1)} %param.19) | copy-start | bytes 196612
  6.5 168.6 %all-gather.2.cloned.1.call-start = ((), (), s32[]{:S(2)}) async-start(), calls=%async_computation.4 | async-start | bytes 17825792 | tf_op jit(solution)/shard_map/wgather/all_gather | solution.py:112
  10.7 11.2 %copy-start.10 = (f32[256,64]{0,1:T(8,128)}, f32[256,64]{0,1:T(8,128)S(1)}, u32[]{:S(2)}) copy-start(f32[256,64]{0,1:T(8,128)S(1)} %get-tuple-element.32) | copy-start | bytes 196612
  15.7 9.3 %copy-start.12 = (f32[256,64]{0,1:T(8,128)}, f32[256,64]{0,1:T(8,128)S(1)}, u32[]{:S(2)}) copy-start(f32[256,64]{0,1:T(8,128)S(1)} %bitcast_bitcast_fusion) | copy-start | bytes 196612
  28.6 45.2 %all-to-all-start = ((f32[16,4,8320]{2,1,0:T(4,128)}), f32[16,4,8320]{2,1,0:T(4,128)}, u32[]{:S(2)}, u32[]{:S(2)}) async-start(f32[16,4,8320]{2,1,0:T(4,128)} %pad_maximum_fusion), calls=%async_computation | async-start | bytes 4259840 | tf_op jit(solution)/shard_map/all_to_all | solution.py:78
  79.8 8.0 %copy-start.8 = (bf16[256,128]{1,0:T(8,128)(2,1)S(1)}, bf16[256,128]{1,0:T(8,128)(2,1)}, u32[]{:S(2)}) copy-start(bf16[256,128]{1,0:T(8,128)(2,1)} %param.20) | copy-start | bytes 196612
  82.5 47.6 %all-to-all-start.1 = ((f32[16,4,8192]{2,1,0:T(4,128)}), f32[16,4,8192]{2,1,0:T(4,128)}, u32[]{:S(2)}, u32[]{:S(2)}) async-start(f32[16,4,8192]{2,1,0:T(4,128)} %copy.102), calls=%async_computation.1 | async-start | bytes 4194304 | tf_op jit(solution)/shard_map/all_to_all | solution.py:90
  130.1 7.4 %copy-start.13 = (f32[256,64]{0,1:T(8,128)S(1)}, f32[256,64]{0,1:T(8,128)}, u32[]{:S(2)}) copy-start(f32[256,64]{0,1:T(8,128)} %copy-done.12) | copy-start | bytes 196612
  133.8 3.6 copy-start.5
  133.8 3.7 copy-start.7
  133.8 3.7 copy-start.11
  133.8 3.7 copy-start.20
  145.0 10.4 %copy-start.15 = (f32[4096]{0:T(1024)S(1)}, f32[4096]{0:T(1024)}, u32[]{:S(2)}) copy-start(f32[4096]{0:T(1024)} %param.25) | copy-start | bytes 49156
  150.6 4.8 %copy-start.1 = (f32[256,4096]{1,0:T(8,128)S(1)}, f32[256,4096]{1,0:T(8,128)}, u32[]{:S(2)}) copy-start(f32[256,4096]{1,0:T(8,128)} %copy.103) | copy-start | bytes 12582916
  150.6 5.2 %copy-start.3 = (bf16[256,4096]{1,0:T(8,128)(2,1)S(1)}, bf16[256,4096]{1,0:T(8,128)(2,1)}, u32[]{:S(2)}) copy-start(bf16[256,4096]{1,0:T(8,128)(2,1)} %param.18) | copy-start | bytes 6291460
  157.5 1.3 copy-start.4
  158.9 28.8 %copy-start.14 = (s32[256,2]{0,1:T(2,128)S(1)}, s32[256,2]{0,1:T(2,128)}, u32[]{:S(2)}) copy-start(s32[256,2]{0,1:T(2,128)} %param.30) | copy-start | bytes 6148
  158.9 3.1 collective-permute-start
  187.7 10.8 %collective-permute-start.1 = (f32[256,4096]{1,0:T(8,128)}, f32[256,4096]{1,0:T(8,128)}, u32[]{:S(2)}, u32[]{:S(2)}) collective-permute-start(f32[256,4096]{1,0:T(8,128)} %fusion.64), channel_id=1, source_target_pairs={{0,1},{1,0},{2,3},{3,2},{4,5},{5,4},{6,7},{7,6},{8,9},{9,8},{10,11... | collective-permute-start | bytes 12582920 | tf_op jit(solution)/shard_map/ppermute | solution.py:122
  189.9 8.6 %copy-start.6 = (bf16[256,4096]{1,0:T(8,128)(2,1)S(1)}, bf16[256,4096]{1,0:T(8,128)(2,1)}, u32[]{:S(2)}) copy-start(bf16[256,4096]{1,0:T(8,128)(2,1)} %param.27) | copy-start | bytes 6291460
  198.5 3.2 copy-start.16
  201.7 2.0 copy-start.2
  203.7 80.7 %copy-start.17 = (bf16[1,4096,384]{2,1,0:T(8,128)(2,1)S(1)}, bf16[1,4096,384]{2,1,0:T(8,128)(2,1)}, u32[]{:S(2)}) copy-start(bf16[1,4096,384]{2,1,0:T(8,128)(2,1)} %param.31) | copy-start | bytes 9437188
  284.4 3.4 copy-start.18
  296.7 5.1 %copy-start.19 = (bf16[4096,16]{0,1:T(8,128)(2,1)S(1)}, bf16[4096,16]{0,1:T(8,128)(2,1)}, u32[]{:S(2)}) copy-start(bf16[4096,16]{0,1:T(8,128)(2,1)} %param.29) | copy-start | bytes 393220
  296.7 97.4 %all-to-all-start.3 = ((bf16[16,48,4096]{2,1,0:T(8,128)(2,1)}), bf16[16,48,4096]{2,1,0:T(8,128)(2,1)}, u32[]{:S(2)}, u32[]{:S(2)}) async-start(bf16[16,48,4096]{2,1,0:T(8,128)(2,1)} %bitcast.103), calls=%async_computation.3 | async-start | bytes 12582912 | tf_op jit(solution)/shard_map/all_to_all | solution.py:165
Sparse Core Ops, SparseCore 0:
  9.4 165.6 all-gather.1

commit v4 on v3

--- a/solution.py
+++ b/solution.py
@@ -117,8 +117,11 @@
     partner_rows = lax.ppermute(
         lax.dynamic_slice_in_dim(normed, (1 - core) * depth, depth, axis=1), "batch", partners
     )
-    own_part = jnp.dot(own_rows, w_rows, preferred_element_type=jnp.float32)
-    partner_part = jnp.dot(partner_rows, w_rows, preferred_element_type=jnp.float32)
+    both_parts = jnp.dot(
+        jnp.concatenate([partner_rows, own_rows], axis=0), w_rows, preferred_element_type=jnp.float32
+    )
+    partner_part = both_parts[:tokens_here]
+    own_part = both_parts[tokens_here:]
     other_part = lax.ppermute(partner_part, "batch", partners)
     mixer_out = (own_part + other_part).astype(jnp.bfloat16)
     hidden = (residual.astype(jnp.float32) + mixer_out.astype(jnp.float32)).astype(jnp.bfloat16)
@@ -145,31 +148,35 @@
     target = flat_ids * capacity + slot_of
     slots = experts_all * capacity
     target_pairs = target.reshape(tokens_here, fanout)
-    slot_ids = jnp.arange(slots, dtype=jnp.int32)
-    placing = jnp.zeros((slots, tokens_here), jnp.bool_)
-    for k in range(fanout):
-        placing = placing | (slot_ids[:, None] == target_pairs[None, :, k])
-    departing_state = jnp.dot(
-        placing.astype(jnp.bfloat16), moe_input, preferred_element_type=jnp.float32
-    ).astype(jnp.bfloat16)
-    departing_state = departing_state.reshape(experts_all, capacity, width)
-    batch = lax.all_to_all(departing_state, "seq", split_axis=0, concat_axis=0, tiled=True)
-    flat_rows = batch.reshape(-1, width)
-    gate_part = jnp.dot(flat_rows, w_gate[0], preferred_element_type=jnp.float32)
-    up_part = jnp.dot(flat_rows, w_up[0], preferred_element_type=jnp.float32)
-    expert_hidden = (jax.nn.silu(gate_part) * up_part).astype(jnp.bfloat16)
-    result = jnp.dot(expert_hidden, w_down[0], preferred_element_type=jnp.float32).astype(
-        jnp.bfloat16
-    )
-    finished = result.reshape(batch.shape)
-    returned = lax.all_to_all(finished, "seq", split_axis=0, concat_axis=0, tiled=True).reshape(
-        experts_all * capacity, width
-    )
+    stages = 2
+    chunk = capacity // stages
+    slot_grid = jnp.arange(slots, dtype=jnp.int32).reshape(experts_all, stages, chunk)
     total = hidden_wide
-    for k in range(fanout):
-        picking = (target_pairs[:, k][:, None] == slot_ids[None, :]).astype(jnp.bfloat16)
-        fetched = jnp.dot(picking, returned, preferred_element_type=jnp.float32)
-        total = total + combine[:, k][:, None] * fetched
+    for h in range(stages):
+        slot_ids = slot_grid[:, h, :].reshape(-1)
+        placing = jnp.zeros((slot_ids.shape[0], tokens_here), jnp.bool_)
+        for k in range(fanout):
+            placing = placing | (slot_ids[:, None] == target_pairs[None, :, k])
+        departing_state = jnp.dot(
+            placing.astype(jnp.bfloat16), moe_input, preferred_element_type=jnp.float32
+        ).astype(jnp.bfloat16)
+        departing_state = departing_state.reshape(experts_all, chunk, width)
+        batch = lax.all_to_all(departing_state, "seq", split_axis=0, concat_axis=0, tiled=True)
+        flat_rows = batch.reshape(-1, width)
+        gate_part = jnp.dot(flat_rows, w_gate[0], preferred_element_type=jnp.float32)
+        up_part = jnp.dot(flat_rows, w_up[0], preferred_element_type=jnp.float32)
+        expert_hidden = (jax.nn.silu(gate_part) * up_part).astype(jnp.bfloat16)
+        result = jnp.dot(expert_hidden, w_down[0], preferred_element_type=jnp.float32).astype(
+            jnp.bfloat16
+        )
+        finished = result.reshape(batch.shape)
+        returned = lax.all_to_all(
+            finished, "seq", split_axis=0, concat_axis=0, tiled=True
+        ).reshape(-1, width)
+        for k in range(fanout):
+            picking = (target_pairs[:, k][:, None] == slot_ids[None, :]).astype(jnp.bfloat16)
+            fetched = jnp.dot(picking, returned, preferred_element_type=jnp.float32)
+            total = total + combine[:, k][:, None] * fetched
     return total.astype(jnp.bfloat16)
 
 

time: 420 us -> 431 us (1.026)
  blocking collectives: 80.7 us -> 0 us
  waiting for transfers between devices: 177 us -> 232 us
  matrix products: 72.3 us -> 90.3 us
  starting transfers between devices: 16.8 us -> 31 us
    all_to_all x1 -> x0, blocking collectives: 80.7 us -> none  [shards(): lax.all_to_all(departing_state, 'seq', split_axis=0, concat_axis=0, tiled...]
    all_to_all x0 -> x2, waiting for transfers between devices: none -> 76.8 us  [shards(): lax.all_to_all(departing_state, 'seq', split_axis=0, concat_axis=0, tiled...]
    all_to_all x1 -> x2, waiting for transfers between devices: 85.2 us -> 55.4 us  [shards(): lax.all_to_all(finished, 'seq', split_axis=0, concat_axis=0, tiled=True)]
    dot_general x3 -> x1, matrix products: 24.6 us -> 12.2 us  [shards(): jnp.dot(jnp.concatenate([partner_rows, own_rows], axis=0), w_rows, prefer...]
    dot_general x1 -> x2, matrix products: 5.41 us -> 16.1 us  [shards(): jnp.dot(expert_hidden, w_down[0], preferred_element_type=jnp.float32)]
    all_to_all x0 -> x2, starting transfers between devices: none -> 9.47 us  [shards(): lax.all_to_all(departing_state, 'seq', split_axis=0, concat_axis=0, tiled...]
    dot_general x1 -> x2, matrix products: 3.4 us -> 10.9 us  [shards(): jnp.dot(flat_rows, w_gate[0], preferred_element_type=jnp.float32)]
    dot_general x2 -> x4, matrix products: 11.4 us -> 18.2 us  [shards(): fetched = jnp.dot(picking, returned, preferred_element_type=jnp.float32)]
  transfers between devices with their start and end apart: 6 -> 9, of which waited for: 5 -> 9; matrix products, arithmetic and copies ran while one was open for 19% -> 26% of each run, Pallas kernels for 0% -> 0%
where the time goes in v4:
time: 431 us; the launch traced here: 424 us
  waiting for transfers between devices  232 us (54%)
  matrix products  90.3 us (21%)
  local copies, waits for them, and re-layouts  37.3 us (9%)
  starting transfers between devices  31 us (7%)
  other arithmetic  18.8 us (4%)
  between operations  14.3 us (3%)
    all_to_all x2, waiting for transfers between devices, shards(): lax.all_to_all(departing_state, 'seq', split_axis=0, concat_axis=0, tiled...  76.8 us
    all_to_all x2, waiting for transfers between devices, shards(): lax.all_to_all(finished, 'seq', split_axis=0, concat_axis=0, tiled=True)  55.4 us
    all_to_all x1, waiting for transfers between devices, shards(): received = lax.all_to_all(packed, 'seq', 0, 0, tiled=True)  39.2 us
    all_to_all x1, waiting for transfers between devices, shards(): lax.all_to_all(entering_each, 'seq', 0, 0, tiled=True)  38.7 us
    dot_general x4, matrix products, shards(): fetched = jnp.dot(picking, returned, preferred_element_type=jnp.float32)  18.2 us
    dot_general x2, matrix products, shards(): jnp.dot(expert_hidden, w_down[0], preferred_element_type=jnp.float32)  16.1 us
    all_gather x1, waiting for transfers between devices, shards(): lax.all_gather(lax.dynamic_slice_in_dim(w_out, core * depth, depth, axis=...  14.4 us
    dot_general x1, matrix products, shards(): jnp.dot(jnp.concatenate([partner_rows, own_rows], axis=0), w_rows, prefer...  12.2 us
  transfers between devices with their start and end apart: 9, of which 9 were waited for; matrix products, arithmetic and copies ran while one was open for 26% of the time, Pallas kernels for 0%

profile of v4, /device:TPU:0, one launch (start us, length us, event | category | flops | bytes accessed | tf_op | source)
XLA Modules:
  0.0 424.1 jit_solution(10681595834030918811)
XLA Ops:
  6.6 2.5 constant_dynamic-slice_fusion
  9.3 0.6 reduce-window.16
  9.9 0.2 slice_reduce_fusion
  10.1 4.1 copy.98
  14.3 0.2 slice_reduce_fusion.2
  14.6 0.7 fusion.107
  15.3 5.1 %add_bitcast_fusion = f32[64,64,128]{2,1,0:T(8,128)} fusion(bf16[256,64,64]{0,2,1:T(8,128)(2,1)} %bitcast.126, f32[256,128]{1,0:T(8,128)S(1)} %convert_element_type.76, f32[256,64]{0,1:T(8,128)S(1)} %get-tuple-element.40, f32[64]{0:T(128)S(1)} %exponential_multiply_fusion.1), kind=kOutput, calls=%fused_computation.64 | convolution fusion | flops 273154048 | bytes 4391168 | tf_op jit(solution)/shard_map/while/body/eval_jaxpr/shn,shp->hpn/dot_general | solution.py:27
  20.5 3.2 concatenate.9
  23.7 3.5 pad_maximum_fusion
  27.3 7.2 %all-to-all-start = ((f32[16,4,8320]{2,1,0:T(4,128)}), f32[16,4,8320]{2,1,0:T(4,128)}, u32[]{:S(2)}, u32[]{:S(2)}) async-start(f32[16,4,8320]{2,1,0:T(4,128)} %pad_maximum_fusion), calls=%async_computation | async-start | bytes 4259840 | tf_op jit(solution)/shard_map/all_to_all | solution.py:78
  34.5 39.2 %all-to-all-done = f32[16,4,8320]{2,1,0:T(4,128)} async-done(((f32[16,4,8320]{2,1,0:T(4,128)}), f32[16,4,8320]{2,1,0:T(4,128)}, u32[]{:S(2)}, u32[]{:S(2)}) %all-to-all-start) | async-done | bytes 2129952 | tf_op jit(solution)/shard_map/all_to_all | solution.py:78
  73.8 0.8 slice.90
  74.6 1.7 slice.89
  76.4 0.2 select_reduce_fusion
  76.7 3.1 convolution_bitcast_fusion
  79.8 2.7 copy.102
  82.5 4.7 %all-to-all-start.1 = ((f32[16,4,8192]{2,1,0:T(4,128)}), f32[16,4,8192]{2,1,0:T(4,128)}, u32[]{:S(2)}, u32[]{:S(2)}) async-start(f32[16,4,8192]{2,1,0:T(4,128)} %copy.102), calls=%async_computation.1 | async-start | bytes 4194304 | tf_op jit(solution)/shard_map/all_to_all | solution.py:90
  87.2 0.7 iota_compare_fusion
  87.9 0.2 fusion.116
  88.1 3.7 fusion.52
  91.8 38.7 %all-to-all-done.1 = f32[16,4,8192]{2,1,0:T(4,128)} async-done(((f32[16,4,8192]{2,1,0:T(4,128)}), f32[16,4,8192]{2,1,0:T(4,128)}, u32[]{:S(2)}, u32[]{:S(2)}) %all-to-all-start.1) | async-done | bytes 2097184 | tf_op jit(solution)/shard_map/all_to_all | solution.py:90
  130.5 3.8 reshape.270
  134.3 3.6 fusion.94
  138.0 7.4 %fusion.21 = f32[256,64,64]{0,2,1:T(8,128)} fusion(f32[64,64,256]{2,1,0:T(8,128)S(1)} %fusion.94, f32[64,64,256]{2,1,0:T(8,128)S(1)} %copy-done.5, bf16[256,64,64]{0,2,1:T(8,128)(2,1)S(1)} %bitcast.127, f32[256,64]{0,1:T(8,128)S(1)} %copy-done.10, f32[256,64]{0,1:T(8,128)S(1)} %copy-done.12, f32[256,256]{1,0:T(8,128)S(1)} %fusion.116, ...), kind=kOutput, calls=%fused_computation.40 | convolution fusion | flops 565182464 | bytes 15204608 | tf_op jit(solution)/shard_map/while/body/eval_jaxpr/tsh,shp->thp/dot_general | solution.py:18
  145.4 5.6 %copy.103 = f32[256,4096]{1,0:T(8,128)} copy(f32[256,4096]{0,1:T(8,128)} %bitcast.121) | data formatting | bytes 8388608 | tf_op jit(solution)/shard_map/reshape | solution.py:102
  151.1 4.7 %multiply_reduce_fusion = f32[256]{0:T(256)S(1)} fusion(f32[256,4096]{1,0:T(8,128)} %copy.103, bf16[256,4096]{1,0:T(8,128)(2,1)} %param.18), kind=kLoop, calls=%fused_computation.45 | loop fusion | flops 8388352 | bytes 6292480 | tf_op jit(solution)/shard_map/reduce_sum | solution.py:105
  155.8 0.4 copy-done.4
  156.2 1.7 multiply_convert_fusion.4
  157.9 1.2 constant_dynamic-slice_fusion.2
  159.0 2.8 collective-permute-done
  161.8 14.4 %all-gather.2.cloned.1.call-done = bf16[2048,4096]{1,0:T(8,128)(2,1)} async-done(((bf16[2048,256]{1,0:T(8,128)(2,1)}), bf16[2048,4096]{1,0:T(8,128)(2,1)}) %all-gather.2.cloned.1.call-update) | async-done | bytes 16777232 | tf_op jit(solution)/shard_map/wgather/all_gather | solution.py:112
  176.2 12.2 %fusion.35 = f32[512,4096]{1,0:T(8,128)S(1)} fusion(bf16[2048,4096]{1,0:T(8,128)(2,1)} %all-gather.2.cloned.1.call-done, bf16[256,2048]{1,0:T(8,128)(2,1)} %get-tuple-element.38, bf16[256,2048]{1,0:T(8,128)(2,1)} %collective-permute-done), kind=kOutput, calls=%fused_computation.59 | convolution fusion | flops 8594128896 | bytes 27262976 | tf_op jit(solution)/shard_map/dot_general | solution.py:120
  188.5 2.7 slice.92
  191.2 1.7 copy-done.3
  192.9 0.2 collective-permute-start.1
  193.3 0.1 eq.147
  193.4 0.1 eq.143
  193.6 1.2 reduce-window.24
  194.7 0.2 slice_reduce_fusion.1
  195.1 0.1 sub.48
  195.5 5.1 %collective-permute-done.1 = f32[256,4096]{1,0:T(8,128)} collective-permute-done((f32[256,4096]{1,0:T(8,128)}, f32[256,4096]{1,0:T(8,128)}, u32[]{:S(2)}, u32[]{:S(2)}) %collective-permute-start.1) | collective-permute-done | bytes 4194336 | tf_op jit(solution)/shard_map/ppermute | solution.py:125
  200.6 5.0 %fusion.15 = (f32[256]{0:T(256)S(1)}, bf16[256,4096]{1,0:T(8,128)(2,1)S(1)}) fusion(f32[256,4096]{1,0:T(8,128)} %collective-permute-done.1, f32[512,4096]{1,0:T(8,128)} %copy-done.3, bf16[256,4096]{1,0:T(8,128)(2,1)} %param.27), kind=kLoop, calls=%fused_computation.32 | loop fusion | flops 9436928 | bytes 12583936 | tf_op jit(solution)/shard_map/reduce_sum | solution.py:131
  205.7 2.8 convolution_convert_fusion.3
  208.5 5.0 %all-to-all-start.2 = ((bf16[16,24,4096]{2,1,0:T(8,128)(2,1)}), bf16[16,24,4096]{2,1,0:T(8,128)(2,1)}, u32[]{:S(2)}, u32[]{:S(2)}) async-start(bf16[16,24,4096]{2,1,0:T(8,128)(2,1)} %bitcast.125), calls=%async_computation.2 | async-start | bytes 6291456 | tf_op jit(solution)/shard_map/all_to_all | solution.py:164
  213.6 4.4 %convolution_convert_fusion.1 = bf16[384,4096]{1,0:T(8,128)(2,1)} fusion(s32[256]{0:T(256)S(1)} %bitcast.130, s32[256]{0:T(256)S(1)} %bitcast.134, s32[384]{0:T(512)S(1)} %eq.164, bf16[256,4096]{1,0:T(8,128)(2,1)} %copy-done.2, f32[4096]{0:T(1024)S(1)} %copy-done.18, f32[256]{0:T(256)S(1)} %add_rsqrt_fusion), kind=kOutput, calls=%fused_computation.15 | convolution fusion | flops 811368448 | bytes 5263872 | tf_op jit(solution)/shard_map/dot_general | solution.py:160
  218.0 44.0 %all-to-all-done.2 = bf16[16,24,4096]{2,1,0:T(8,128)(2,1)} async-done(((bf16[16,24,4096]{2,1,0:T(8,128)(2,1)}), bf16[16,24,4096]{2,1,0:T(8,128)(2,1)}, u32[]{:S(2)}, u32[]{:S(2)}) %all-to-all-start.2) | async-done | bytes 3145760 | tf_op jit(solution)/shard_map/all_to_all | solution.py:164
  262.0 4.5 %all-to-all-start.4 = ((bf16[16,24,4096]{2,1,0:T(8,128)(2,1)}), bf16[16,24,4096]{2,1,0:T(8,128)(2,1)}, u32[]{:S(2)}, u32[]{:S(2)}) async-start(bf16[16,24,4096]{2,1,0:T(8,128)(2,1)} %bitcast.124), calls=%async_computation.4 | async-start | bytes 6291456 | tf_op jit(solution)/shard_map/all_to_all | solution.py:164
  266.5 5.5 %fusion.33 = f32[384,384]{1,0:T(8,128)} fusion(bf16[384,4096]{1,0:T(8,128)(2,1)} %bitcast.17, bf16[1,4096,384]{2,1,0:T(8,128)(2,1)} %param.31), kind=kOutput, calls=%fused_computation.56 | convolution fusion | flops 1207959552 | bytes 6881280 | tf_op jit(solution)/shard_map/dot_general | solution.py:166
  272.0 8.1 %convolution_convert_fusion.2 = bf16[384,4096]{1,0:T(8,128)(2,1)} fusion(bf16[1,384,4096]{2,1,0:T(8,128)(2,1)S(1)} %copy-done, bf16[384,4096]{1,0:T(8,128)(2,1)} %bitcast.17, bf16[1,4096,384]{2,1,0:T(8,128)(2,1)} %param.32, f32[384,384]{1,0:T(8,128)} %fusion.33), kind=kOutput, calls=%fused_computation.16 | convolution fusion | flops 2418376704 | bytes 13172736 | tf_op jit(solution)/shard_map/dot_general | solution.py:169
  280.0 32.8 %all-to-all-done.4 = bf16[16,24,4096]{2,1,0:T(8,128)(2,1)} async-done(((bf16[16,24,4096]{2,1,0:T(8,128)(2,1)}), bf16[16,24,4096]{2,1,0:T(8,128)(2,1)}, u32[]{:S(2)}, u32[]{:S(2)}) %all-to-all-start.4) | async-done | bytes 3145760 | tf_op jit(solution)/shard_map/all_to_all | solution.py:164
  312.8 4.5 %all-to-all-start.3 = ((bf16[16,24,4096]{2,1,0:T(8,128)(2,1)}), bf16[16,24,4096]{2,1,0:T(8,128)(2,1)}, u32[]{:S(2)}, u32[]{:S(2)}) async-start(bf16[16,24,4096]{2,1,0:T(8,128)(2,1)} %bitcast.123), calls=%async_computation.3 | async-start | bytes 6291456 | tf_op jit(solution)/shard_map/all_to_all | solution.py:173
  317.3 5.5 %fusion.31 = f32[384,384]{1,0:T(8,128)} fusion(bf16[384,4096]{1,0:T(8,128)(2,1)} %bitcast.25, bf16[1,4096,384]{2,1,0:T(8,128)(2,1)} %param.31), kind=kOutput, calls=%fused_computation.54 | convolution fusion | flops 1207959552 | bytes 6881280 | tf_op jit(solution)/shard_map/dot_general | solution.py:166
  322.8 8.0 %convolution_convert_fusion = bf16[384,4096]{1,0:T(8,128)(2,1)} fusion(bf16[1,384,4096]{2,1,0:T(8,128)(2,1)S(1)} %copy-done, bf16[384,4096]{1,0:T(8,128)(2,1)} %bitcast.25, bf16[1,4096,384]{2,1,0:T(8,128)(2,1)} %param.32, f32[384,384]{1,0:T(8,128)} %fusion.31), kind=kOutput, calls=%fused_computation.14 | convolution fusion | flops 2418376704 | bytes 13172736 | tf_op jit(solution)/shard_map/dot_general | solution.py:169
  330.8 30.1 %all-to-all-done.3 = bf16[16,24,4096]{2,1,0:T(8,128)(2,1)} async-done(((bf16[16,24,4096]{2,1,0:T(8,128)(2,1)}), bf16[16,24,4096]{2,1,0:T(8,128)(2,1)}, u32[]{:S(2)}, u32[]{:S(2)}) %all-to-all-start.3) | async-done | bytes 3145760 | tf_op jit(solution)/shard_map/all_to_all | solution.py:173
  361.0 4.9 %all-to-all-start.5 = ((bf16[16,24,4096]{2,1,0:T(8,128)(2,1)}), bf16[16,24,4096]{2,1,0:T(8,128)(2,1)}, u32[]{:S(2)}, u32[]{:S(2)}) async-start(bf16[16,24,4096]{2,1,0:T(8,128)(2,1)} %bitcast.122), calls=%async_computation.5 | async-start | bytes 6291456 | tf_op jit(solution)/shard_map/all_to_all | solution.py:173
  366.0 0.1 reshape.288
  366.1 2.3 fusion.110
  368.5 4.6 %gather_fusion = f32[512]{0:T(512)S(1)} fusion(f32[256,16]{0,1:T(8,128)S(1)} %fusion.110, s32[512]{0:T(512)S(1)} %reshape.288), kind=kCustom, calls=%fused_computation | custom fusion | bytes 8192 | tf_op jit(solution)/shard_map/jit(take_along_axis)/gather | solution.py:135
  373.0 0.1 reshape.291
  373.3 3.9 convert_add_fusion
  377.2 5.2 %fusion.9 = f32[256,4096]{1,0:T(8,128)} fusion(f32[256,4096]{1,0:T(8,128)S(1)} %convert_add_fusion, bf16[384,4096]{1,0:T(8,128)(2,1)} %bitcast.22, f32[256]{0:T(256)S(1)} %bitcast.137, s32[384]{0:T(512)S(1)} %eq.153, s32[256]{0:T(256)S(1)} %bitcast.131), kind=kOutput, calls=%fused_computation.23 | convolution fusion | flops 807501824 | bytes 11537920 | tf_op jit(solution)/shard_map/dot_general | solution.py:178
  382.4 25.2 %all-to-all-done.5 = bf16[16,24,4096]{2,1,0:T(8,128)(2,1)} async-done(((bf16[16,24,4096]{2,1,0:T(8,128)(2,1)}), bf16[16,24,4096]{2,1,0:T(8,128)(2,1)}, u32[]{:S(2)}, u32[]{:S(2)}) %all-to-all-start.5) | async-done | bytes 3145760 | tf_op jit(solution)/shard_map/all_to_all | solution.py:173
  407.7 4.5 %fusion.8 = f32[256,4096]{1,0:T(8,128)S(1)} fusion(f32[256,4096]{1,0:T(8,128)} %fusion.9, bf16[384,4096]{1,0:T(8,128)(2,1)} %bitcast.27, f32[256]{0:T(256)S(1)} %bitcast.140, s32[384]{0:T(512)S(1)} %eq.164, s32[256]{0:T(256)S(1)} %bitcast.136), kind=kOutput, calls=%fused_computation.21 | convolution fusion | flops 807501824 | bytes 11537920 | tf_op jit(solution)/shard_map/dot_general | solution.py:178
  412.2 4.6 %fusion.10 = bf16[256,4096]{1,0:T(8,128)(2,1)} fusion(f32[256,4096]{1,0:T(8,128)S(1)} %fusion.8, bf16[384,4096]{1,0:T(8,128)(2,1)} %bitcast.27, f32[256]{0:T(256)S(1)} %bitcast.138, s32[384]{0:T(512)S(1)} %eq.164, s32[256]{0:T(256)S(1)} %bitcast.132), kind=kOutput, calls=%fused_computation.27 | convolution fusion | flops 808550400 | bytes 9440768 | tf_op jit(solution)/shard_map/dot_general | solution.py:178
  (79 shorter events, 1.6 us)
Async XLA Ops:
  6.5 265.4 %copy-start = (bf16[1,384,4096]{2,1,0:T(8,128)(2,1)S(1)}, bf16[1,384,4096]{2,1,0:T(8,128)(2,1)}, u32[]{:S(2)}) copy-start(bf16[1,384,4096]{2,1,0:T(8,128)(2,1)} %param.33) | copy-start | bytes 9437188
  6.5 2.6 copy-start.19
  6.5 2.6 copy-start.13
  6.5 2.6 copy-start.16
  6.5 169.7 %all-gather.2.cloned.1.call-start = ((), (), s32[]{:S(2)}) async-start(), calls=%async_computation.6 | async-start | bytes 17825792 | tf_op jit(solution)/shard_map/wgather/all_gather | solution.py:112
  9.1 5.1 %copy-start.8 = (bf16[256,128]{1,0:T(8,128)(2,1)S(1)}, bf16[256,128]{1,0:T(8,128)(2,1)}, u32[]{:S(2)}) copy-start(bf16[256,128]{1,0:T(8,128)(2,1)} %param.19) | copy-start | bytes 196612
  9.3 11.2 %copy-start.9 = (f32[256,64]{0,1:T(8,128)}, f32[256,64]{0,1:T(8,128)S(1)}, u32[]{:S(2)}) copy-start(f32[256,64]{0,1:T(8,128)S(1)} %get-tuple-element.36) | copy-start | bytes 196612
  14.3 9.3 %copy-start.11 = (f32[256,64]{0,1:T(8,128)}, f32[256,64]{0,1:T(8,128)S(1)}, u32[]{:S(2)}) copy-start(f32[256,64]{0,1:T(8,128)S(1)} %bitcast_bitcast_fusion) | copy-start | bytes 196612
  27.3 46.5 %all-to-all-start = ((f32[16,4,8320]{2,1,0:T(4,128)}), f32[16,4,8320]{2,1,0:T(4,128)}, u32[]{:S(2)}, u32[]{:S(2)}) async-start(f32[16,4,8320]{2,1,0:T(4,128)} %pad_maximum_fusion), calls=%async_computation | async-start | bytes 4259840 | tf_op jit(solution)/shard_map/all_to_all | solution.py:78
  82.5 5.4 %copy-start.7 = (bf16[256,128]{1,0:T(8,128)(2,1)S(1)}, bf16[256,128]{1,0:T(8,128)(2,1)}, u32[]{:S(2)}) copy-start(bf16[256,128]{1,0:T(8,128)(2,1)} %param.20) | copy-start | bytes 196612
  82.5 48.0 %all-to-all-start.1 = ((f32[16,4,8192]{2,1,0:T(4,128)}), f32[16,4,8192]{2,1,0:T(4,128)}, u32[]{:S(2)}, u32[]{:S(2)}) async-start(f32[16,4,8192]{2,1,0:T(4,128)} %copy.102), calls=%async_computation.1 | async-start | bytes 4194304 | tf_op jit(solution)/shard_map/all_to_all | solution.py:90
  130.5 7.4 %copy-start.12 = (f32[256,64]{0,1:T(8,128)S(1)}, f32[256,64]{0,1:T(8,128)}, u32[]{:S(2)}) copy-start(f32[256,64]{0,1:T(8,128)} %copy-done.11) | copy-start | bytes 196612
  134.3 3.7 copy-start.5
  134.3 3.7 copy-start.6
  134.3 3.7 copy-start.10
  134.3 3.7 copy-start.20
  145.4 10.4 %copy-start.15 = (f32[4096]{0:T(1024)S(1)}, f32[4096]{0:T(1024)}, u32[]{:S(2)}) copy-start(f32[4096]{0:T(1024)} %param.25) | copy-start | bytes 49156
  151.1 4.7 %copy-start.1 = (f32[256,4096]{1,0:T(8,128)S(1)}, f32[256,4096]{1,0:T(8,128)}, u32[]{:S(2)}) copy-start(f32[256,4096]{1,0:T(8,128)} %copy.103) | copy-start | bytes 12582916
  151.1 5.1 %copy-start.4 = (bf16[256,4096]{1,0:T(8,128)(2,1)S(1)}, bf16[256,4096]{1,0:T(8,128)(2,1)}, u32[]{:S(2)}) copy-start(bf16[256,4096]{1,0:T(8,128)(2,1)} %param.18) | copy-start | bytes 6291460
  159.0 2.8 collective-permute-start
  188.4 4.5 %copy-start.3 = (f32[512,4096]{1,0:T(8,128)}, f32[512,4096]{1,0:T(8,128)S(1)}, u32[]{:S(2)}) copy-start(f32[512,4096]{1,0:T(8,128)S(1)} %fusion.35) | copy-start | bytes 25165828
  188.5 4.7 %copy-start.14 = (s32[256,2]{0,1:T(2,128)S(1)}, s32[256,2]{0,1:T(2,128)}, u32[]{:S(2)}) copy-start(s32[256,2]{0,1:T(2,128)} %param.30) | copy-start | bytes 6148
  192.9 7.7 %collective-permute-start.1 = (f32[256,4096]{1,0:T(8,128)}, f32[256,4096]{1,0:T(8,128)}, u32[]{:S(2)}, u32[]{:S(2)}) collective-permute-start(f32[256,4096]{1,0:T(8,128)} %slice.92), channel_id=1, source_target_pairs={{0,1},{1,0},{2,3},{3,2},{4,5},{5,4},{6,7},{7,6},{8,9},{9,8},{10,11... | collective-permute-start | bytes 12582920 | tf_op jit(solution)/shard_map/ppermute | solution.py:125
  195.5 10.2 %copy-start.18 = (f32[4096]{0:T(1024)S(1)}, f32[4096]{0:T(1024)}, u32[]{:S(2)}) copy-start(f32[4096]{0:T(1024)} %param.28) | copy-start | bytes 49156
  205.6 2.8 copy-start.2
  208.5 53.5 %all-to-all-start.2 = ((bf16[16,24,4096]{2,1,0:T(8,128)(2,1)}), bf16[16,24,4096]{2,1,0:T(8,128)(2,1)}, u32[]{:S(2)}, u32[]{:S(2)}) async-start(bf16[16,24,4096]{2,1,0:T(8,128)(2,1)} %bitcast.125), calls=%async_computation.2 | async-start | bytes 6291456 | tf_op jit(solution)/shard_map/all_to_all | solution.py:164
  262.0 50.8 %all-to-all-start.4 = ((bf16[16,24,4096]{2,1,0:T(8,128)(2,1)}), bf16[16,24,4096]{2,1,0:T(8,128)(2,1)}, u32[]{:S(2)}, u32[]{:S(2)}) async-start(bf16[16,24,4096]{2,1,0:T(8,128)(2,1)} %bitcast.124), calls=%async_computation.4 | async-start | bytes 6291456 | tf_op jit(solution)/shard_map/all_to_all | solution.py:164
  312.8 48.1 %all-to-all-start.3 = ((bf16[16,24,4096]{2,1,0:T(8,128)(2,1)}), bf16[16,24,4096]{2,1,0:T(8,128)(2,1)}, u32[]{:S(2)}, u32[]{:S(2)}) async-start(bf16[16,24,4096]{2,1,0:T(8,128)(2,1)} %bitcast.123), calls=%async_computation.3 | async-start | bytes 6291456 | tf_op jit(solution)/shard_map/all_to_all | solution.py:173
  361.0 5.2 %copy-start.17 = (bf16[4096,16]{0,1:T(8,128)(2,1)S(1)}, bf16[4096,16]{0,1:T(8,128)(2,1)}, u32[]{:S(2)}) copy-start(bf16[4096,16]{0,1:T(8,128)(2,1)} %param.29) | copy-start | bytes 393220
  361.0 46.7 %all-to-all-start.5 = ((bf16[16,24,4096]{2,1,0:T(8,128)(2,1)}), bf16[16,24,4096]{2,1,0:T(8,128)(2,1)}, u32[]{:S(2)}, u32[]{:S(2)}) async-start(bf16[16,24,4096]{2,1,0:T(8,128)(2,1)} %bitcast.122), calls=%async_computation.5 | async-start | bytes 6291456 | tf_op jit(solution)/shard_map/all_to_all | solution.py:173
Sparse Core Ops, SparseCore 0:
  9.5 166.7 all-gather.1

commit v5 on v3

--- a/solution.py
+++ b/solution.py
@@ -70,23 +70,22 @@
     slab_total = slab_log[-1]
     n_seq = lax.axis_size("seq")
     per_chunk = heads // n_seq
-    flat_state = segment_state.reshape(heads, head_width * state_width)
-    with jax.named_scope("state_pack"):
-        packed = jnp.concatenate(
-            [flat_state, jnp.broadcast_to(slab_total[:, None], (heads, 128))], axis=1
-        ).reshape(n_seq, per_chunk, head_width * state_width + 128)
+    chunk_rows = per_chunk * head_width
+    state_rows = segment_state.reshape(n_seq, chunk_rows, state_width)
+    total_rows = jnp.broadcast_to(slab_total.reshape(n_seq, per_chunk, 1), (n_seq, per_chunk, state_width))
+    total_block = jnp.pad(total_rows, ((0, 0), (0, 8 - per_chunk), (0, 0)))
+    packed = jnp.concatenate([state_rows, total_block], axis=1)
     received = lax.all_to_all(packed, "seq", 0, 0, tiled=True)
-    slab_states = received[:, :, : head_width * state_width]
-    slab_totals = received[:, :, head_width * state_width]
-
+    slab_states = received[:, :chunk_rows].reshape(n_seq, per_chunk, head_width, state_width)
+    slab_totals = received[:, chunk_rows : chunk_rows + per_chunk, 0]
     order = jnp.arange(n_seq)
     between = (order[None, None, :] > order[None, :, None]) & (order[None, None, :] < order[:, None, None])
     span = jnp.sum(jnp.where(between[:, :, :, None], slab_totals[None, None, :, :], 0.0), axis=2)
     earlier = (order[:, None] > order[None, :])[:, :, None]
     carry_weights = jnp.where(earlier, jnp.exp(span), 0.0)
-    entering_each = jnp.einsum(
-        "ijh,jhx->ihx", carry_weights, slab_states, precision=lax.Precision.HIGHEST
-    )
+    entering_each = jnp.sum(
+        carry_weights[:, :, :, None, None] * slab_states[None], axis=1
+    ).reshape(n_seq, chunk_rows, state_width)
     entering = lax.all_to_all(entering_each, "seq", 0, 0, tiled=True).reshape(
         heads, head_width, state_width
     )

time: 420 us -> 420 us (level)
  waiting for transfers between devices: 177 us -> 189 us
  local copies, waits for them, and re-layouts: 33.5 us -> 24 us
    all_gather x1, waiting for transfers between devices: 13.2 us -> 19.6 us  [shards(): lax.all_gather(lax.dynamic_slice_in_dim(w_out, core * depth, depth, axis=...]
    reduce_sum x0 -> x1, other arithmetic: none -> 5.48 us  [shards(): jnp.sum(carry_weights[:, :, :, None, None] * slab_states[None], axis=1)]
  transfers between devices with their start and end apart: 6 -> 6, of which waited for: 5 -> 5; matrix products, arithmetic and copies ran while one was open for 19% -> 16% of each run, Pallas kernels for 0% -> 0%
where the time goes in v5:
time: 420 us; the launch traced here: 414 us
  waiting for transfers between devices  189 us (45%)
  blocking collectives  79.7 us (19%)
  matrix products  68.8 us (16%)
  local copies, waits for them, and re-layouts  24 us (6%)
  other arithmetic  21 us (5%)
  starting transfers between devices  16.9 us (4%)
  between operations  14.3 us (3%)
    all_to_all x1, waiting for transfers between devices, shards(): lax.all_to_all(finished, 'seq', split_axis=0, concat_axis=0, tiled=True)  85.2 us
    all_to_all x1, blocking collectives, shards(): lax.all_to_all(departing_state, 'seq', split_axis=0, concat_axis=0, tiled...  79.7 us
    all_to_all x1, waiting for transfers between devices, shards(): received = lax.all_to_all(packed, 'seq', 0, 0, tiled=True)  41.1 us
    all_to_all x1, waiting for transfers between devices, shards(): lax.all_to_all(entering_each, 'seq', 0, 0, tiled=True)  40.4 us
    all_gather x1, waiting for transfers between devices, shards(): lax.all_gather(lax.dynamic_slice_in_dim(w_out, core * depth, depth, axis=...  19.6 us
    dot_general x1, matrix products, shards(): jnp.dot(partner_rows, w_rows, preferred_element_type=jnp.float32)  12.5 us
    dot_general x2, matrix products, shards(): fetched = jnp.dot(picking, returned, preferred_element_type=jnp.float32)  11.4 us
    dot_general x1, matrix products, shards(): own_part = jnp.dot(own_rows, w_rows, preferred_element_type=jnp.float32)  8.58 us
  transfers between devices with their start and end apart: 6, of which 5 were waited for; matrix products, arithmetic and copies ran while one was open for 16% of the time, Pallas kernels for 0%

profile of v5, /device:TPU:0, one launch (start us, length us, event | category | flops | bytes accessed | tf_op | source)
XLA Modules:
  0.0 413.7 jit_solution(16397261112441772093)
XLA Ops:
  6.5 2.5 constant_dynamic-slice_fusion.1
  9.1 0.7 exp.47
  9.8 1.0 multiply_bitcast_fusion
  10.7 0.6 reduce-window.16
  11.3 0.2 slice_reduce_fusion
  11.6 4.1 copy.95
  15.7 0.1 bitcast_bitcast_fusion
  15.8 0.2 slice_reduce_fusion.2
  15.9 0.1 broadcast_in_dim.120
  16.0 0.7 fusion.57
  16.7 4.6 %fusion.27 = f32[64,128,64]{1,2,0:T(8,128)S(1)} fusion(bf16[256,64,64]{0,2,1:T(8,128)(2,1)} %bitcast.111, f32[256,128]{1,0:T(8,128)S(1)} %convert_element_type.66, f32[256,64]{0,1:T(8,128)S(1)} %get-tuple-element.36, f32[64]{0:T(128)S(1)} %exponential_multiply_fusion.1), kind=kOutput, calls=%fused_computation.48 | convolution fusion | flops 273154048 | bytes 4391168 | tf_op jit(solution)/shard_map/while/body/eval_jaxpr/shn,shp->hpn/dot_general | solution.py:27
  21.4 0.1 broadcast_in_dim.121
  21.4 1.5 select_maximum_fusion
  22.9 7.2 %all-to-all-start = ((f32[16,264,128]{2,1,0:T(8,128)}), f32[16,264,128]{2,1,0:T(8,128)}, u32[]{:S(2)}, u32[]{:S(2)}) async-start(f32[16,264,128]{2,1,0:T(8,128)} %select_maximum_fusion), calls=%async_computation | async-start | bytes 4325376 | tf_op jit(solution)/shard_map/all_to_all | solution.py:78
  30.2 41.1 %all-to-all-done = f32[16,264,128]{2,1,0:T(8,128)} async-done(((f32[16,264,128]{2,1,0:T(8,128)}), f32[16,264,128]{2,1,0:T(8,128)}, u32[]{:S(2)}, u32[]{:S(2)}) %all-to-all-start) | async-done | bytes 2162720 | tf_op jit(solution)/shard_map/all_to_all | solution.py:78
  71.3 0.8 slice.55
  72.2 0.1 copy.96
  72.3 0.2 select_reduce_fusion
  72.5 0.2 copy.97
  72.7 1.7 slice.56
  74.5 5.5 %multiply_reduce_fusion = f32[16,4,64,128]{3,2,1,0:T(8,128)} fusion(f32[16,4,64,128]{3,2,1,0:T(8,128)S(1)} %bitcast.106, f32[16,16,4]{2,1,0:T(8,128)S(1)} %copy.97), kind=kLoop, calls=%fused_computation.1 | loop fusion | flops 16252928 | bytes 4198400 | tf_op jit(solution)/shard_map/reduce_sum | solution.py:86
  80.0 4.6 %all-to-all-start.1 = ((f32[16,256,128]{2,1,0:T(8,128)}), f32[16,256,128]{2,1,0:T(8,128)}, u32[]{:S(2)}, u32[]{:S(2)}) async-start(f32[16,256,128]{2,1,0:T(8,128)} %bitcast.105), calls=%async_computation.1 | async-start | bytes 4194304 | tf_op jit(solution)/shard_map/all_to_all | solution.py:89
  84.6 0.6 iota_compare_fusion.8
  85.2 0.2 fusion.62
  85.4 3.7 fusion.36
  89.1 40.4 %all-to-all-done.1 = f32[16,256,128]{2,1,0:T(8,128)} async-done(((f32[16,256,128]{2,1,0:T(8,128)}), f32[16,256,128]{2,1,0:T(8,128)}, u32[]{:S(2)}, u32[]{:S(2)}) %all-to-all-start.1) | async-done | bytes 2097184 | tf_op jit(solution)/shard_map/all_to_all | solution.py:89
  129.5 3.6 fusion.47
  133.2 0.2 copy-done.7
  133.3 7.5 %fusion.18 = f32[256,64,64]{0,2,1:T(8,128)} fusion(f32[64,64,256]{2,1,0:T(8,128)S(1)} %fusion.47, f32[64,64,256]{2,1,0:T(8,128)S(1)} %copy-done.5, bf16[256,64,64]{0,2,1:T(8,128)(2,1)S(1)} %bitcast.112, f32[256,64]{0,1:T(8,128)S(1)} %copy-done.11, f32[256,64]{0,1:T(8,128)} %copy-done.12, f32[256,256]{1,0:T(8,128)S(1)} %fusion.62, ...), kind=kOutput, calls=%fused_computation.32 | convolution fusion | flops 565182464 | bytes 15204608 | tf_op jit(solution)/shard_map/while/body/eval_jaxpr/tsh,shp->thp/dot_general | solution.py:18
  140.8 5.6 %copy.98 = f32[256,4096]{1,0:T(8,128)} copy(f32[256,4096]{0,1:T(8,128)} %bitcast.110) | data formatting | bytes 8388608 | tf_op jit(solution)/shard_map/reshape | solution.py:101
  146.5 4.5 %multiply_reduce_fusion.1 = f32[256]{0:T(256)S(1)} fusion(f32[256,4096]{1,0:T(8,128)} %copy.98, bf16[256,4096]{1,0:T(8,128)(2,1)} %param.18), kind=kLoop, calls=%fused_computation.38 | loop fusion | flops 8388352 | bytes 6292480 | tf_op jit(solution)/shard_map/reduce_sum | solution.py:104
  151.0 0.2 copy-done.3
  151.2 1.7 multiply_convert_fusion.4
  152.9 1.3 copy-done.4
  154.2 0.1 constant_dynamic-slice_fusion
  154.2 0.3 collective-permute-start
  154.6 2.8 collective-permute-done
  157.3 19.6 %all-gather.2.cloned.1.call-done = bf16[2048,4096]{1,0:T(8,128)(2,1)} async-done(((bf16[2048,256]{1,0:T(8,128)(2,1)}), bf16[2048,4096]{1,0:T(8,128)(2,1)}) %all-gather.2.cloned.1.call-update) | async-done | bytes 16777232 | tf_op jit(solution)/shard_map/wgather/all_gather | solution.py:111
  176.9 12.5 %fusion.63 = f32[256,4096]{1,0:T(8,128)} fusion(bf16[256,2048]{1,0:T(8,128)(2,1)} %collective-permute-done, bf16[2048,4096]{1,0:T(8,128)(2,1)} %all-gather.2.cloned.1.call-done), kind=kOutput, calls=%fused_computation.111 | convolution fusion | flops 4294967296 | bytes 22020096 | tf_op jit(solution)/shard_map/dot_general | solution.py:120
  189.4 0.1 copy.101
  189.6 0.1 eq.87
  189.7 0.1 eq.83
  189.9 1.2 reduce-window.24
  191.0 0.2 slice_reduce_fusion.1
  191.3 0.1 fusion.51
  191.4 0.1 sub.48
  191.5 0.1 copy.104
  191.6 8.6 %fusion.34 = f32[256,4096]{1,0:T(8,128)S(1)} fusion(bf16[2048,4096]{1,0:T(8,128)(2,1)} %all-gather.2.cloned.1.call-done, bf16[256,4096]{1,0:T(8,128)(2,1)} %copy-done.4, s32[]{:T(128)S(6)} %select_n.48), kind=kOutput, calls=%fused_computation.51 | convolution fusion | flops 4294967296 | bytes 22020100 | tf_op jit(solution)/shard_map/dot_general | solution.py:119
  200.3 3.1 fusion.13
  203.4 2.0 convolution_convert_fusion
  205.4 79.7 %all_to_all.20 = bf16[16,48,4096]{2,1,0:T(8,128)(2,1)S(1)} all-to-all(bf16[16,48,4096]{2,1,0:T(8,128)(2,1)S(1)} %bitcast.104), channel_id=1, replica_groups=mesh['seq'=16,'batch'=8] {'seq'}, dimensions={0} | all-to-all | bytes 12582912 | tf_op jit(solution)/shard_map/all_to_all | solution.py:155
  285.2 3.4 fusion.25
  288.6 3.5 fusion.31
  292.1 5.4 %convolution_convert_fusion.1 = bf16[768,4096]{1,0:T(8,128)(2,1)} fusion(bf16[768,384]{1,0:T(8,128)(2,1)S(1)} %fusion.31, bf16[1,384,4096]{2,1,0:T(8,128)(2,1)S(1)} %copy-done), kind=kOutput, calls=%fused_computation.12 | convolution fusion | flops 2419064832 | bytes 10027008 | tf_op jit(solution)/shard_map/dot_general | solution.py:160
  297.5 4.8 %all-to-all-start.3 = ((bf16[16,48,4096]{2,1,0:T(8,128)(2,1)}), bf16[16,48,4096]{2,1,0:T(8,128)(2,1)}, u32[]{:S(2)}, u32[]{:S(2)}) async-start(bf16[16,48,4096]{2,1,0:T(8,128)(2,1)} %bitcast.107), calls=%async_computation.3 | async-start | bytes 12582912 | tf_op jit(solution)/shard_map/all_to_all | solution.py:164
  302.3 0.1 copy.99
  302.4 0.1 reshape.196
  302.6 2.3 fusion.41
  304.9 4.6 %gather_fusion = f32[512]{0:T(512)S(1)} fusion(f32[256,16]{0,1:T(8,128)S(1)} %fusion.41, s32[512]{0:T(512)S(1)} %reshape.196), kind=kCustom, calls=%fused_computation | custom fusion | bytes 8192 | tf_op jit(solution)/shard_map/jit(take_along_axis)/gather | solution.py:131
  309.5 0.1 reshape.199
  309.6 0.1 copy.100
  309.8 85.2 %all-to-all-done.3 = bf16[16,48,4096]{2,1,0:T(8,128)(2,1)} async-done(((bf16[16,48,4096]{2,1,0:T(8,128)(2,1)}), bf16[16,48,4096]{2,1,0:T(8,128)(2,1)}, u32[]{:S(2)}, u32[]{:S(2)}) %all-to-all-start.3) | async-done | bytes 6291488 | tf_op jit(solution)/shard_map/all_to_all | solution.py:164
  394.9 5.3 %convert_add_fusion = f32[256,4096]{1,0:T(8,128)S(1)} fusion(bf16[256,4096]{1,0:T(8,128)(2,1)} %copy-done.2, bf16[768,4096]{1,0:T(8,128)(2,1)} %bitcast.25, f32[256]{0:T(256)S(1)} %bitcast.120, s32[256]{0:T(256)S(1)} %bitcast.116), kind=kOutput, calls=%fused_computation.13 | convolution fusion | flops 1613955072 | bytes 12584960 | tf_op jit(solution)/shard_map/dot_general | solution.py:170
  400.2 6.1 %fusion.8 = bf16[256,4096]{1,0:T(8,128)(2,1)} fusion(f32[256,4096]{1,0:T(8,128)S(1)} %convert_add_fusion, bf16[768,4096]{1,0:T(8,128)(2,1)} %bitcast.25, f32[256]{0:T(256)S(1)} %bitcast.121, s32[256]{0:T(256)S(1)} %bitcast.118), kind=kOutput, calls=%fused_computation.21 | convolution fusion | flops 1613955072 | bytes 12584960 | tf_op jit(solution)/shard_map/dot_general | solution.py:170
  (62 shorter events, 0.4 us)
Async XLA Ops:
  6.5 285.5 %copy-start = (bf16[1,384,4096]{2,1,0:T(8,128)(2,1)S(1)}, bf16[1,384,4096]{2,1,0:T(8,128)(2,1)}, u32[]{:S(2)}) copy-start(bf16[1,384,4096]{2,1,0:T(8,128)(2,1)} %param.33) | copy-start | bytes 9437188
  6.5 9.1 %copy-start.9 = (bf16[256,128]{1,0:T(8,128)(2,1)S(1)}, bf16[256,128]{1,0:T(8,128)(2,1)}, u32[]{:S(2)}) copy-start(bf16[256,128]{1,0:T(8,128)(2,1)} %param.19) | copy-start | bytes 196612
  6.5 170.3 %all-gather.2.cloned.1.call-start = ((), (), s32[]{:S(2)}) async-start(), calls=%async_computation.4 | async-start | bytes 17825792 | tf_op jit(solution)/shard_map/wgather/all_gather | solution.py:111
  10.7 10.6 %copy-start.10 = (f32[256,64]{0,1:T(8,128)}, f32[256,64]{0,1:T(8,128)S(1)}, u32[]{:S(2)}) copy-start(f32[256,64]{0,1:T(8,128)S(1)} %get-tuple-element.32) | copy-start | bytes 196612
  15.7 7.2 %copy-start.12 = (f32[256,64]{0,1:T(8,128)}, f32[256,64]{0,1:T(8,128)S(1)}, u32[]{:S(2)}) copy-start(f32[256,64]{0,1:T(8,128)S(1)} %bitcast_bitcast_fusion) | copy-start | bytes 196612
  22.9 48.4 %all-to-all-start = ((f32[16,264,128]{2,1,0:T(8,128)}), f32[16,264,128]{2,1,0:T(8,128)}, u32[]{:S(2)}, u32[]{:S(2)}) async-start(f32[16,264,128]{2,1,0:T(8,128)} %select_maximum_fusion), calls=%async_computation | async-start | bytes 4325376 | tf_op jit(solution)/shard_map/all_to_all | solution.py:78
  74.5 10.8 %copy-start.8 = (bf16[256,128]{1,0:T(8,128)(2,1)S(1)}, bf16[256,128]{1,0:T(8,128)(2,1)}, u32[]{:S(2)}) copy-start(bf16[256,128]{1,0:T(8,128)(2,1)} %param.20) | copy-start | bytes 196612
  80.0 49.5 %all-to-all-start.1 = ((f32[16,256,128]{2,1,0:T(8,128)}), f32[16,256,128]{2,1,0:T(8,128)}, u32[]{:S(2)}, u32[]{:S(2)}) async-start(f32[16,256,128]{2,1,0:T(8,128)} %bitcast.105), calls=%async_computation.1 | async-start | bytes 4194304 | tf_op jit(solution)/shard_map/all_to_all | solution.py:89
  89.1 44.0 %copy-start.11 = (f32[256,64]{0,1:T(8,128)S(1)}, f32[256,64]{0,1:T(8,128)}, u32[]{:S(2)}) copy-start(f32[256,64]{0,1:T(8,128)} %copy-done.10) | copy-start | bytes 196612
  89.1 44.0 %copy-start.19 = (f32[64]{0:T(128)S(1)}, f32[64]{0:T(128)}, u32[]{:S(2)}) copy-start(f32[64]{0:T(128)} %param.24) | copy-start | bytes 772
  129.5 3.7 copy-start.5
  129.5 3.8 copy-start.7
  140.8 10.2 %copy-start.14 = (f32[4096]{0:T(1024)S(1)}, f32[4096]{0:T(1024)}, u32[]{:S(2)}) copy-start(f32[4096]{0:T(1024)} %param.25) | copy-start | bytes 49156
  146.5 4.5 %copy-start.1 = (f32[256,4096]{1,0:T(8,128)S(1)}, f32[256,4096]{1,0:T(8,128)}, u32[]{:S(2)}) copy-start(f32[256,4096]{1,0:T(8,128)} %copy.98) | copy-start | bytes 12582916
  146.5 4.7 %copy-start.3 = (bf16[256,4096]{1,0:T(8,128)(2,1)S(1)}, bf16[256,4096]{1,0:T(8,128)(2,1)}, u32[]{:S(2)}) copy-start(bf16[256,4096]{1,0:T(8,128)(2,1)} %param.18) | copy-start | bytes 6291460
  152.8 1.3 copy-start.4
  154.2 35.2 %copy-start.13 = (s32[256,2]{0,1:T(2,128)S(1)}, s32[256,2]{0,1:T(2,128)}, u32[]{:S(2)}) copy-start(s32[256,2]{0,1:T(2,128)} %param.30) | copy-start | bytes 6148
  154.2 3.1 collective-permute-start
  189.4 10.8 %collective-permute-start.1 = (f32[256,4096]{1,0:T(8,128)}, f32[256,4096]{1,0:T(8,128)}, u32[]{:S(2)}, u32[]{:S(2)}) collective-permute-start(f32[256,4096]{1,0:T(8,128)} %fusion.63), channel_id=1, source_target_pairs={{0,1},{1,0},{2,3},{3,2},{4,5},{5,4},{6,7},{7,6},{8,9},{9,8},{10,11... | collective-permute-start | bytes 12582920 | tf_op jit(solution)/shard_map/ppermute | solution.py:121
  191.6 8.6 %copy-start.6 = (bf16[256,4096]{1,0:T(8,128)(2,1)S(1)}, bf16[256,4096]{1,0:T(8,128)(2,1)}, u32[]{:S(2)}) copy-start(bf16[256,4096]{1,0:T(8,128)(2,1)} %param.27) | copy-start | bytes 6291460
  200.2 3.2 copy-start.15
  203.4 2.0 copy-start.2
  205.4 79.8 %copy-start.16 = (bf16[1,4096,384]{2,1,0:T(8,128)(2,1)S(1)}, bf16[1,4096,384]{2,1,0:T(8,128)(2,1)}, u32[]{:S(2)}) copy-start(bf16[1,4096,384]{2,1,0:T(8,128)(2,1)} %param.31) | copy-start | bytes 9437188
  285.2 3.4 copy-start.17
  297.5 5.1 %copy-start.18 = (bf16[4096,16]{0,1:T(8,128)(2,1)S(1)}, bf16[4096,16]{0,1:T(8,128)(2,1)}, u32[]{:S(2)}) copy-start(bf16[4096,16]{0,1:T(8,128)(2,1)} %param.29) | copy-start | bytes 393220
  297.5 97.4 %all-to-all-start.3 = ((bf16[16,48,4096]{2,1,0:T(8,128)(2,1)}), bf16[16,48,4096]{2,1,0:T(8,128)(2,1)}, u32[]{:S(2)}, u32[]{:S(2)}) async-start(bf16[16,48,4096]{2,1,0:T(8,128)(2,1)} %bitcast.107), calls=%async_computation.3 | async-start | bytes 12582912 | tf_op jit(solution)/shard_map/all_to_all | solution.py:164
Sparse Core Ops, SparseCore 0:
  9.4 167.3 all-gather.1

commit v6 on v5

--- a/solution.py
+++ b/solution.py
@@ -72,12 +72,25 @@
     per_chunk = heads // n_seq
     chunk_rows = per_chunk * head_width
     state_rows = segment_state.reshape(n_seq, chunk_rows, state_width)
-    total_rows = jnp.broadcast_to(slab_total.reshape(n_seq, per_chunk, 1), (n_seq, per_chunk, state_width))
-    total_block = jnp.pad(total_rows, ((0, 0), (0, 8 - per_chunk), (0, 0)))
-    packed = jnp.concatenate([state_rows, total_block], axis=1)
+    total_hi = slab_total.astype(jnp.bfloat16)
+    rest = slab_total - total_hi.astype(jnp.float32)
+    total_mid = rest.astype(jnp.bfloat16)
+    total_lo = (rest - total_mid.astype(jnp.float32)).astype(jnp.bfloat16)
+    total_parts = jnp.stack([total_hi, total_mid, total_lo]).reshape(3, n_seq, per_chunk)
+    total_rows = jnp.broadcast_to(
+        total_parts.transpose(1, 0, 2).reshape(n_seq, 3 * per_chunk, 1),
+        (n_seq, 3 * per_chunk, state_width),
+    )
+    total_block = jnp.pad(total_rows, ((0, 0), (0, 16 - 3 * per_chunk), (0, 0)))
+    packed = jnp.concatenate([state_rows.astype(jnp.bfloat16), total_block], axis=1)
     received = lax.all_to_all(packed, "seq", 0, 0, tiled=True)
-    slab_states = received[:, :chunk_rows].reshape(n_seq, per_chunk, head_width, state_width)
-    slab_totals = received[:, chunk_rows : chunk_rows + per_chunk, 0]
+    slab_states = (
+        received[:, :chunk_rows].astype(jnp.float32).reshape(n_seq, per_chunk, head_width, state_width)
+    )
+    total_got = received[:, chunk_rows : chunk_rows + 3 * per_chunk, 0].astype(jnp.float32)
+    slab_totals = (
+        total_got[:, :per_chunk] + total_got[:, per_chunk : 2 * per_chunk]
+    ) + total_got[:, 2 * per_chunk :]
     order = jnp.arange(n_seq)
     between = (order[None, None, :] > order[None, :, None]) & (order[None, None, :] < order[:, None, None])
     span = jnp.sum(jnp.where(between[:, :, :, None], slab_totals[None, None, :, :], 0.0), axis=2)

time: 420 us -> 410 us (0.976)
  waiting for transfers between devices: 189 us -> 178 us
    all_to_all x1, waiting for transfers between devices: 41.1 us -> 24.2 us  [shards(): received = lax.all_to_all(packed, 'seq', 0, 0, tiled=True)]
    all_to_all x1, waiting for transfers between devices: 40.4 us -> 45.7 us  [shards(): lax.all_to_all(entering_each, 'seq', 0, 0, tiled=True)]
  transfers between devices with their start and end apart: 6 -> 6, of which waited for: 5 -> 5; matrix products, arithmetic and copies ran while one was open for 16% -> 17% of each run, Pallas kernels for 0% -> 0%
where the time goes in v6:
time: 410 us; the launch traced here: 403 us
  waiting for transfers between devices  178 us (43%)
  blocking collectives  79.7 us (19%)
  matrix products  68.3 us (17%)
  local copies, waits for them, and re-layouts  23.1 us (6%)
  other arithmetic  22.4 us (5%)
  starting transfers between devices  16.8 us (4%)
  between operations  14.3 us (3%)
    all_to_all x1, waiting for transfers between devices, shards(): lax.all_to_all(finished, 'seq', split_axis=0, concat_axis=0, tiled=True)  85.2 us
    all_to_all x1, blocking collectives, shards(): lax.all_to_all(departing_state, 'seq', split_axis=0, concat_axis=0, tiled...  79.7 us
    all_to_all x1, waiting for transfers between devices, shards(): lax.all_to_all(entering_each, 'seq', 0, 0, tiled=True)  45.7 us
    all_to_all x1, waiting for transfers between devices, shards(): received = lax.all_to_all(packed, 'seq', 0, 0, tiled=True)  24.2 us
    all_gather x1, waiting for transfers between devices, shards(): lax.all_gather(lax.dynamic_slice_in_dim(w_out, core * depth, depth, axis=...  20.3 us
    dot_general x1, matrix products, shards(): jnp.dot(partner_rows, w_rows, preferred_element_type=jnp.float32)  12.5 us
    dot_general x2, matrix products, shards(): fetched = jnp.dot(picking, returned, preferred_element_type=jnp.float32)  11.4 us
    dot_general x1, matrix products, shards(): own_part = jnp.dot(own_rows, w_rows, preferred_element_type=jnp.float32)  8.58 us
  transfers between devices with their start and end apart: 6, of which 5 were waited for; matrix products, arithmetic and copies ran while one was open for 17% of the time, Pallas kernels for 0%

profile of v6, /device:TPU:0, one launch (start us, length us, event | category | flops | bytes accessed | tf_op | source)
XLA Modules:
  0.0 402.9 jit_solution(7336698753584395318)
XLA Ops:
  6.5 2.5 constant_dynamic-slice_fusion.1
  9.1 0.7 exp.47
  9.8 1.0 multiply_bitcast_fusion
  10.7 0.6 reduce-window.16
  11.3 0.2 slice_reduce_fusion
  11.6 0.1 bitcast_bitcast_fusion
  11.7 0.2 fusion.61
  12.0 0.1 copy.100
  12.2 0.1 copy.101
  12.5 0.1 copy.103
  12.6 4.1 %copy.99 = bf16[256,4096]{0,1:T(8,128)(2,1)} copy(bf16[256,4096]{1,0:T(8,128)(2,1)} %param.17) | data formatting | bytes 4194304 | tf_op args[0]
  16.7 0.2 slice_reduce_fusion.2
  16.9 0.7 fusion.62
  17.6 4.1 %add_convert_fusion.2 = bf16[64,128,64]{1,2,0:T(8,128)(2,1)S(1)} fusion(bf16[256,64,64]{0,2,1:T(8,128)(2,1)} %bitcast.118, f32[256,128]{1,0:T(8,128)S(1)} %convert_element_type.106, f32[256,64]{0,1:T(8,128)S(1)} %get-tuple-element.39, f32[64]{0:T(128)S(1)} %exponential_multiply_fusion.1), kind=kOutput, calls=%fused_computation.48 | convolution fusion | flops 273678336 | bytes 3342592 | tf_op jit(solution)/shard_map/while/body/eval_jaxpr/shn,shp->hpn/dot_general | solution.py:27
  21.8 0.1 broadcast_in_dim.120
  21.9 1.1 fusion.34
  23.0 7.2 %all-to-all-start = ((bf16[16,272,128]{2,1,0:T(8,128)(2,1)}), bf16[16,272,128]{2,1,0:T(8,128)(2,1)}, u32[]{:S(2)}, u32[]{:S(2)}) async-start(bf16[16,272,128]{2,1,0:T(8,128)(2,1)} %fusion.34), calls=%async_computation | async-start | bytes 2228224 | tf_op jit(solution)/shard_map/all_to_all | solution.py:86
  30.3 24.2 %all-to-all-done = bf16[16,272,128]{2,1,0:T(8,128)(2,1)} async-done(((bf16[16,272,128]{2,1,0:T(8,128)(2,1)}), bf16[16,272,128]{2,1,0:T(8,128)(2,1)}, u32[]{:S(2)}, u32[]{:S(2)}) %all-to-all-start) | async-done | bytes 1114144 | tf_op jit(solution)/shard_map/all_to_all | solution.py:86
  54.5 0.8 slice.67
  55.3 0.2 copy.114
  55.7 0.2 select_reduce_fusion
  56.0 0.2 copy.106
  56.1 1.5 bitcast_convert_fusion.1
  57.6 5.5 %multiply_reduce_fusion = f32[16,4,64,128]{3,2,1,0:T(8,128)} fusion(f32[16,4,64,128]{3,2,1,0:T(8,128)S(1)} %bitcast_convert_fusion.1, f32[16,16,4]{2,1,0:T(8,128)S(1)} %copy.106), kind=kLoop, calls=%fused_computation.1 | loop fusion | flops 16252928 | bytes 4198400 | tf_op jit(solution)/shard_map/reduce_sum | solution.py:99
  63.1 4.6 %all-to-all-start.1 = ((f32[16,256,128]{2,1,0:T(8,128)}), f32[16,256,128]{2,1,0:T(8,128)}, u32[]{:S(2)}, u32[]{:S(2)}) async-start(f32[16,256,128]{2,1,0:T(8,128)} %bitcast.113), calls=%async_computation.1 | async-start | bytes 4194304 | tf_op jit(solution)/shard_map/all_to_all | solution.py:102
  67.7 0.6 iota_compare_fusion.8
  68.4 0.2 fusion.67
  68.5 3.7 fusion.37
  72.3 45.7 %all-to-all-done.1 = f32[16,256,128]{2,1,0:T(8,128)} async-done(((f32[16,256,128]{2,1,0:T(8,128)}), f32[16,256,128]{2,1,0:T(8,128)}, u32[]{:S(2)}, u32[]{:S(2)}) %all-to-all-start.1) | async-done | bytes 2097184 | tf_op jit(solution)/shard_map/all_to_all | solution.py:102
  118.0 3.6 fusion.48
  121.7 0.2 copy-done.7
  121.9 7.5 %fusion.18 = f32[256,64,64]{0,2,1:T(8,128)} fusion(f32[64,64,256]{2,1,0:T(8,128)S(1)} %fusion.48, f32[64,64,256]{2,1,0:T(8,128)S(1)} %copy-done.5, bf16[256,64,64]{0,2,1:T(8,128)(2,1)S(1)} %bitcast.119, f32[256,64]{0,1:T(8,128)S(1)} %copy-done.11, f32[256,64]{0,1:T(8,128)} %copy-done.12, f32[256,256]{1,0:T(8,128)S(1)} %fusion.67, ...), kind=kOutput, calls=%fused_computation.32 | convolution fusion | flops 565182464 | bytes 15204608 | tf_op jit(solution)/shard_map/while/body/eval_jaxpr/tsh,shp->thp/dot_general | solution.py:18
  129.3 5.6 %copy.107 = f32[256,4096]{1,0:T(8,128)} copy(f32[256,4096]{0,1:T(8,128)} %bitcast.117) | data formatting | bytes 8388608 | tf_op jit(solution)/shard_map/reshape | solution.py:114
  135.0 4.5 %multiply_reduce_fusion.1 = f32[256]{0:T(256)S(1)} fusion(f32[256,4096]{1,0:T(8,128)} %copy.107, bf16[256,4096]{1,0:T(8,128)(2,1)} %param.18), kind=kLoop, calls=%fused_computation.38 | loop fusion | flops 8388352 | bytes 6292480 | tf_op jit(solution)/shard_map/reduce_sum | solution.py:117
  139.5 0.2 copy-done.3
  139.7 1.7 multiply_convert_fusion.4
  141.4 1.3 copy-done.4
  142.8 0.3 collective-permute-start
  143.1 2.8 collective-permute-done
  145.9 20.3 %all-gather.2.cloned.1.call-done = bf16[2048,4096]{1,0:T(8,128)(2,1)} async-done(((bf16[2048,256]{1,0:T(8,128)(2,1)}), bf16[2048,4096]{1,0:T(8,128)(2,1)}) %all-gather.2.cloned.1.call-update) | async-done | bytes 16777232 | tf_op jit(solution)/shard_map/wgather/all_gather | solution.py:124
  166.1 12.5 %fusion.68 = f32[256,4096]{1,0:T(8,128)} fusion(bf16[256,2048]{1,0:T(8,128)(2,1)} %collective-permute-done, bf16[2048,4096]{1,0:T(8,128)(2,1)} %all-gather.2.cloned.1.call-done), kind=kOutput, calls=%fused_computation.124 | convolution fusion | flops 4294967296 | bytes 22020096 | tf_op jit(solution)/shard_map/dot_general | solution.py:133
  178.7 0.1 copy.110
  178.8 0.1 eq.87
  179.0 0.1 eq.83
  179.1 1.2 reduce-window.24
  180.3 0.2 slice_reduce_fusion.1
  180.5 0.1 fusion.52
  180.6 0.1 sub.59
  180.9 8.6 %fusion.35 = f32[256,4096]{1,0:T(8,128)S(1)} fusion(bf16[2048,4096]{1,0:T(8,128)(2,1)} %all-gather.2.cloned.1.call-done, bf16[256,4096]{1,0:T(8,128)(2,1)} %copy-done.4, s32[]{:T(128)S(6)} %select_n.48), kind=kOutput, calls=%fused_computation.52 | convolution fusion | flops 4294967296 | bytes 22020100 | tf_op jit(solution)/shard_map/dot_general | solution.py:132
  189.5 3.1 fusion.13
  192.7 2.0 convolution_convert_fusion
  194.7 79.7 %all_to_all.20 = bf16[16,48,4096]{2,1,0:T(8,128)(2,1)S(1)} all-to-all(bf16[16,48,4096]{2,1,0:T(8,128)(2,1)S(1)} %bitcast.112), channel_id=1, replica_groups=mesh['seq'=16,'batch'=8] {'seq'}, dimensions={0} | all-to-all | bytes 12582912 | tf_op jit(solution)/shard_map/all_to_all | solution.py:168
  274.4 3.4 fusion.25
  277.8 3.5 fusion.31
  281.3 5.4 %convolution_convert_fusion.1 = bf16[768,4096]{1,0:T(8,128)(2,1)} fusion(bf16[768,384]{1,0:T(8,128)(2,1)S(1)} %fusion.31, bf16[1,384,4096]{2,1,0:T(8,128)(2,1)S(1)} %copy-done), kind=kOutput, calls=%fused_computation.12 | convolution fusion | flops 2419064832 | bytes 10027008 | tf_op jit(solution)/shard_map/dot_general | solution.py:173
  286.8 4.8 %all-to-all-start.3 = ((bf16[16,48,4096]{2,1,0:T(8,128)(2,1)}), bf16[16,48,4096]{2,1,0:T(8,128)(2,1)}, u32[]{:S(2)}, u32[]{:S(2)}) async-start(bf16[16,48,4096]{2,1,0:T(8,128)(2,1)} %bitcast.114), calls=%async_computation.3 | async-start | bytes 12582912 | tf_op jit(solution)/shard_map/all_to_all | solution.py:177
  291.5 0.1 copy.108
  291.7 0.1 reshape.203
  291.8 2.3 fusion.42
  294.2 4.6 %gather_fusion = f32[512]{0:T(512)S(1)} fusion(f32[256,16]{0,1:T(8,128)S(1)} %fusion.42, s32[512]{0:T(512)S(1)} %reshape.203), kind=kCustom, calls=%fused_computation | custom fusion | bytes 8192 | tf_op jit(solution)/shard_map/jit(take_along_axis)/gather | solution.py:144
  298.7 0.1 reshape.206
  299.0 85.2 %all-to-all-done.3 = bf16[16,48,4096]{2,1,0:T(8,128)(2,1)} async-done(((bf16[16,48,4096]{2,1,0:T(8,128)(2,1)}), bf16[16,48,4096]{2,1,0:T(8,128)(2,1)}, u32[]{:S(2)}, u32[]{:S(2)}) %all-to-all-start.3) | async-done | bytes 6291488 | tf_op jit(solution)/shard_map/all_to_all | solution.py:177
  384.2 5.3 %convert_add_fusion = f32[256,4096]{1,0:T(8,128)S(1)} fusion(bf16[256,4096]{1,0:T(8,128)(2,1)} %copy-done.2, bf16[768,4096]{1,0:T(8,128)(2,1)} %bitcast.27, f32[256]{0:T(256)S(1)} %bitcast.126, s32[256]{0:T(256)S(1)} %bitcast.123), kind=kOutput, calls=%fused_computation.13 | convolution fusion | flops 1613955072 | bytes 12584960 | tf_op jit(solution)/shard_map/dot_general | solution.py:183
  389.5 6.1 %fusion.8 = bf16[256,4096]{1,0:T(8,128)(2,1)} fusion(f32[256,4096]{1,0:T(8,128)S(1)} %convert_add_fusion, bf16[768,4096]{1,0:T(8,128)(2,1)} %bitcast.27, f32[256]{0:T(256)S(1)} %bitcast.127, s32[256]{0:T(256)S(1)} %bitcast.125), kind=kOutput, calls=%fused_computation.21 | convolution fusion | flops 1613955072 | bytes 12584960 | tf_op jit(solution)/shard_map/dot_general | solution.py:183
  (74 shorter events, 1.1 us)
Async XLA Ops:
  6.5 274.8 %copy-start = (bf16[1,384,4096]{2,1,0:T(8,128)(2,1)S(1)}, bf16[1,384,4096]{2,1,0:T(8,128)(2,1)}, u32[]{:S(2)}) copy-start(bf16[1,384,4096]{2,1,0:T(8,128)(2,1)} %param.33) | copy-start | bytes 9437188
  6.5 10.1 %copy-start.9 = (bf16[256,128]{1,0:T(8,128)(2,1)S(1)}, bf16[256,128]{1,0:T(8,128)(2,1)}, u32[]{:S(2)}) copy-start(bf16[256,128]{1,0:T(8,128)(2,1)} %param.19) | copy-start | bytes 196612
  6.5 159.6 %all-gather.2.cloned.1.call-start = ((), (), s32[]{:S(2)}) async-start(), calls=%async_computation.4 | async-start | bytes 17825792 | tf_op jit(solution)/shard_map/wgather/all_gather | solution.py:124
  10.7 11.0 %copy-start.10 = (f32[256,64]{0,1:T(8,128)}, f32[256,64]{0,1:T(8,128)S(1)}, u32[]{:S(2)}) copy-start(f32[256,64]{0,1:T(8,128)S(1)} %get-tuple-element.37) | copy-start | bytes 196612
  11.7 10.1 %copy-start.12 = (f32[256,64]{0,1:T(8,128)}, f32[256,64]{0,1:T(8,128)S(1)}, u32[]{:S(2)}) copy-start(f32[256,64]{0,1:T(8,128)S(1)} %bitcast_bitcast_fusion) | copy-start | bytes 196612
  23.0 31.5 %all-to-all-start = ((bf16[16,272,128]{2,1,0:T(8,128)(2,1)}), bf16[16,272,128]{2,1,0:T(8,128)(2,1)}, u32[]{:S(2)}, u32[]{:S(2)}) async-start(bf16[16,272,128]{2,1,0:T(8,128)(2,1)} %fusion.34), calls=%async_computation | async-start | bytes 2228224 | tf_op jit(solution)/shard_map/all_to_all | solution.py:86
  57.6 10.8 %copy-start.8 = (bf16[256,128]{1,0:T(8,128)(2,1)S(1)}, bf16[256,128]{1,0:T(8,128)(2,1)}, u32[]{:S(2)}) copy-start(bf16[256,128]{1,0:T(8,128)(2,1)} %param.20) | copy-start | bytes 196612
  63.1 54.9 %all-to-all-start.1 = ((f32[16,256,128]{2,1,0:T(8,128)}), f32[16,256,128]{2,1,0:T(8,128)}, u32[]{:S(2)}, u32[]{:S(2)}) async-start(f32[16,256,128]{2,1,0:T(8,128)} %bitcast.113), calls=%async_computation.1 | async-start | bytes 4194304 | tf_op jit(solution)/shard_map/all_to_all | solution.py:102
  72.3 49.4 %copy-start.11 = (f32[256,64]{0,1:T(8,128)S(1)}, f32[256,64]{0,1:T(8,128)}, u32[]{:S(2)}) copy-start(f32[256,64]{0,1:T(8,128)} %copy-done.10) | copy-start | bytes 196612
  72.3 49.4 %copy-start.19 = (f32[64]{0:T(128)S(1)}, f32[64]{0:T(128)}, u32[]{:S(2)}) copy-start(f32[64]{0:T(128)} %param.24) | copy-start | bytes 772
  118.0 3.7 copy-start.5
  118.0 3.8 copy-start.7
  129.3 10.2 %copy-start.14 = (f32[4096]{0:T(1024)S(1)}, f32[4096]{0:T(1024)}, u32[]{:S(2)}) copy-start(f32[4096]{0:T(1024)} %param.25) | copy-start | bytes 49156
  135.0 4.5 %copy-start.1 = (f32[256,4096]{1,0:T(8,128)S(1)}, f32[256,4096]{1,0:T(8,128)}, u32[]{:S(2)}) copy-start(f32[256,4096]{1,0:T(8,128)} %copy.107) | copy-start | bytes 12582916
  135.0 4.7 %copy-start.3 = (bf16[256,4096]{1,0:T(8,128)(2,1)S(1)}, bf16[256,4096]{1,0:T(8,128)(2,1)}, u32[]{:S(2)}) copy-start(bf16[256,4096]{1,0:T(8,128)(2,1)} %param.18) | copy-start | bytes 6291460
  141.4 1.3 copy-start.4
  142.8 35.9 %copy-start.13 = (s32[256,2]{0,1:T(2,128)S(1)}, s32[256,2]{0,1:T(2,128)}, u32[]{:S(2)}) copy-start(s32[256,2]{0,1:T(2,128)} %param.30) | copy-start | bytes 6148
  142.8 3.1 collective-permute-start
  178.7 10.8 %collective-permute-start.1 = (f32[256,4096]{1,0:T(8,128)}, f32[256,4096]{1,0:T(8,128)}, u32[]{:S(2)}, u32[]{:S(2)}) collective-permute-start(f32[256,4096]{1,0:T(8,128)} %fusion.68), channel_id=1, source_target_pairs={{0,1},{1,0},{2,3},{3,2},{4,5},{5,4},{6,7},{7,6},{8,9},{9,8},{10,11... | collective-permute-start | bytes 12582920 | tf_op jit(solution)/shard_map/ppermute | solution.py:134
  180.9 8.6 %copy-start.6 = (bf16[256,4096]{1,0:T(8,128)(2,1)S(1)}, bf16[256,4096]{1,0:T(8,128)(2,1)}, u32[]{:S(2)}) copy-start(bf16[256,4096]{1,0:T(8,128)(2,1)} %param.27) | copy-start | bytes 6291460
  189.5 3.2 copy-start.15
  192.7 2.0 copy-start.2
  194.7 79.8 %copy-start.16 = (bf16[1,4096,384]{2,1,0:T(8,128)(2,1)S(1)}, bf16[1,4096,384]{2,1,0:T(8,128)(2,1)}, u32[]{:S(2)}) copy-start(bf16[1,4096,384]{2,1,0:T(8,128)(2,1)} %param.31) | copy-start | bytes 9437188
  274.4 3.4 copy-start.17
  286.8 5.1 %copy-start.18 = (bf16[4096,16]{0,1:T(8,128)(2,1)S(1)}, bf16[4096,16]{0,1:T(8,128)(2,1)}, u32[]{:S(2)}) copy-start(bf16[4096,16]{0,1:T(8,128)(2,1)} %param.29) | copy-start | bytes 393220
  286.8 97.4 %all-to-all-start.3 = ((bf16[16,48,4096]{2,1,0:T(8,128)(2,1)}), bf16[16,48,4096]{2,1,0:T(8,128)(2,1)}, u32[]{:S(2)}, u32[]{:S(2)}) async-start(bf16[16,48,4096]{2,1,0:T(8,128)(2,1)} %bitcast.114), calls=%async_computation.3 | async-start | bytes 12582912 | tf_op jit(solution)/shard_map/all_to_all | solution.py:177
Sparse Core Ops, SparseCore 0:
  9.4 156.6 all-gather.1

commit v7 on v5

--- a/solution.py
+++ b/solution.py
@@ -164,11 +164,13 @@
     returned = lax.all_to_all(finished, "seq", split_axis=0, concat_axis=0, tiled=True).reshape(
         experts_all * capacity, width
     )
+    picking = (target_pairs.T.reshape(-1)[:, None] == slot_ids[None, :]).astype(jnp.bfloat16)
+    fetched = jnp.dot(picking, returned, preferred_element_type=jnp.float32).reshape(
+        fanout, tokens_here, width
+    )
     total = hidden_wide
     for k in range(fanout):
-        picking = (target_pairs[:, k][:, None] == slot_ids[None, :]).astype(jnp.bfloat16)
-        fetched = jnp.dot(picking, returned, preferred_element_type=jnp.float32)
-        total = total + combine[:, k][:, None] * fetched
+        total = total + combine[:, k][:, None] * fetched[k]
     return total.astype(jnp.bfloat16)
 
 

time: 420 us -> 411 us (0.979); the launches traced: 414 us -> 410 us
  matrix products: 68.8 us -> 63.1 us
    dot_general x2 -> x1, matrix products: 11.4 us -> 5.75 us  [shards(): jnp.dot(picking, returned, preferred_element_type=jnp.float32)]
  transfers between devices with their start and end apart: 6 -> 6, of which waited for: 5 -> 5; matrix products, arithmetic and copies ran while one was open for 16% -> 17% of each run, Pallas kernels for 0% -> 0%
where the time goes in v7:
time: 411 us; the launch traced here: 410 us
  waiting for transfers between devices  189 us (46%)
  blocking collectives  79.5 us (19%)
  matrix products  63.1 us (15%)
  local copies, waits for them, and re-layouts  24 us (6%)
  other arithmetic  23.7 us (6%)
  starting transfers between devices  16.9 us (4%)
  between operations  13.9 us (3%)
    all_to_all x1, waiting for transfers between devices, shards(): lax.all_to_all(finished, 'seq', split_axis=0, concat_axis=0, tiled=True)  85.2 us
    all_to_all x1, blocking collectives, shards(): lax.all_to_all(departing_state, 'seq', split_axis=0, concat_axis=0, tiled...  79.5 us
    all_to_all x1, waiting for transfers between devices, shards(): received = lax.all_to_all(packed, 'seq', 0, 0, tiled=True)  41.1 us
    all_to_all x1, waiting for transfers between devices, shards(): lax.all_to_all(entering_each, 'seq', 0, 0, tiled=True)  40.3 us
    all_gather x1, waiting for transfers between devices, shards(): lax.all_gather(lax.dynamic_slice_in_dim(w_out, core * depth, depth, axis=...  19.5 us
    dot_general x1, matrix products, shards(): jnp.dot(partner_rows, w_rows, preferred_element_type=jnp.float32)  12.5 us
    dot_general x1, matrix products, shards(): own_part = jnp.dot(own_rows, w_rows, preferred_element_type=jnp.float32)  8.58 us
  transfers between devices with their start and end apart: 6, of which 5 were waited for; matrix products, arithmetic and copies ran while one was open for 17% of the time, Pallas kernels for 0%

profile of v7, /device:TPU:0, one launch (start us, length us, event | category | flops | bytes accessed | tf_op | source)
XLA Modules:
  0.0 409.9 jit_solution(7743349969969193069)
XLA Ops:
  6.5 2.5 constant_dynamic-slice_fusion.1
  9.1 0.7 exp.47
  9.8 1.0 multiply_bitcast_fusion
  10.7 0.6 reduce-window.16
  11.3 0.2 slice_reduce_fusion
  11.6 4.1 copy.98
  15.7 0.1 bitcast_bitcast_fusion
  15.7 0.2 slice_reduce_fusion.2
  15.9 0.1 broadcast_in_dim.119
  16.0 0.7 fusion.57
  16.8 4.6 %fusion.27 = f32[64,128,64]{1,2,0:T(8,128)S(1)} fusion(bf16[256,64,64]{0,2,1:T(8,128)(2,1)} %bitcast.113, f32[256,128]{1,0:T(8,128)S(1)} %convert_element_type.65, f32[256,64]{0,1:T(8,128)S(1)} %get-tuple-element.36, f32[64]{0:T(128)S(1)} %exponential_multiply_fusion.1), kind=kOutput, calls=%fused_computation.48 | convolution fusion | flops 273154048 | bytes 4391168 | tf_op jit(solution)/shard_map/while/body/eval_jaxpr/shn,shp->hpn/dot_general | solution.py:27
  21.4 0.1 broadcast_in_dim.120
  21.5 1.5 select_maximum_fusion
  22.9 7.2 %all-to-all-start = ((f32[16,264,128]{2,1,0:T(8,128)}), f32[16,264,128]{2,1,0:T(8,128)}, u32[]{:S(2)}, u32[]{:S(2)}) async-start(f32[16,264,128]{2,1,0:T(8,128)} %select_maximum_fusion), calls=%async_computation | async-start | bytes 4325376 | tf_op jit(solution)/shard_map/all_to_all | solution.py:78
  30.2 41.1 %all-to-all-done = f32[16,264,128]{2,1,0:T(8,128)} async-done(((f32[16,264,128]{2,1,0:T(8,128)}), f32[16,264,128]{2,1,0:T(8,128)}, u32[]{:S(2)}, u32[]{:S(2)}) %all-to-all-start) | async-done | bytes 2162720 | tf_op jit(solution)/shard_map/all_to_all | solution.py:78
  71.3 0.8 slice.63
  72.1 0.1 copy.99
  72.3 0.2 select_reduce_fusion
  72.5 0.2 copy.100
  72.7 1.7 slice.64
  74.5 5.5 %multiply_reduce_fusion = f32[16,4,64,128]{3,2,1,0:T(8,128)} fusion(f32[16,4,64,128]{3,2,1,0:T(8,128)S(1)} %bitcast.108, f32[16,16,4]{2,1,0:T(8,128)S(1)} %copy.100), kind=kLoop, calls=%fused_computation.1 | loop fusion | flops 16252928 | bytes 4198400 | tf_op jit(solution)/shard_map/reduce_sum | solution.py:86
  79.9 4.6 %all-to-all-start.1 = ((f32[16,256,128]{2,1,0:T(8,128)}), f32[16,256,128]{2,1,0:T(8,128)}, u32[]{:S(2)}, u32[]{:S(2)}) async-start(f32[16,256,128]{2,1,0:T(8,128)} %bitcast.107), calls=%async_computation.1 | async-start | bytes 4194304 | tf_op jit(solution)/shard_map/all_to_all | solution.py:89
  84.6 0.6 iota_compare_fusion.6
  85.2 0.2 fusion.62
  85.4 3.7 fusion.37
  89.2 40.3 %all-to-all-done.1 = f32[16,256,128]{2,1,0:T(8,128)} async-done(((f32[16,256,128]{2,1,0:T(8,128)}), f32[16,256,128]{2,1,0:T(8,128)}, u32[]{:S(2)}, u32[]{:S(2)}) %all-to-all-start.1) | async-done | bytes 2097184 | tf_op jit(solution)/shard_map/all_to_all | solution.py:89
  129.5 3.6 fusion.47
  133.2 0.2 copy-done.8
  133.3 7.5 %fusion.18 = f32[256,64,64]{0,2,1:T(8,128)} fusion(f32[64,64,256]{2,1,0:T(8,128)S(1)} %fusion.47, f32[64,64,256]{2,1,0:T(8,128)S(1)} %copy-done.6, bf16[256,64,64]{0,2,1:T(8,128)(2,1)S(1)} %bitcast.114, f32[256,64]{0,1:T(8,128)S(1)} %copy-done.12, f32[256,64]{0,1:T(8,128)} %copy-done.13, f32[256,256]{1,0:T(8,128)S(1)} %fusion.62, ...), kind=kOutput, calls=%fused_computation.32 | convolution fusion | flops 565182464 | bytes 15204608 | tf_op jit(solution)/shard_map/while/body/eval_jaxpr/tsh,shp->thp/dot_general | solution.py:18
  140.8 5.6 %copy.101 = f32[256,4096]{1,0:T(8,128)} copy(f32[256,4096]{0,1:T(8,128)} %bitcast.112) | data formatting | bytes 8388608 | tf_op jit(solution)/shard_map/reshape | solution.py:101
  146.5 4.5 %multiply_reduce_fusion.1 = f32[256]{0:T(256)S(1)} fusion(f32[256,4096]{1,0:T(8,128)} %copy.101, bf16[256,4096]{1,0:T(8,128)(2,1)} %param.18), kind=kLoop, calls=%fused_computation.38 | loop fusion | flops 8388352 | bytes 6292480 | tf_op jit(solution)/shard_map/reduce_sum | solution.py:104
  151.0 0.2 copy-done.4
  151.2 1.7 multiply_convert_fusion.4
  152.9 1.3 copy-done.5
  154.2 0.1 constant_dynamic-slice_fusion
  154.3 0.3 collective-permute-start
  154.6 2.8 collective-permute-done
  157.4 19.5 %all-gather.2.cloned.1.call-done = bf16[2048,4096]{1,0:T(8,128)(2,1)} async-done(((bf16[2048,256]{1,0:T(8,128)(2,1)}), bf16[2048,4096]{1,0:T(8,128)(2,1)}) %all-gather.2.cloned.1.call-update) | async-done | bytes 16777232 | tf_op jit(solution)/shard_map/wgather/all_gather | solution.py:111
  176.9 12.5 %fusion.63 = f32[256,4096]{1,0:T(8,128)} fusion(bf16[256,2048]{1,0:T(8,128)(2,1)} %collective-permute-done, bf16[2048,4096]{1,0:T(8,128)(2,1)} %all-gather.2.cloned.1.call-done), kind=kOutput, calls=%fused_computation.110 | convolution fusion | flops 4294967296 | bytes 22020096 | tf_op jit(solution)/shard_map/dot_general | solution.py:120
  189.4 0.1 copy.104
  189.6 0.1 eq.76
  189.7 0.1 eq.72
  189.9 1.2 reduce-window.24
  191.0 0.2 slice_reduce_fusion.1
  191.3 0.1 fusion.51
  191.4 0.1 sub.48
  191.6 0.1 copy.107
  191.7 8.6 %fusion.35 = f32[256,4096]{1,0:T(8,128)S(1)} fusion(bf16[2048,4096]{1,0:T(8,128)(2,1)} %all-gather.2.cloned.1.call-done, bf16[256,4096]{1,0:T(8,128)(2,1)} %copy-done.5, s32[]{:T(128)S(6)} %select_n.48), kind=kOutput, calls=%fused_computation.53 | convolution fusion | flops 4294967296 | bytes 22020100 | tf_op jit(solution)/shard_map/dot_general | solution.py:119
  200.3 3.1 fusion.11
  203.5 2.0 convolution_convert_fusion
  205.5 79.5 %all_to_all.20 = bf16[16,48,4096]{2,1,0:T(8,128)(2,1)S(1)} all-to-all(bf16[16,48,4096]{2,1,0:T(8,128)(2,1)S(1)} %bitcast.106), channel_id=1, replica_groups=mesh['seq'=16,'batch'=8] {'seq'}, dimensions={0} | all-to-all | bytes 12582912 | tf_op jit(solution)/shard_map/all_to_all | solution.py:155
  285.0 3.4 fusion.25
  288.4 3.5 fusion.32
  291.9 5.4 %convolution_convert_fusion.1 = bf16[768,4096]{1,0:T(8,128)(2,1)} fusion(bf16[768,384]{1,0:T(8,128)(2,1)S(1)} %fusion.32, bf16[1,384,4096]{2,1,0:T(8,128)(2,1)S(1)} %copy-done), kind=kOutput, calls=%fused_computation.12 | convolution fusion | flops 2419064832 | bytes 10027008 | tf_op jit(solution)/shard_map/dot_general | solution.py:160
  297.3 4.8 %all-to-all-start.3 = ((bf16[16,48,4096]{2,1,0:T(8,128)(2,1)}), bf16[16,48,4096]{2,1,0:T(8,128)(2,1)}, u32[]{:S(2)}, u32[]{:S(2)}) async-start(bf16[16,48,4096]{2,1,0:T(8,128)(2,1)} %bitcast.109), calls=%async_computation.3 | async-start | bytes 12582912 | tf_op jit(solution)/shard_map/all_to_all | solution.py:164
  302.0 0.1 copy.102
  302.2 0.1 reshape.202
  302.4 2.3 fusion.43
  304.7 4.6 %gather_fusion = f32[512]{0:T(512)S(1)} fusion(f32[256,16]{0,1:T(8,128)S(1)} %fusion.43, s32[512]{0:T(512)S(1)} %reshape.202), kind=kCustom, calls=%fused_computation | custom fusion | bytes 8192 | tf_op jit(solution)/shard_map/jit(take_along_axis)/gather | solution.py:131
  309.2 0.1 reshape.205
  309.4 0.1 copy.103
  309.5 85.2 %all-to-all-done.3 = bf16[16,48,4096]{2,1,0:T(8,128)(2,1)} async-done(((bf16[16,48,4096]{2,1,0:T(8,128)(2,1)}), bf16[16,48,4096]{2,1,0:T(8,128)(2,1)}, u32[]{:S(2)}, u32[]{:S(2)}) %all-to-all-start.3) | async-done | bytes 6291488 | tf_op jit(solution)/shard_map/all_to_all | solution.py:164
  394.7 5.7 %fusion.28 = f32[512,4096]{1,0:T(8,128)S(1)} fusion(bf16[768,4096]{1,0:T(8,128)(2,1)} %bitcast.26, s32[512]{0:T(512)S(1)} %bitcast.123), kind=kOutput, calls=%fused_computation.50 | convolution fusion | flops 3221618688 | bytes 14682112 | tf_op jit(solution)/shard_map/dot_general | solution.py:168
  400.4 2.6 fusion.15
  (65 shorter events, 0.4 us)
Async XLA Ops:
  6.5 285.3 %copy-start = (bf16[1,384,4096]{2,1,0:T(8,128)(2,1)S(1)}, bf16[1,384,4096]{2,1,0:T(8,128)(2,1)}, u32[]{:S(2)}) copy-start(bf16[1,384,4096]{2,1,0:T(8,128)(2,1)} %param.33) | copy-start | bytes 9437188
  6.5 9.1 %copy-start.10 = (bf16[256,128]{1,0:T(8,128)(2,1)S(1)}, bf16[256,128]{1,0:T(8,128)(2,1)}, u32[]{:S(2)}) copy-start(bf16[256,128]{1,0:T(8,128)(2,1)} %param.19) | copy-start | bytes 196612
  6.5 170.4 %all-gather.2.cloned.1.call-start = ((), (), s32[]{:S(2)}) async-start(), calls=%async_computation.4 | async-start | bytes 17825792 | tf_op jit(solution)/shard_map/wgather/all_gather | solution.py:111
  10.7 10.7 %copy-start.11 = (f32[256,64]{0,1:T(8,128)}, f32[256,64]{0,1:T(8,128)S(1)}, u32[]{:S(2)}) copy-start(f32[256,64]{0,1:T(8,128)S(1)} %get-tuple-element.32) | copy-start | bytes 196612
  15.7 7.2 %copy-start.13 = (f32[256,64]{0,1:T(8,128)}, f32[256,64]{0,1:T(8,128)S(1)}, u32[]{:S(2)}) copy-start(f32[256,64]{0,1:T(8,128)S(1)} %bitcast_bitcast_fusion) | copy-start | bytes 196612
  22.9 48.4 %all-to-all-start = ((f32[16,264,128]{2,1,0:T(8,128)}), f32[16,264,128]{2,1,0:T(8,128)}, u32[]{:S(2)}, u32[]{:S(2)}) async-start(f32[16,264,128]{2,1,0:T(8,128)} %select_maximum_fusion), calls=%async_computation | async-start | bytes 4325376 | tf_op jit(solution)/shard_map/all_to_all | solution.py:78
  74.4 10.8 %copy-start.9 = (bf16[256,128]{1,0:T(8,128)(2,1)S(1)}, bf16[256,128]{1,0:T(8,128)(2,1)}, u32[]{:S(2)}) copy-start(bf16[256,128]{1,0:T(8,128)(2,1)} %param.20) | copy-start | bytes 196612
  79.9 49.6 %all-to-all-start.1 = ((f32[16,256,128]{2,1,0:T(8,128)}), f32[16,256,128]{2,1,0:T(8,128)}, u32[]{:S(2)}, u32[]{:S(2)}) async-start(f32[16,256,128]{2,1,0:T(8,128)} %bitcast.107), calls=%async_computation.1 | async-start | bytes 4194304 | tf_op jit(solution)/shard_map/all_to_all | solution.py:89
  89.1 44.0 %copy-start.12 = (f32[256,64]{0,1:T(8,128)S(1)}, f32[256,64]{0,1:T(8,128)}, u32[]{:S(2)}) copy-start(f32[256,64]{0,1:T(8,128)} %copy-done.11) | copy-start | bytes 196612
  89.2 44.0 %copy-start.20 = (f32[64]{0:T(128)S(1)}, f32[64]{0:T(128)}, u32[]{:S(2)}) copy-start(f32[64]{0:T(128)} %param.24) | copy-start | bytes 772
  129.5 3.7 copy-start.6
  129.5 3.8 copy-start.8
  140.8 10.2 %copy-start.15 = (f32[4096]{0:T(1024)S(1)}, f32[4096]{0:T(1024)}, u32[]{:S(2)}) copy-start(f32[4096]{0:T(1024)} %param.25) | copy-start | bytes 49156
  146.5 4.5 %copy-start.1 = (f32[256,4096]{1,0:T(8,128)S(1)}, f32[256,4096]{1,0:T(8,128)}, u32[]{:S(2)}) copy-start(f32[256,4096]{1,0:T(8,128)} %copy.101) | copy-start | bytes 12582916
  146.5 4.7 %copy-start.4 = (bf16[256,4096]{1,0:T(8,128)(2,1)S(1)}, bf16[256,4096]{1,0:T(8,128)(2,1)}, u32[]{:S(2)}) copy-start(bf16[256,4096]{1,0:T(8,128)(2,1)} %param.18) | copy-start | bytes 6291460
  152.9 1.3 copy-start.5
  154.3 35.2 %copy-start.14 = (s32[256,2]{0,1:T(2,128)S(1)}, s32[256,2]{0,1:T(2,128)}, u32[]{:S(2)}) copy-start(s32[256,2]{0,1:T(2,128)} %param.30) | copy-start | bytes 6148
  154.3 3.1 collective-permute-start
  189.4 10.8 %collective-permute-start.1 = (f32[256,4096]{1,0:T(8,128)}, f32[256,4096]{1,0:T(8,128)}, u32[]{:S(2)}, u32[]{:S(2)}) collective-permute-start(f32[256,4096]{1,0:T(8,128)} %fusion.63), channel_id=1, source_target_pairs={{0,1},{1,0},{2,3},{3,2},{4,5},{5,4},{6,7},{7,6},{8,9},{9,8},{10,11... | collective-permute-start | bytes 12582920 | tf_op jit(solution)/shard_map/ppermute | solution.py:121
  191.7 8.6 %copy-start.7 = (bf16[256,4096]{1,0:T(8,128)(2,1)S(1)}, bf16[256,4096]{1,0:T(8,128)(2,1)}, u32[]{:S(2)}) copy-start(bf16[256,4096]{1,0:T(8,128)(2,1)} %param.27) | copy-start | bytes 6291460
  200.3 3.2 copy-start.16
  203.4 2.0 copy-start.2
  205.4 79.5 %copy-start.17 = (bf16[1,4096,384]{2,1,0:T(8,128)(2,1)S(1)}, bf16[1,4096,384]{2,1,0:T(8,128)(2,1)}, u32[]{:S(2)}) copy-start(bf16[1,4096,384]{2,1,0:T(8,128)(2,1)} %param.31) | copy-start | bytes 9437188
  285.0 3.4 copy-start.18
  297.3 5.1 %copy-start.19 = (bf16[4096,16]{0,1:T(8,128)(2,1)S(1)}, bf16[4096,16]{0,1:T(8,128)(2,1)}, u32[]{:S(2)}) copy-start(bf16[4096,16]{0,1:T(8,128)(2,1)} %param.29) | copy-start | bytes 393220
  297.3 97.4 %all-to-all-start.3 = ((bf16[16,48,4096]{2,1,0:T(8,128)(2,1)}), bf16[16,48,4096]{2,1,0:T(8,128)(2,1)}, u32[]{:S(2)}, u32[]{:S(2)}) async-start(bf16[16,48,4096]{2,1,0:T(8,128)(2,1)} %bitcast.109), calls=%async_computation.3 | async-start | bytes 12582912 | tf_op jit(solution)/shard_map/all_to_all | solution.py:164
  394.7 5.8 %copy-start.3 = (bf16[256,4096]{1,0:T(8,128)(2,1)S(1)}, bf16[256,4096]{1,0:T(8,128)(2,1)}, u32[]{:S(2)}) copy-start(bf16[256,4096]{1,0:T(8,128)(2,1)} %copy-done.2) | copy-start | bytes 6291460
Sparse Core Ops, SparseCore 0:
  9.4 167.4 all-gather.1

commit v8 on v7

--- a/solution.py
+++ b/solution.py
@@ -154,8 +154,14 @@
     departing_state = departing_state.reshape(experts_all, capacity, width)
     batch = lax.all_to_all(departing_state, "seq", split_axis=0, concat_axis=0, tiled=True)
     flat_rows = batch.reshape(-1, width)
-    gate_part = jnp.dot(flat_rows, w_gate[0], preferred_element_type=jnp.float32)
-    up_part = jnp.dot(flat_rows, w_up[0], preferred_element_type=jnp.float32)
+    hidden_units = w_gate.shape[2]
+    both_proj = jnp.dot(
+        flat_rows,
+        jnp.concatenate([w_gate[0], w_up[0]], axis=1),
+        preferred_element_type=jnp.float32,
+    )
+    gate_part = both_proj[:, :hidden_units]
+    up_part = both_proj[:, hidden_units:]
     expert_hidden = (jax.nn.silu(gate_part) * up_part).astype(jnp.bfloat16)
     result = jnp.dot(expert_hidden, w_down[0], preferred_element_type=jnp.float32).astype(
         jnp.bfloat16

time: 411 us -> 409 us (level)
  no operation moved by 1% of the time
where the time goes in v8:
time: 409 us; the launch traced here: 408 us
  waiting for transfers between devices  189 us (46%)
  blocking collectives  79.5 us (19%)
  matrix products  61.2 us (15%)
  local copies, waits for them, and re-layouts  24 us (6%)
  other arithmetic  23.7 us (6%)
  starting transfers between devices  16.9 us (4%)
  between operations  13.9 us (3%)
    all_to_all x1, waiting for transfers between devices, shards(): lax.all_to_all(finished, 'seq', split_axis=0, concat_axis=0, tiled=True)  85.2 us
    all_to_all x1, blocking collectives, shards(): lax.all_to_all(departing_state, 'seq', split_axis=0, concat_axis=0, tiled...  79.5 us
    all_to_all x1, waiting for transfers between devices, shards(): received = lax.all_to_all(packed, 'seq', 0, 0, tiled=True)  41.1 us
    all_to_all x1, waiting for transfers between devices, shards(): lax.all_to_all(entering_each, 'seq', 0, 0, tiled=True)  40.3 us
    all_gather x1, waiting for transfers between devices, shards(): lax.all_gather(lax.dynamic_slice_in_dim(w_out, core * depth, depth, axis=...  19.5 us
    dot_general x1, matrix products, shards(): jnp.dot(partner_rows, w_rows, preferred_element_type=jnp.float32)  12.5 us
    dot_general x1, matrix products, shards(): own_part = jnp.dot(own_rows, w_rows, preferred_element_type=jnp.float32)  8.58 us
  transfers between devices with their start and end apart: 6, of which 5 were waited for; matrix products, arithmetic and copies ran while one was open for 17% of the time, Pallas kernels for 0%

profile of v8, /device:TPU:0, one launch (start us, length us, event | category | flops | bytes accessed | tf_op | source)
XLA Modules:
  0.0 408.1 jit_solution(837041813532308375)
XLA Ops:
  6.5 2.5 constant_dynamic-slice_fusion.1
  9.1 0.0 all-gather.2.cloned.1.call-update
  9.1 0.7 exp.47
  9.8 1.0 multiply_bitcast_fusion
  10.7 0.6 reduce-window.16
  11.3 0.2 slice_reduce_fusion
  11.6 4.1 copy.98
  15.7 0.1 bitcast_bitcast_fusion
  15.7 0.2 slice_reduce_fusion.2
  15.9 0.1 broadcast_in_dim.119
  16.0 0.7 fusion.56
  16.8 4.6 %fusion.27 = f32[64,128,64]{1,2,0:T(8,128)S(1)} fusion(bf16[256,64,64]{0,2,1:T(8,128)(2,1)} %bitcast.102, f32[256,128]{1,0:T(8,128)S(1)} %convert_element_type.65, f32[256,64]{0,1:T(8,128)S(1)} %get-tuple-element.36, f32[64]{0:T(128)S(1)} %exponential_multiply_fusion.1), kind=kOutput, calls=%fused_computation.48 | convolution fusion | flops 273154048 | bytes 4391168 | tf_op jit(solution)/shard_map/while/body/eval_jaxpr/shn,shp->hpn/dot_general | solution.py:27
  21.4 0.1 broadcast_in_dim.120
  21.5 1.5 select_maximum_fusion
  22.9 7.2 %all-to-all-start = ((f32[16,264,128]{2,1,0:T(8,128)}), f32[16,264,128]{2,1,0:T(8,128)}, u32[]{:S(2)}, u32[]{:S(2)}) async-start(f32[16,264,128]{2,1,0:T(8,128)} %select_maximum_fusion), calls=%async_computation | async-start | bytes 4325376 | tf_op jit(solution)/shard_map/all_to_all | solution.py:78
  30.2 41.1 %all-to-all-done = f32[16,264,128]{2,1,0:T(8,128)} async-done(((f32[16,264,128]{2,1,0:T(8,128)}), f32[16,264,128]{2,1,0:T(8,128)}, u32[]{:S(2)}, u32[]{:S(2)}) %all-to-all-start) | async-done | bytes 2162720 | tf_op jit(solution)/shard_map/all_to_all | solution.py:78
  71.3 0.8 slice.71
  72.1 0.1 copy.99
  72.3 0.2 select_reduce_fusion
  72.5 0.2 copy.100
  72.7 1.7 slice.72
  74.5 5.5 %multiply_reduce_fusion = f32[16,4,64,128]{3,2,1,0:T(8,128)} fusion(f32[16,4,64,128]{3,2,1,0:T(8,128)S(1)} %bitcast.98, f32[16,16,4]{2,1,0:T(8,128)S(1)} %copy.100), kind=kLoop, calls=%fused_computation.1 | loop fusion | flops 16252928 | bytes 4198400 | tf_op jit(solution)/shard_map/reduce_sum | solution.py:86
  79.9 4.6 %all-to-all-start.1 = ((f32[16,256,128]{2,1,0:T(8,128)}), f32[16,256,128]{2,1,0:T(8,128)}, u32[]{:S(2)}, u32[]{:S(2)}) async-start(f32[16,256,128]{2,1,0:T(8,128)} %bitcast.97), calls=%async_computation.1 | async-start | bytes 4194304 | tf_op jit(solution)/shard_map/all_to_all | solution.py:89
  84.6 0.6 iota_compare_fusion.6
  85.2 0.2 fusion.61
  85.4 3.7 fusion.32
  89.2 40.3 %all-to-all-done.1 = f32[16,256,128]{2,1,0:T(8,128)} async-done(((f32[16,256,128]{2,1,0:T(8,128)}), f32[16,256,128]{2,1,0:T(8,128)}, u32[]{:S(2)}, u32[]{:S(2)}) %all-to-all-start.1) | async-done | bytes 2097184 | tf_op jit(solution)/shard_map/all_to_all | solution.py:89
  129.5 3.6 fusion.44
  133.2 0.2 copy-done.8
  133.3 7.5 %fusion.22 = f32[256,64,64]{0,2,1:T(8,128)} fusion(f32[64,64,256]{2,1,0:T(8,128)S(1)} %fusion.44, f32[64,64,256]{2,1,0:T(8,128)S(1)} %copy-done.6, bf16[256,64,64]{0,2,1:T(8,128)(2,1)S(1)} %bitcast.103, f32[256,64]{0,1:T(8,128)S(1)} %copy-done.12, f32[256,64]{0,1:T(8,128)} %copy-done.13, f32[256,256]{1,0:T(8,128)S(1)} %fusion.61, ...), kind=kOutput, calls=%fused_computation.36 | convolution fusion | flops 565182464 | bytes 15204608 | tf_op jit(solution)/shard_map/while/body/eval_jaxpr/tsh,shp->thp/dot_general | solution.py:18
  140.8 5.6 %copy.101 = f32[256,4096]{1,0:T(8,128)} copy(f32[256,4096]{0,1:T(8,128)} %bitcast.101) | data formatting | bytes 8388608 | tf_op jit(solution)/shard_map/reshape | solution.py:101
  146.5 4.5 %multiply_reduce_fusion.1 = f32[256]{0:T(256)S(1)} fusion(f32[256,4096]{1,0:T(8,128)} %copy.101, bf16[256,4096]{1,0:T(8,128)(2,1)} %param.18), kind=kLoop, calls=%fused_computation.42 | loop fusion | flops 8388352 | bytes 6292480 | tf_op jit(solution)/shard_map/reduce_sum | solution.py:104
  151.0 0.2 copy-done.4
  151.2 1.7 multiply_convert_fusion.4
  152.9 1.3 copy-done.5
  154.2 0.1 constant_dynamic-slice_fusion
  154.3 0.3 collective-permute-start
  154.6 2.8 collective-permute-done
  157.4 19.5 %all-gather.2.cloned.1.call-done = bf16[2048,4096]{1,0:T(8,128)(2,1)} async-done(((bf16[2048,256]{1,0:T(8,128)(2,1)}), bf16[2048,4096]{1,0:T(8,128)(2,1)}) %all-gather.2.cloned.1.call-update) | async-done | bytes 16777232 | tf_op jit(solution)/shard_map/wgather/all_gather | solution.py:111
  176.9 12.5 %fusion.62 = f32[256,4096]{1,0:T(8,128)} fusion(bf16[256,2048]{1,0:T(8,128)(2,1)} %collective-permute-done, bf16[2048,4096]{1,0:T(8,128)(2,1)} %all-gather.2.cloned.1.call-done), kind=kOutput, calls=%fused_computation.113 | convolution fusion | flops 4294967296 | bytes 22020096 | tf_op jit(solution)/shard_map/dot_general | solution.py:120
  189.4 0.1 copy.104
  189.6 0.1 eq.76
  189.7 0.1 eq.72
  189.9 1.2 reduce-window.24
  191.0 0.2 slice_reduce_fusion.1
  191.3 0.1 fusion.48
  191.4 0.1 sub.48
  191.6 0.1 copy.107
  191.7 8.6 %fusion.30 = f32[256,4096]{1,0:T(8,128)S(1)} fusion(bf16[2048,4096]{1,0:T(8,128)(2,1)} %all-gather.2.cloned.1.call-done, bf16[256,4096]{1,0:T(8,128)(2,1)} %copy-done.5, s32[]{:T(128)S(6)} %select_n.48), kind=kOutput, calls=%fused_computation.53 | convolution fusion | flops 4294967296 | bytes 22020100 | tf_op jit(solution)/shard_map/dot_general | solution.py:119
  200.3 3.1 fusion.15
  203.5 2.0 convolution_convert_fusion
  205.5 79.5 %all_to_all.20 = bf16[16,48,4096]{2,1,0:T(8,128)(2,1)S(1)} all-to-all(bf16[16,48,4096]{2,1,0:T(8,128)(2,1)S(1)} %bitcast.96), channel_id=1, replica_groups=mesh['seq'=16,'batch'=8] {'seq'}, dimensions={0} | all-to-all | bytes 12582912 | tf_op jit(solution)/shard_map/all_to_all | solution.py:155
  285.0 5.0 %fusion.7 = f32[768,768]{1,0:T(8,128)S(1)} fusion(bf16[768,4096]{1,0:T(8,128)(2,1)S(1)} %bitcast.100, bf16[4096,384]{1,0:T(8,128)(2,1)S(1)} %bitcast.113, bf16[4096,384]{1,0:T(8,128)(2,1)S(1)} %bitcast.114), kind=kOutput, calls=%fused_computation.13 | convolution fusion | flops 4844421120 | bytes 14942208 | tf_op jit(solution)/shard_map/dot_general | solution.py:158
  290.0 5.4 %convolution_convert_fusion.1 = bf16[768,4096]{1,0:T(8,128)(2,1)} fusion(bf16[1,384,4096]{2,1,0:T(8,128)(2,1)S(1)} %copy-done, f32[768,768]{1,0:T(8,128)S(1)} %fusion.7), kind=kOutput, calls=%fused_computation.12 | convolution fusion | flops 2420834304 | bytes 11796480 | tf_op jit(solution)/shard_map/dot_general | solution.py:166
  295.4 4.8 %all-to-all-start.3 = ((bf16[16,48,4096]{2,1,0:T(8,128)(2,1)}), bf16[16,48,4096]{2,1,0:T(8,128)(2,1)}, u32[]{:S(2)}, u32[]{:S(2)}) async-start(bf16[16,48,4096]{2,1,0:T(8,128)(2,1)} %bitcast.99), calls=%async_computation.3 | async-start | bytes 12582912 | tf_op jit(solution)/shard_map/all_to_all | solution.py:170
  300.2 0.1 copy.102
  300.3 0.1 reshape.202
  300.5 2.3 fusion.38
  302.8 4.6 %gather_fusion = f32[512]{0:T(512)S(1)} fusion(f32[256,16]{0,1:T(8,128)S(1)} %fusion.38, s32[512]{0:T(512)S(1)} %reshape.202), kind=kCustom, calls=%fused_computation | custom fusion | bytes 8192 | tf_op jit(solution)/shard_map/jit(take_along_axis)/gather | solution.py:131
  307.4 0.1 reshape.205
  307.5 0.1 copy.103
  307.7 85.2 %all-to-all-done.3 = bf16[16,48,4096]{2,1,0:T(8,128)(2,1)} async-done(((bf16[16,48,4096]{2,1,0:T(8,128)(2,1)}), bf16[16,48,4096]{2,1,0:T(8,128)(2,1)}, u32[]{:S(2)}, u32[]{:S(2)}) %all-to-all-start.3) | async-done | bytes 6291488 | tf_op jit(solution)/shard_map/all_to_all | solution.py:170
  392.9 5.7 %fusion.28 = f32[512,4096]{1,0:T(8,128)S(1)} fusion(bf16[768,4096]{1,0:T(8,128)(2,1)} %bitcast.26, s32[512]{0:T(512)S(1)} %bitcast.112), kind=kOutput, calls=%fused_computation.50 | convolution fusion | flops 3221618688 | bytes 14682112 | tf_op jit(solution)/shard_map/dot_general | solution.py:174
  398.6 2.6 fusion.19
  (64 shorter events, 0.4 us)
Async XLA Ops:
  6.5 283.5 %copy-start = (bf16[1,384,4096]{2,1,0:T(8,128)(2,1)S(1)}, bf16[1,384,4096]{2,1,0:T(8,128)(2,1)}, u32[]{:S(2)}) copy-start(bf16[1,384,4096]{2,1,0:T(8,128)(2,1)} %param.33) | copy-start | bytes 9437188
  6.5 9.1 %copy-start.10 = (bf16[256,128]{1,0:T(8,128)(2,1)S(1)}, bf16[256,128]{1,0:T(8,128)(2,1)}, u32[]{:S(2)}) copy-start(bf16[256,128]{1,0:T(8,128)(2,1)} %param.19) | copy-start | bytes 196612
  6.5 170.4 %all-gather.2.cloned.1.call-start = ((), (), s32[]{:S(2)}) async-start(), calls=%async_computation.4 | async-start | bytes 17825792 | tf_op jit(solution)/shard_map/wgather/all_gather | solution.py:111
  10.7 10.7 %copy-start.11 = (f32[256,64]{0,1:T(8,128)}, f32[256,64]{0,1:T(8,128)S(1)}, u32[]{:S(2)}) copy-start(f32[256,64]{0,1:T(8,128)S(1)} %get-tuple-element.32) | copy-start | bytes 196612
  15.7 7.2 %copy-start.13 = (f32[256,64]{0,1:T(8,128)}, f32[256,64]{0,1:T(8,128)S(1)}, u32[]{:S(2)}) copy-start(f32[256,64]{0,1:T(8,128)S(1)} %bitcast_bitcast_fusion) | copy-start | bytes 196612
  22.9 48.4 %all-to-all-start = ((f32[16,264,128]{2,1,0:T(8,128)}), f32[16,264,128]{2,1,0:T(8,128)}, u32[]{:S(2)}, u32[]{:S(2)}) async-start(f32[16,264,128]{2,1,0:T(8,128)} %select_maximum_fusion), calls=%async_computation | async-start | bytes 4325376 | tf_op jit(solution)/shard_map/all_to_all | solution.py:78
  74.4 10.8 %copy-start.9 = (bf16[256,128]{1,0:T(8,128)(2,1)S(1)}, bf16[256,128]{1,0:T(8,128)(2,1)}, u32[]{:S(2)}) copy-start(bf16[256,128]{1,0:T(8,128)(2,1)} %param.20) | copy-start | bytes 196612
  79.9 49.6 %all-to-all-start.1 = ((f32[16,256,128]{2,1,0:T(8,128)}), f32[16,256,128]{2,1,0:T(8,128)}, u32[]{:S(2)}, u32[]{:S(2)}) async-start(f32[16,256,128]{2,1,0:T(8,128)} %bitcast.97), calls=%async_computation.1 | async-start | bytes 4194304 | tf_op jit(solution)/shard_map/all_to_all | solution.py:89
  89.1 44.0 %copy-start.12 = (f32[256,64]{0,1:T(8,128)S(1)}, f32[256,64]{0,1:T(8,128)}, u32[]{:S(2)}) copy-start(f32[256,64]{0,1:T(8,128)} %copy-done.11) | copy-start | bytes 196612
  89.2 44.0 %copy-start.20 = (f32[64]{0:T(128)S(1)}, f32[64]{0:T(128)}, u32[]{:S(2)}) copy-start(f32[64]{0:T(128)} %param.24) | copy-start | bytes 772
  129.5 3.7 copy-start.6
  129.5 3.8 copy-start.8
  140.8 10.2 %copy-start.15 = (f32[4096]{0:T(1024)S(1)}, f32[4096]{0:T(1024)}, u32[]{:S(2)}) copy-start(f32[4096]{0:T(1024)} %param.25) | copy-start | bytes 49156
  146.5 4.5 %copy-start.1 = (f32[256,4096]{1,0:T(8,128)S(1)}, f32[256,4096]{1,0:T(8,128)}, u32[]{:S(2)}) copy-start(f32[256,4096]{1,0:T(8,128)} %copy.101) | copy-start | bytes 12582916
  146.5 4.7 %copy-start.4 = (bf16[256,4096]{1,0:T(8,128)(2,1)S(1)}, bf16[256,4096]{1,0:T(8,128)(2,1)}, u32[]{:S(2)}) copy-start(bf16[256,4096]{1,0:T(8,128)(2,1)} %param.18) | copy-start | bytes 6291460
  152.9 1.3 copy-start.5
  154.3 35.2 %copy-start.14 = (s32[256,2]{0,1:T(2,128)S(1)}, s32[256,2]{0,1:T(2,128)}, u32[]{:S(2)}) copy-start(s32[256,2]{0,1:T(2,128)} %param.30) | copy-start | bytes 6148
  154.3 3.1 collective-permute-start
  189.4 10.8 %collective-permute-start.1 = (f32[256,4096]{1,0:T(8,128)}, f32[256,4096]{1,0:T(8,128)}, u32[]{:S(2)}, u32[]{:S(2)}) collective-permute-start(f32[256,4096]{1,0:T(8,128)} %fusion.62), channel_id=1, source_target_pairs={{0,1},{1,0},{2,3},{3,2},{4,5},{5,4},{6,7},{7,6},{8,9},{9,8},{10,11... | collective-permute-start | bytes 12582920 | tf_op jit(solution)/shard_map/ppermute | solution.py:121
  191.7 8.6 %copy-start.7 = (bf16[256,4096]{1,0:T(8,128)(2,1)S(1)}, bf16[256,4096]{1,0:T(8,128)(2,1)}, u32[]{:S(2)}) copy-start(bf16[256,4096]{1,0:T(8,128)(2,1)} %param.27) | copy-start | bytes 6291460
  200.3 3.2 copy-start.16
  203.4 2.0 copy-start.2
  205.4 79.5 %copy-start.17 = (bf16[1,4096,384]{2,1,0:T(8,128)(2,1)S(1)}, bf16[1,4096,384]{2,1,0:T(8,128)(2,1)}, u32[]{:S(2)}) copy-start(bf16[1,4096,384]{2,1,0:T(8,128)(2,1)} %param.32) | copy-start | bytes 9437188
  205.5 79.5 %copy-start.18 = (bf16[1,4096,384]{2,1,0:T(8,128)(2,1)S(1)}, bf16[1,4096,384]{2,1,0:T(8,128)(2,1)}, u32[]{:S(2)}) copy-start(bf16[1,4096,384]{2,1,0:T(8,128)(2,1)} %param.31) | copy-start | bytes 9437188
  295.4 5.1 %copy-start.19 = (bf16[4096,16]{0,1:T(8,128)(2,1)S(1)}, bf16[4096,16]{0,1:T(8,128)(2,1)}, u32[]{:S(2)}) copy-start(bf16[4096,16]{0,1:T(8,128)(2,1)} %param.29) | copy-start | bytes 393220
  295.4 97.4 %all-to-all-start.3 = ((bf16[16,48,4096]{2,1,0:T(8,128)(2,1)}), bf16[16,48,4096]{2,1,0:T(8,128)(2,1)}, u32[]{:S(2)}, u32[]{:S(2)}) async-start(bf16[16,48,4096]{2,1,0:T(8,128)(2,1)} %bitcast.99), calls=%async_computation.3 | async-start | bytes 12582912 | tf_op jit(solution)/shard_map/all_to_all | solution.py:170
  392.9 5.8 %copy-start.3 = (bf16[256,4096]{1,0:T(8,128)(2,1)S(1)}, bf16[256,4096]{1,0:T(8,128)(2,1)}, u32[]{:S(2)}) copy-start(bf16[256,4096]{1,0:T(8,128)(2,1)} %copy-done.2) | copy-start | bytes 6291460
Sparse Core Ops, SparseCore 0:
  9.4 167.4 all-gather.1

commit v9 on v8

--- a/solution.py
+++ b/solution.py
@@ -109,7 +109,7 @@
     depth = w_out.shape[0] // 2
     with jax.named_scope("wgather"):
         w_rows = lax.all_gather(
-            lax.dynamic_slice_in_dim(w_out, core * depth, depth, axis=0), "seq", axis=1, tiled=True
+            jnp.where(core == 0, w_out[:depth], w_out[depth:]), "seq", axis=1, tiled=True
         )
     partners = [(b, b ^ 1) for b in range(n_batch)]
     own_rows = lax.dynamic_slice_in_dim(normed, core * depth, depth, axis=1)

time: 409 us -> 409 us (level)
  transfers between devices with their start and end apart: 6 -> 6, of which waited for: 5 -> 5; matrix products, arithmetic and copies ran while one was open for 17% -> 16% of each run, Pallas kernels for 0% -> 0%
where the time goes in v9:
time: 409 us; the launch traced here: 408 us
  waiting for transfers between devices  190 us (46%)
  blocking collectives  79.5 us (19%)
  matrix products  61.3 us (15%)
  other arithmetic  25.7 us (6%)
  local copies, waits for them, and re-layouts  20.9 us (5%)
  starting transfers between devices  16.9 us (4%)
  between operations  13.9 us (3%)
    all_to_all x1, waiting for transfers between devices, shards(): lax.all_to_all(finished, 'seq', split_axis=0, concat_axis=0, tiled=True)  85.2 us
    all_to_all x1, blocking collectives, shards(): lax.all_to_all(departing_state, 'seq', split_axis=0, concat_axis=0, tiled...  79.5 us
    all_to_all x1, waiting for transfers between devices, shards(): lax.all_to_all(entering_each, 'seq', 0, 0, tiled=True)  41.3 us
    all_to_all x1, waiting for transfers between devices, shards(): received = lax.all_to_all(packed, 'seq', 0, 0, tiled=True)  41.2 us
    all_gather x1, waiting for transfers between devices, shards(): lax.all_gather(jnp.where(core == 0, w_out[:depth], w_out[depth:]), 'seq',...  19.5 us
    dot_general x1, matrix products, shards(): jnp.dot(partner_rows, w_rows, preferred_element_type=jnp.float32)  12.5 us
    dot_general x1, matrix products, shards(): own_part = jnp.dot(own_rows, w_rows, preferred_element_type=jnp.float32)  8.58 us
  transfers between devices with their start and end apart: 6, of which 5 were waited for; matrix products, arithmetic and copies ran while one was open for 16% of the time, Pallas kernels for 0%

profile of v9, /device:TPU:0, one launch (start us, length us, event | category | flops | bytes accessed | tf_op | source)
XLA Modules:
  0.0 408.1 jit_solution(17707491736658875464)
XLA Ops:
  6.5 0.0 all-gather.2.cloned.1.call-start
  6.6 2.9 slice_select_fusion
  9.5 0.0 all-gather.2.cloned.1.call-update
  9.5 0.1 multiply_bitcast_fusion
  9.7 0.6 reduce-window.16
  10.3 0.2 slice_reduce_fusion
  10.5 4.1 copy.98
  14.6 0.1 bitcast_bitcast_fusion
  14.7 0.2 slice_reduce_fusion.2
  14.9 0.1 broadcast_in_dim.119
  15.0 0.7 fusion.56
  15.7 4.6 %fusion.27 = f32[64,128,64]{1,2,0:T(8,128)S(1)} fusion(bf16[256,64,64]{0,2,1:T(8,128)(2,1)} %bitcast.102, f32[256,128]{1,0:T(8,128)S(1)} %convert_element_type.65, f32[256,64]{0,1:T(8,128)S(1)} %get-tuple-element.36, f32[64]{0:T(128)S(1)} %exponential_multiply_fusion.1), kind=kOutput, calls=%fused_computation.48 | convolution fusion | flops 273154048 | bytes 4391168 | tf_op jit(solution)/shard_map/while/body/eval_jaxpr/shn,shp->hpn/dot_general | solution.py:27
  20.3 0.1 broadcast_in_dim.120
  20.4 1.5 select_maximum_fusion
  21.9 7.2 %all-to-all-start = ((f32[16,264,128]{2,1,0:T(8,128)}), f32[16,264,128]{2,1,0:T(8,128)}, u32[]{:S(2)}, u32[]{:S(2)}) async-start(f32[16,264,128]{2,1,0:T(8,128)} %select_maximum_fusion), calls=%async_computation | async-start | bytes 4325376 | tf_op jit(solution)/shard_map/all_to_all | solution.py:78
  29.1 41.2 %all-to-all-done = f32[16,264,128]{2,1,0:T(8,128)} async-done(((f32[16,264,128]{2,1,0:T(8,128)}), f32[16,264,128]{2,1,0:T(8,128)}, u32[]{:S(2)}, u32[]{:S(2)}) %all-to-all-start) | async-done | bytes 2162720 | tf_op jit(solution)/shard_map/all_to_all | solution.py:78
  70.4 0.8 slice.79
  71.2 0.1 copy.99
  71.3 0.2 select_reduce_fusion
  71.6 0.2 copy.100
  71.7 1.7 slice.80
  73.5 5.5 %multiply_reduce_fusion = f32[16,4,64,128]{3,2,1,0:T(8,128)} fusion(f32[16,4,64,128]{3,2,1,0:T(8,128)S(1)} %bitcast.98, f32[16,16,4]{2,1,0:T(8,128)S(1)} %copy.100), kind=kLoop, calls=%fused_computation.1 | loop fusion | flops 16252928 | bytes 4198400 | tf_op jit(solution)/shard_map/reduce_sum | solution.py:86
  79.0 4.6 %all-to-all-start.1 = ((f32[16,256,128]{2,1,0:T(8,128)}), f32[16,256,128]{2,1,0:T(8,128)}, u32[]{:S(2)}, u32[]{:S(2)}) async-start(f32[16,256,128]{2,1,0:T(8,128)} %bitcast.97), calls=%async_computation.1 | async-start | bytes 4194304 | tf_op jit(solution)/shard_map/all_to_all | solution.py:89
  83.6 0.6 iota_compare_fusion.6
  84.3 0.2 fusion.61
  84.5 3.7 fusion.32
  88.2 41.3 %all-to-all-done.1 = f32[16,256,128]{2,1,0:T(8,128)} async-done(((f32[16,256,128]{2,1,0:T(8,128)}), f32[16,256,128]{2,1,0:T(8,128)}, u32[]{:S(2)}, u32[]{:S(2)}) %all-to-all-start.1) | async-done | bytes 2097184 | tf_op jit(solution)/shard_map/all_to_all | solution.py:89
  129.5 3.6 fusion.44
  133.1 0.2 copy-done.8
  133.3 7.5 %fusion.22 = f32[256,64,64]{0,2,1:T(8,128)} fusion(f32[64,64,256]{2,1,0:T(8,128)S(1)} %fusion.44, f32[64,64,256]{2,1,0:T(8,128)S(1)} %copy-done.6, bf16[256,64,64]{0,2,1:T(8,128)(2,1)S(1)} %bitcast.103, f32[256,64]{0,1:T(8,128)S(1)} %copy-done.12, f32[256,64]{0,1:T(8,128)} %copy-done.13, f32[256,256]{1,0:T(8,128)S(1)} %fusion.61, ...), kind=kOutput, calls=%fused_computation.36 | convolution fusion | flops 565182464 | bytes 15204608 | tf_op jit(solution)/shard_map/while/body/eval_jaxpr/tsh,shp->thp/dot_general | solution.py:18
  140.8 5.7 %copy.101 = f32[256,4096]{1,0:T(8,128)} copy(f32[256,4096]{0,1:T(8,128)} %bitcast.101) | data formatting | bytes 8388608 | tf_op jit(solution)/shard_map/reshape | solution.py:101
  146.5 4.5 %multiply_reduce_fusion.1 = f32[256]{0:T(256)S(1)} fusion(f32[256,4096]{1,0:T(8,128)} %copy.101, bf16[256,4096]{1,0:T(8,128)(2,1)} %param.18), kind=kLoop, calls=%fused_computation.42 | loop fusion | flops 8388352 | bytes 6292480 | tf_op jit(solution)/shard_map/reduce_sum | solution.py:104
  151.0 0.2 copy-done.4
  151.2 1.7 multiply_convert_fusion.4
  152.9 1.3 copy-done.5
  154.2 0.1 constant_dynamic-slice_fusion
  154.3 0.3 collective-permute-start
  154.6 2.8 collective-permute-done
  157.3 19.5 %all-gather.2.cloned.1.call-done = bf16[2048,4096]{1,0:T(8,128)(2,1)} async-done(((bf16[2048,256]{1,0:T(8,128)(2,1)}), bf16[2048,4096]{1,0:T(8,128)(2,1)}) %all-gather.2.cloned.1.call-update) | async-done | bytes 16777232 | tf_op jit(solution)/shard_map/wgather/all_gather | solution.py:111
  176.9 12.5 %fusion.62 = f32[256,4096]{1,0:T(8,128)} fusion(bf16[256,2048]{1,0:T(8,128)(2,1)} %collective-permute-done, bf16[2048,4096]{1,0:T(8,128)(2,1)} %all-gather.2.cloned.1.call-done), kind=kOutput, calls=%fused_computation.113 | convolution fusion | flops 4294967296 | bytes 22020096 | tf_op jit(solution)/shard_map/dot_general | solution.py:120
  189.4 0.1 copy.104
  189.6 0.1 eq.80
  189.7 0.1 eq.76
  189.9 1.2 reduce-window.24
  191.0 0.2 slice_reduce_fusion.1
  191.3 0.1 fusion.48
  191.4 0.1 sub.48
  191.5 0.1 copy.107
  191.6 8.6 %fusion.30 = f32[256,4096]{1,0:T(8,128)S(1)} fusion(bf16[2048,4096]{1,0:T(8,128)(2,1)} %all-gather.2.cloned.1.call-done, bf16[256,4096]{1,0:T(8,128)(2,1)} %copy-done.5, s32[]{:T(128)S(6)} %select_n.55), kind=kOutput, calls=%fused_computation.54 | convolution fusion | flops 4294967296 | bytes 22020100 | tf_op jit(solution)/shard_map/dot_general | solution.py:119
  200.3 3.1 fusion.15
  203.4 2.0 convolution_convert_fusion
  205.4 79.5 %all_to_all.20 = bf16[16,48,4096]{2,1,0:T(8,128)(2,1)S(1)} all-to-all(bf16[16,48,4096]{2,1,0:T(8,128)(2,1)S(1)} %bitcast.96), channel_id=1, replica_groups=mesh['seq'=16,'batch'=8] {'seq'}, dimensions={0} | all-to-all | bytes 12582912 | tf_op jit(solution)/shard_map/all_to_all | solution.py:155
  284.9 5.0 %fusion.7 = f32[768,768]{1,0:T(8,128)S(1)} fusion(bf16[768,4096]{1,0:T(8,128)(2,1)S(1)} %bitcast.100, bf16[4096,384]{1,0:T(8,128)(2,1)S(1)} %bitcast.113, bf16[4096,384]{1,0:T(8,128)(2,1)S(1)} %bitcast.114), kind=kOutput, calls=%fused_computation.13 | convolution fusion | flops 4844421120 | bytes 14942208 | tf_op jit(solution)/shard_map/dot_general | solution.py:158
  290.0 5.4 %convolution_convert_fusion.1 = bf16[768,4096]{1,0:T(8,128)(2,1)} fusion(bf16[1,384,4096]{2,1,0:T(8,128)(2,1)S(1)} %copy-done, f32[768,768]{1,0:T(8,128)S(1)} %fusion.7), kind=kOutput, calls=%fused_computation.12 | convolution fusion | flops 2420834304 | bytes 11796480 | tf_op jit(solution)/shard_map/dot_general | solution.py:166
  295.4 4.8 %all-to-all-start.3 = ((bf16[16,48,4096]{2,1,0:T(8,128)(2,1)}), bf16[16,48,4096]{2,1,0:T(8,128)(2,1)}, u32[]{:S(2)}, u32[]{:S(2)}) async-start(bf16[16,48,4096]{2,1,0:T(8,128)(2,1)} %bitcast.99), calls=%async_computation.3 | async-start | bytes 12582912 | tf_op jit(solution)/shard_map/all_to_all | solution.py:170
  300.2 0.1 copy.102
  300.4 0.1 reshape.202
  300.5 2.3 fusion.38
  302.8 4.6 %gather_fusion = f32[512]{0:T(512)S(1)} fusion(f32[256,16]{0,1:T(8,128)S(1)} %fusion.38, s32[512]{0:T(512)S(1)} %reshape.202), kind=kCustom, calls=%fused_computation | custom fusion | bytes 8192 | tf_op jit(solution)/shard_map/jit(take_along_axis)/gather | solution.py:131
  307.4 0.1 reshape.205
  307.5 0.1 copy.103
  307.7 85.2 %all-to-all-done.3 = bf16[16,48,4096]{2,1,0:T(8,128)(2,1)} async-done(((bf16[16,48,4096]{2,1,0:T(8,128)(2,1)}), bf16[16,48,4096]{2,1,0:T(8,128)(2,1)}, u32[]{:S(2)}, u32[]{:S(2)}) %all-to-all-start.3) | async-done | bytes 6291488 | tf_op jit(solution)/shard_map/all_to_all | solution.py:170
  392.9 5.7 %fusion.28 = f32[512,4096]{1,0:T(8,128)S(1)} fusion(bf16[768,4096]{1,0:T(8,128)(2,1)} %bitcast.26, s32[512]{0:T(512)S(1)} %bitcast.112), kind=kOutput, calls=%fused_computation.50 | convolution fusion | flops 3221618688 | bytes 14682112 | tf_op jit(solution)/shard_map/dot_general | solution.py:174
  398.6 2.6 fusion.19
  (70 shorter events, 0.4 us)
Async XLA Ops:
  6.5 283.5 %copy-start = (bf16[1,384,4096]{2,1,0:T(8,128)(2,1)S(1)}, bf16[1,384,4096]{2,1,0:T(8,128)(2,1)}, u32[]{:S(2)}) copy-start(bf16[1,384,4096]{2,1,0:T(8,128)(2,1)} %param.33) | copy-start | bytes 9437188
  6.5 2.9 copy-start.22
  6.5 3.0 copy-start.14
  6.5 3.0 copy-start.18
  6.5 170.3 %all-gather.2.cloned.1.call-start = ((), (), s32[]{:S(2)}) async-start(), calls=%async_computation.4 | async-start | bytes 17825792 | tf_op jit(solution)/shard_map/wgather/all_gather | solution.py:111
  6.6 8.0 %copy-start.10 = (bf16[256,128]{1,0:T(8,128)(2,1)S(1)}, bf16[256,128]{1,0:T(8,128)(2,1)}, u32[]{:S(2)}) copy-start(bf16[256,128]{1,0:T(8,128)(2,1)} %param.19) | copy-start | bytes 196612
  9.6 10.7 %copy-start.11 = (f32[256,64]{0,1:T(8,128)}, f32[256,64]{0,1:T(8,128)S(1)}, u32[]{:S(2)}) copy-start(f32[256,64]{0,1:T(8,128)S(1)} %get-tuple-element.32) | copy-start | bytes 196612
  14.7 7.2 %copy-start.13 = (f32[256,64]{0,1:T(8,128)}, f32[256,64]{0,1:T(8,128)S(1)}, u32[]{:S(2)}) copy-start(f32[256,64]{0,1:T(8,128)S(1)} %bitcast_bitcast_fusion) | copy-start | bytes 196612
  21.9 48.5 %all-to-all-start = ((f32[16,264,128]{2,1,0:T(8,128)}), f32[16,264,128]{2,1,0:T(8,128)}, u32[]{:S(2)}, u32[]{:S(2)}) async-start(f32[16,264,128]{2,1,0:T(8,128)} %select_maximum_fusion), calls=%async_computation | async-start | bytes 4325376 | tf_op jit(solution)/shard_map/all_to_all | solution.py:78
  73.5 10.8 %copy-start.9 = (bf16[256,128]{1,0:T(8,128)(2,1)S(1)}, bf16[256,128]{1,0:T(8,128)(2,1)}, u32[]{:S(2)}) copy-start(bf16[256,128]{1,0:T(8,128)(2,1)} %param.20) | copy-start | bytes 196612
  79.0 50.5 %all-to-all-start.1 = ((f32[16,256,128]{2,1,0:T(8,128)}), f32[16,256,128]{2,1,0:T(8,128)}, u32[]{:S(2)}, u32[]{:S(2)}) async-start(f32[16,256,128]{2,1,0:T(8,128)} %bitcast.97), calls=%async_computation.1 | async-start | bytes 4194304 | tf_op jit(solution)/shard_map/all_to_all | solution.py:89
  88.2 44.9 %copy-start.12 = (f32[256,64]{0,1:T(8,128)S(1)}, f32[256,64]{0,1:T(8,128)}, u32[]{:S(2)}) copy-start(f32[256,64]{0,1:T(8,128)} %copy-done.11) | copy-start | bytes 196612
  88.2 44.9 %copy-start.23 = (f32[64]{0:T(128)S(1)}, f32[64]{0:T(128)}, u32[]{:S(2)}) copy-start(f32[64]{0:T(128)} %param.24) | copy-start | bytes 772
  129.5 3.7 copy-start.6
  129.5 3.8 copy-start.8
  140.8 10.2 %copy-start.16 = (f32[4096]{0:T(1024)S(1)}, f32[4096]{0:T(1024)}, u32[]{:S(2)}) copy-start(f32[4096]{0:T(1024)} %param.25) | copy-start | bytes 49156
  146.5 4.5 %copy-start.1 = (f32[256,4096]{1,0:T(8,128)S(1)}, f32[256,4096]{1,0:T(8,128)}, u32[]{:S(2)}) copy-start(f32[256,4096]{1,0:T(8,128)} %copy.101) | copy-start | bytes 12582916
  146.5 4.7 %copy-start.4 = (bf16[256,4096]{1,0:T(8,128)(2,1)S(1)}, bf16[256,4096]{1,0:T(8,128)(2,1)}, u32[]{:S(2)}) copy-start(bf16[256,4096]{1,0:T(8,128)(2,1)} %param.18) | copy-start | bytes 6291460
  152.9 1.3 copy-start.5
  154.2 35.2 %copy-start.15 = (s32[256,2]{0,1:T(2,128)S(1)}, s32[256,2]{0,1:T(2,128)}, u32[]{:S(2)}) copy-start(s32[256,2]{0,1:T(2,128)} %param.30) | copy-start | bytes 6148
  154.3 3.1 collective-permute-start
  189.4 10.8 %collective-permute-start.1 = (f32[256,4096]{1,0:T(8,128)}, f32[256,4096]{1,0:T(8,128)}, u32[]{:S(2)}, u32[]{:S(2)}) collective-permute-start(f32[256,4096]{1,0:T(8,128)} %fusion.62), channel_id=1, source_target_pairs={{0,1},{1,0},{2,3},{3,2},{4,5},{5,4},{6,7},{7,6},{8,9},{9,8},{10,11... | collective-permute-start | bytes 12582920 | tf_op jit(solution)/shard_map/ppermute | solution.py:121
  191.6 8.6 %copy-start.7 = (bf16[256,4096]{1,0:T(8,128)(2,1)S(1)}, bf16[256,4096]{1,0:T(8,128)(2,1)}, u32[]{:S(2)}) copy-start(bf16[256,4096]{1,0:T(8,128)(2,1)} %param.27) | copy-start | bytes 6291460
  200.2 3.2 copy-start.17
  203.4 2.0 copy-start.2
  205.4 79.5 %copy-start.19 = (bf16[1,4096,384]{2,1,0:T(8,128)(2,1)S(1)}, bf16[1,4096,384]{2,1,0:T(8,128)(2,1)}, u32[]{:S(2)}) copy-start(bf16[1,4096,384]{2,1,0:T(8,128)(2,1)} %param.32) | copy-start | bytes 9437188
  205.4 79.5 %copy-start.20 = (bf16[1,4096,384]{2,1,0:T(8,128)(2,1)S(1)}, bf16[1,4096,384]{2,1,0:T(8,128)(2,1)}, u32[]{:S(2)}) copy-start(bf16[1,4096,384]{2,1,0:T(8,128)(2,1)} %param.31) | copy-start | bytes 9437188
  295.4 5.1 %copy-start.21 = (bf16[4096,16]{0,1:T(8,128)(2,1)S(1)}, bf16[4096,16]{0,1:T(8,128)(2,1)}, u32[]{:S(2)}) copy-start(bf16[4096,16]{0,1:T(8,128)(2,1)} %param.29) | copy-start | bytes 393220
  295.4 97.4 %all-to-all-start.3 = ((bf16[16,48,4096]{2,1,0:T(8,128)(2,1)}), bf16[16,48,4096]{2,1,0:T(8,128)(2,1)}, u32[]{:S(2)}, u32[]{:S(2)}) async-start(bf16[16,48,4096]{2,1,0:T(8,128)(2,1)} %bitcast.99), calls=%async_computation.3 | async-start | bytes 12582912 | tf_op jit(solution)/shard_map/all_to_all | solution.py:170
  392.9 5.8 %copy-start.3 = (bf16[256,4096]{1,0:T(8,128)(2,1)S(1)}, bf16[256,4096]{1,0:T(8,128)(2,1)}, u32[]{:S(2)}) copy-start(bf16[256,4096]{1,0:T(8,128)(2,1)} %copy-done.2) | copy-start | bytes 6291460
Sparse Core Ops, SparseCore 0:
  9.6 167.2 all-gather.1

commit v10 on v8

--- a/solution.py
+++ b/solution.py
@@ -171,12 +171,14 @@
         experts_all * capacity, width
     )
     picking = (target_pairs.T.reshape(-1)[:, None] == slot_ids[None, :]).astype(jnp.bfloat16)
-    fetched = jnp.dot(picking, returned, preferred_element_type=jnp.float32).reshape(
-        fanout, tokens_here, width
+    fetched = (
+        jnp.dot(picking, returned, preferred_element_type=jnp.float32)
+        .astype(jnp.bfloat16)
+        .reshape(fanout, tokens_here, width)
     )
     total = hidden_wide
     for k in range(fanout):
-        total = total + combine[:, k][:, None] * fetched[k]
+        total = total + combine[:, k][:, None] * fetched[k].astype(jnp.float32)
     return total.astype(jnp.bfloat16)
 
 

time: 409 us -> 410 us (level)
  no operation moved by 1% of the time
where the time goes in v10:
time: 410 us; the launch traced here: 409 us
  waiting for transfers between devices  189 us (46%)
  blocking collectives  79.5 us (19%)
  matrix products  62.1 us (15%)
  local copies, waits for them, and re-layouts  24 us (6%)
  other arithmetic  23.9 us (6%)
  starting transfers between devices  16.9 us (4%)
  between operations  13.9 us (3%)
    all_to_all x1, waiting for transfers between devices, shards(): lax.all_to_all(finished, 'seq', split_axis=0, concat_axis=0, tiled=True)  85.2 us
    all_to_all x1, blocking collectives, shards(): lax.all_to_all(departing_state, 'seq', split_axis=0, concat_axis=0, tiled...  79.5 us
    all_to_all x1, waiting for transfers between devices, shards(): received = lax.all_to_all(packed, 'seq', 0, 0, tiled=True)  41.1 us
    all_to_all x1, waiting for transfers between devices, shards(): lax.all_to_all(entering_each, 'seq', 0, 0, tiled=True)  40.3 us
    all_gather x1, waiting for transfers between devices, shards(): lax.all_gather(lax.dynamic_slice_in_dim(w_out, core * depth, depth, axis=...  19.5 us
    dot_general x1, matrix products, shards(): jnp.dot(partner_rows, w_rows, preferred_element_type=jnp.float32)  12.5 us
    dot_general x1, matrix products, shards(): own_part = jnp.dot(own_rows, w_rows, preferred_element_type=jnp.float32)  8.58 us
  transfers between devices with their start and end apart: 6, of which 5 were waited for; matrix products, arithmetic and copies ran while one was open for 17% of the time, Pallas kernels for 0%

profile of v10, /device:TPU:0, one launch (start us, length us, event | category | flops | bytes accessed | tf_op | source)
XLA Modules:
  0.0 409.3 jit_solution(18296791106345416006)
XLA Ops:
  6.5 2.5 constant_dynamic-slice_fusion.1
  9.1 0.0 all-gather.2.cloned.1.call-update
  9.1 0.7 exp.47
  9.8 1.0 multiply_bitcast_fusion
  10.7 0.6 reduce-window.16
  11.3 0.2 slice_reduce_fusion
  11.6 4.1 copy.98
  15.7 0.1 bitcast_bitcast_fusion
  15.7 0.2 slice_reduce_fusion.2
  15.9 0.1 broadcast_in_dim.119
  16.0 0.7 fusion.55
  16.8 4.6 %fusion.27 = f32[64,128,64]{1,2,0:T(8,128)S(1)} fusion(bf16[256,64,64]{0,2,1:T(8,128)(2,1)} %bitcast.102, f32[256,128]{1,0:T(8,128)S(1)} %convert_element_type.74, f32[256,64]{0,1:T(8,128)S(1)} %get-tuple-element.36, f32[64]{0:T(128)S(1)} %exponential_multiply_fusion.1), kind=kOutput, calls=%fused_computation.47 | convolution fusion | flops 273154048 | bytes 4391168 | tf_op jit(solution)/shard_map/while/body/eval_jaxpr/shn,shp->hpn/dot_general | solution.py:27
  21.4 0.1 broadcast_in_dim.120
  21.5 1.5 select_maximum_fusion
  22.9 7.2 %all-to-all-start = ((f32[16,264,128]{2,1,0:T(8,128)}), f32[16,264,128]{2,1,0:T(8,128)}, u32[]{:S(2)}, u32[]{:S(2)}) async-start(f32[16,264,128]{2,1,0:T(8,128)} %select_maximum_fusion), calls=%async_computation | async-start | bytes 4325376 | tf_op jit(solution)/shard_map/all_to_all | solution.py:78
  30.2 41.1 %all-to-all-done = f32[16,264,128]{2,1,0:T(8,128)} async-done(((f32[16,264,128]{2,1,0:T(8,128)}), f32[16,264,128]{2,1,0:T(8,128)}, u32[]{:S(2)}, u32[]{:S(2)}) %all-to-all-start) | async-done | bytes 2162720 | tf_op jit(solution)/shard_map/all_to_all | solution.py:78
  71.3 0.8 slice.71
  72.1 0.1 copy.99
  72.3 0.2 select_reduce_fusion
  72.5 0.2 copy.100
  72.7 1.7 slice.72
  74.5 5.5 %multiply_reduce_fusion = f32[16,4,64,128]{3,2,1,0:T(8,128)} fusion(f32[16,4,64,128]{3,2,1,0:T(8,128)S(1)} %bitcast.98, f32[16,16,4]{2,1,0:T(8,128)S(1)} %copy.100), kind=kLoop, calls=%fused_computation.1 | loop fusion | flops 16252928 | bytes 4198400 | tf_op jit(solution)/shard_map/reduce_sum | solution.py:86
  79.9 4.6 %all-to-all-start.1 = ((f32[16,256,128]{2,1,0:T(8,128)}), f32[16,256,128]{2,1,0:T(8,128)}, u32[]{:S(2)}, u32[]{:S(2)}) async-start(f32[16,256,128]{2,1,0:T(8,128)} %bitcast.97), calls=%async_computation.1 | async-start | bytes 4194304 | tf_op jit(solution)/shard_map/all_to_all | solution.py:89
  84.6 0.6 iota_compare_fusion.6
  85.2 0.2 fusion.60
  85.4 3.7 fusion.31
  89.2 40.3 %all-to-all-done.1 = f32[16,256,128]{2,1,0:T(8,128)} async-done(((f32[16,256,128]{2,1,0:T(8,128)}), f32[16,256,128]{2,1,0:T(8,128)}, u32[]{:S(2)}, u32[]{:S(2)}) %all-to-all-start.1) | async-done | bytes 2097184 | tf_op jit(solution)/shard_map/all_to_all | solution.py:89
  129.5 3.6 fusion.43
  133.2 0.2 copy-done.8
  133.3 7.5 %fusion.22 = f32[256,64,64]{0,2,1:T(8,128)} fusion(f32[64,64,256]{2,1,0:T(8,128)S(1)} %fusion.43, f32[64,64,256]{2,1,0:T(8,128)S(1)} %copy-done.6, bf16[256,64,64]{0,2,1:T(8,128)(2,1)S(1)} %bitcast.103, f32[256,64]{0,1:T(8,128)S(1)} %copy-done.12, f32[256,64]{0,1:T(8,128)} %copy-done.13, f32[256,256]{1,0:T(8,128)S(1)} %fusion.60, ...), kind=kOutput, calls=%fused_computation.35 | convolution fusion | flops 565182464 | bytes 15204608 | tf_op jit(solution)/shard_map/while/body/eval_jaxpr/tsh,shp->thp/dot_general | solution.py:18
  140.8 5.6 %copy.101 = f32[256,4096]{1,0:T(8,128)} copy(f32[256,4096]{0,1:T(8,128)} %bitcast.101) | data formatting | bytes 8388608 | tf_op jit(solution)/shard_map/reshape | solution.py:101
  146.5 4.5 %multiply_reduce_fusion.1 = f32[256]{0:T(256)S(1)} fusion(f32[256,4096]{1,0:T(8,128)} %copy.101, bf16[256,4096]{1,0:T(8,128)(2,1)} %param.18), kind=kLoop, calls=%fused_computation.41 | loop fusion | flops 8388352 | bytes 6292480 | tf_op jit(solution)/shard_map/reduce_sum | solution.py:104
  151.0 0.2 copy-done.4
  151.2 1.7 multiply_convert_fusion.4
  152.9 1.3 copy-done.5
  154.2 0.1 constant_dynamic-slice_fusion
  154.3 0.3 collective-permute-start
  154.6 2.8 collective-permute-done
  157.4 19.5 %all-gather.2.cloned.1.call-done = bf16[2048,4096]{1,0:T(8,128)(2,1)} async-done(((bf16[2048,256]{1,0:T(8,128)(2,1)}), bf16[2048,4096]{1,0:T(8,128)(2,1)}) %all-gather.2.cloned.1.call-update) | async-done | bytes 16777232 | tf_op jit(solution)/shard_map/wgather/all_gather | solution.py:111
  176.9 12.5 %fusion.61 = f32[256,4096]{1,0:T(8,128)} fusion(bf16[256,2048]{1,0:T(8,128)(2,1)} %collective-permute-done, bf16[2048,4096]{1,0:T(8,128)(2,1)} %all-gather.2.cloned.1.call-done), kind=kOutput, calls=%fused_computation.111 | convolution fusion | flops 4294967296 | bytes 22020096 | tf_op jit(solution)/shard_map/dot_general | solution.py:120
  189.4 0.1 copy.104
  189.6 0.1 eq.76
  189.7 0.1 eq.72
  189.9 1.2 reduce-window.24
  191.0 0.2 slice_reduce_fusion.1
  191.3 0.1 fusion.47
  191.4 0.1 sub.48
  191.6 0.1 copy.107
  191.7 8.6 %fusion.29 = f32[256,4096]{1,0:T(8,128)S(1)} fusion(bf16[2048,4096]{1,0:T(8,128)(2,1)} %all-gather.2.cloned.1.call-done, bf16[256,4096]{1,0:T(8,128)(2,1)} %copy-done.5, s32[]{:T(128)S(6)} %select_n.48), kind=kOutput, calls=%fused_computation.51 | convolution fusion | flops 4294967296 | bytes 22020100 | tf_op jit(solution)/shard_map/dot_general | solution.py:119
  200.3 3.1 fusion.15
  203.5 2.0 convolution_convert_fusion
  205.5 79.5 %all_to_all.20 = bf16[16,48,4096]{2,1,0:T(8,128)(2,1)S(1)} all-to-all(bf16[16,48,4096]{2,1,0:T(8,128)(2,1)S(1)} %bitcast.96), channel_id=1, replica_groups=mesh['seq'=16,'batch'=8] {'seq'}, dimensions={0} | all-to-all | bytes 12582912 | tf_op jit(solution)/shard_map/all_to_all | solution.py:155
  285.0 5.0 %fusion.7 = f32[768,768]{1,0:T(8,128)S(1)} fusion(bf16[768,4096]{1,0:T(8,128)(2,1)S(1)} %bitcast.100, bf16[4096,384]{1,0:T(8,128)(2,1)S(1)} %bitcast.113, bf16[4096,384]{1,0:T(8,128)(2,1)S(1)} %bitcast.114), kind=kOutput, calls=%fused_computation.13 | convolution fusion | flops 4844421120 | bytes 14942208 | tf_op jit(solution)/shard_map/dot_general | solution.py:158
  290.0 5.4 %convolution_convert_fusion.1 = bf16[768,4096]{1,0:T(8,128)(2,1)} fusion(bf16[1,384,4096]{2,1,0:T(8,128)(2,1)S(1)} %copy-done, f32[768,768]{1,0:T(8,128)S(1)} %fusion.7), kind=kOutput, calls=%fused_computation.12 | convolution fusion | flops 2420834304 | bytes 11796480 | tf_op jit(solution)/shard_map/dot_general | solution.py:166
  295.4 4.8 %all-to-all-start.3 = ((bf16[16,48,4096]{2,1,0:T(8,128)(2,1)}), bf16[16,48,4096]{2,1,0:T(8,128)(2,1)}, u32[]{:S(2)}, u32[]{:S(2)}) async-start(bf16[16,48,4096]{2,1,0:T(8,128)(2,1)} %bitcast.99), calls=%async_computation.3 | async-start | bytes 12582912 | tf_op jit(solution)/shard_map/all_to_all | solution.py:170
  300.2 0.1 copy.102
  300.3 0.1 reshape.202
  300.5 2.3 fusion.37
  302.8 4.6 %gather_fusion = f32[512]{0:T(512)S(1)} fusion(f32[256,16]{0,1:T(8,128)S(1)} %fusion.37, s32[512]{0:T(512)S(1)} %reshape.202), kind=kCustom, calls=%fused_computation | custom fusion | bytes 8192 | tf_op jit(solution)/shard_map/jit(take_along_axis)/gather | solution.py:131
  307.4 0.1 reshape.205
  307.5 0.1 copy.103
  307.7 85.2 %all-to-all-done.3 = bf16[16,48,4096]{2,1,0:T(8,128)(2,1)} async-done(((bf16[16,48,4096]{2,1,0:T(8,128)(2,1)}), bf16[16,48,4096]{2,1,0:T(8,128)(2,1)}, u32[]{:S(2)}, u32[]{:S(2)}) %all-to-all-start.3) | async-done | bytes 6291488 | tf_op jit(solution)/shard_map/all_to_all | solution.py:170
  392.9 6.7 %convolution_convert_fusion.2 = bf16[512,4096]{1,0:T(8,128)(2,1)S(1)} fusion(bf16[768,4096]{1,0:T(8,128)(2,1)} %bitcast.26, s32[512]{0:T(512)S(1)} %bitcast.112), kind=kOutput, calls=%fused_computation.20 | convolution fusion | flops 3223715840 | bytes 10487808 | tf_op jit(solution)/shard_map/dot_general | solution.py:175
  399.5 2.9 fusion.19
  (64 shorter events, 0.4 us)
Async XLA Ops:
  6.5 283.5 %copy-start = (bf16[1,384,4096]{2,1,0:T(8,128)(2,1)S(1)}, bf16[1,384,4096]{2,1,0:T(8,128)(2,1)}, u32[]{:S(2)}) copy-start(bf16[1,384,4096]{2,1,0:T(8,128)(2,1)} %param.33) | copy-start | bytes 9437188
  6.5 9.1 %copy-start.10 = (bf16[256,128]{1,0:T(8,128)(2,1)S(1)}, bf16[256,128]{1,0:T(8,128)(2,1)}, u32[]{:S(2)}) copy-start(bf16[256,128]{1,0:T(8,128)(2,1)} %param.19) | copy-start | bytes 196612
  6.5 170.4 %all-gather.2.cloned.1.call-start = ((), (), s32[]{:S(2)}) async-start(), calls=%async_computation.4 | async-start | bytes 17825792 | tf_op jit(solution)/shard_map/wgather/all_gather | solution.py:111
  10.7 10.7 %copy-start.11 = (f32[256,64]{0,1:T(8,128)}, f32[256,64]{0,1:T(8,128)S(1)}, u32[]{:S(2)}) copy-start(f32[256,64]{0,1:T(8,128)S(1)} %get-tuple-element.32) | copy-start | bytes 196612
  15.7 7.2 %copy-start.13 = (f32[256,64]{0,1:T(8,128)}, f32[256,64]{0,1:T(8,128)S(1)}, u32[]{:S(2)}) copy-start(f32[256,64]{0,1:T(8,128)S(1)} %bitcast_bitcast_fusion) | copy-start | bytes 196612
  22.9 48.4 %all-to-all-start = ((f32[16,264,128]{2,1,0:T(8,128)}), f32[16,264,128]{2,1,0:T(8,128)}, u32[]{:S(2)}, u32[]{:S(2)}) async-start(f32[16,264,128]{2,1,0:T(8,128)} %select_maximum_fusion), calls=%async_computation | async-start | bytes 4325376 | tf_op jit(solution)/shard_map/all_to_all | solution.py:78
  74.4 10.8 %copy-start.9 = (bf16[256,128]{1,0:T(8,128)(2,1)S(1)}, bf16[256,128]{1,0:T(8,128)(2,1)}, u32[]{:S(2)}) copy-start(bf16[256,128]{1,0:T(8,128)(2,1)} %param.20) | copy-start | bytes 196612
  79.9 49.6 %all-to-all-start.1 = ((f32[16,256,128]{2,1,0:T(8,128)}), f32[16,256,128]{2,1,0:T(8,128)}, u32[]{:S(2)}, u32[]{:S(2)}) async-start(f32[16,256,128]{2,1,0:T(8,128)} %bitcast.97), calls=%async_computation.1 | async-start | bytes 4194304 | tf_op jit(solution)/shard_map/all_to_all | solution.py:89
  89.1 44.0 %copy-start.12 = (f32[256,64]{0,1:T(8,128)S(1)}, f32[256,64]{0,1:T(8,128)}, u32[]{:S(2)}) copy-start(f32[256,64]{0,1:T(8,128)} %copy-done.11) | copy-start | bytes 196612
  89.2 44.0 %copy-start.20 = (f32[64]{0:T(128)S(1)}, f32[64]{0:T(128)}, u32[]{:S(2)}) copy-start(f32[64]{0:T(128)} %param.24) | copy-start | bytes 772
  129.5 3.7 copy-start.6
  129.5 3.8 copy-start.8
  140.8 10.2 %copy-start.15 = (f32[4096]{0:T(1024)S(1)}, f32[4096]{0:T(1024)}, u32[]{:S(2)}) copy-start(f32[4096]{0:T(1024)} %param.25) | copy-start | bytes 49156
  146.5 4.5 %copy-start.1 = (f32[256,4096]{1,0:T(8,128)S(1)}, f32[256,4096]{1,0:T(8,128)}, u32[]{:S(2)}) copy-start(f32[256,4096]{1,0:T(8,128)} %copy.101) | copy-start | bytes 12582916
  146.5 4.7 %copy-start.4 = (bf16[256,4096]{1,0:T(8,128)(2,1)S(1)}, bf16[256,4096]{1,0:T(8,128)(2,1)}, u32[]{:S(2)}) copy-start(bf16[256,4096]{1,0:T(8,128)(2,1)} %param.18) | copy-start | bytes 6291460
  152.9 1.3 copy-start.5
  154.3 35.2 %copy-start.14 = (s32[256,2]{0,1:T(2,128)S(1)}, s32[256,2]{0,1:T(2,128)}, u32[]{:S(2)}) copy-start(s32[256,2]{0,1:T(2,128)} %param.30) | copy-start | bytes 6148
  154.3 3.1 collective-permute-start
  189.4 10.8 %collective-permute-start.1 = (f32[256,4096]{1,0:T(8,128)}, f32[256,4096]{1,0:T(8,128)}, u32[]{:S(2)}, u32[]{:S(2)}) collective-permute-start(f32[256,4096]{1,0:T(8,128)} %fusion.61), channel_id=1, source_target_pairs={{0,1},{1,0},{2,3},{3,2},{4,5},{5,4},{6,7},{7,6},{8,9},{9,8},{10,11... | collective-permute-start | bytes 12582920 | tf_op jit(solution)/shard_map/ppermute | solution.py:121
  191.7 8.6 %copy-start.7 = (bf16[256,4096]{1,0:T(8,128)(2,1)S(1)}, bf16[256,4096]{1,0:T(8,128)(2,1)}, u32[]{:S(2)}) copy-start(bf16[256,4096]{1,0:T(8,128)(2,1)} %param.27) | copy-start | bytes 6291460
  200.3 3.2 copy-start.16
  203.4 2.0 copy-start.2
  205.4 79.5 %copy-start.17 = (bf16[1,4096,384]{2,1,0:T(8,128)(2,1)S(1)}, bf16[1,4096,384]{2,1,0:T(8,128)(2,1)}, u32[]{:S(2)}) copy-start(bf16[1,4096,384]{2,1,0:T(8,128)(2,1)} %param.32) | copy-start | bytes 9437188
  205.5 79.5 %copy-start.18 = (bf16[1,4096,384]{2,1,0:T(8,128)(2,1)S(1)}, bf16[1,4096,384]{2,1,0:T(8,128)(2,1)}, u32[]{:S(2)}) copy-start(bf16[1,4096,384]{2,1,0:T(8,128)(2,1)} %param.31) | copy-start | bytes 9437188
  295.4 5.1 %copy-start.19 = (bf16[4096,16]{0,1:T(8,128)(2,1)S(1)}, bf16[4096,16]{0,1:T(8,128)(2,1)}, u32[]{:S(2)}) copy-start(bf16[4096,16]{0,1:T(8,128)(2,1)} %param.29) | copy-start | bytes 393220
  295.4 97.4 %all-to-all-start.3 = ((bf16[16,48,4096]{2,1,0:T(8,128)(2,1)}), bf16[16,48,4096]{2,1,0:T(8,128)(2,1)}, u32[]{:S(2)}, u32[]{:S(2)}) async-start(bf16[16,48,4096]{2,1,0:T(8,128)(2,1)} %bitcast.99), calls=%async_computation.3 | async-start | bytes 12582912 | tf_op jit(solution)/shard_map/all_to_all | solution.py:170
  392.9 6.7 %copy-start.3 = (bf16[256,4096]{1,0:T(8,128)(2,1)S(1)}, bf16[256,4096]{1,0:T(8,128)(2,1)}, u32[]{:S(2)}) copy-start(bf16[256,4096]{1,0:T(8,128)(2,1)} %copy-done.2) | copy-start | bytes 6291460
Sparse Core Ops, SparseCore 0:
  9.4 167.4 all-gather.1

commit v11 on v8

--- a/solution.py
+++ b/solution.py
@@ -116,8 +116,11 @@
     partner_rows = lax.ppermute(
         lax.dynamic_slice_in_dim(normed, (1 - core) * depth, depth, axis=1), "batch", partners
     )
-    own_part = jnp.dot(own_rows, w_rows, preferred_element_type=jnp.float32)
-    partner_part = jnp.dot(partner_rows, w_rows, preferred_element_type=jnp.float32)
+    both_parts = jnp.dot(
+        jnp.concatenate([partner_rows, own_rows], axis=0), w_rows, preferred_element_type=jnp.float32
+    )
+    partner_part = both_parts[:tokens_here]
+    own_part = both_parts[tokens_here:]
     other_part = lax.ppermute(partner_part, "batch", partners)
     mixer_out = (own_part + other_part).astype(jnp.bfloat16)
     hidden = (residual.astype(jnp.float32) + mixer_out.astype(jnp.float32)).astype(jnp.bfloat16)

time: 409 us -> 410 us (level)
  matrix products: 61.2 us -> 52.3 us
  waiting for transfers between devices: 189 us -> 194 us
  local copies, waits for them, and re-layouts: 24 us -> 28.2 us
    dot_general x2 -> x1, matrix products: 21.1 us -> 12.2 us  [shards(): jnp.dot(jnp.concatenate([partner_rows, own_rows], axis=0), w_rows, prefer...]
    ppermute x1, waiting for transfers between devices: 0.01 us -> 5.28 us  [shards(): other_part = lax.ppermute(partner_part, 'batch', partners)]
  transfers between devices with their start and end apart: 6 -> 6, of which waited for: 5 -> 6; matrix products, arithmetic and copies ran while one was open for 17% -> 15% of each run, Pallas kernels for 0% -> 0%
where the time goes in v11:
time: 410 us; the launch traced here: 409 us
  waiting for transfers between devices  194 us (47%)
  blocking collectives  78.6 us (19%)
  matrix products  52.3 us (13%)
  local copies, waits for them, and re-layouts  28.2 us (7%)
  other arithmetic  25.5 us (6%)
  starting transfers between devices  16.8 us (4%)
  between operations  13.8 us (3%)
    all_to_all x1, waiting for transfers between devices, shards(): lax.all_to_all(finished, 'seq', split_axis=0, concat_axis=0, tiled=True)  84.4 us
    all_to_all x1, blocking collectives, shards(): lax.all_to_all(departing_state, 'seq', split_axis=0, concat_axis=0, tiled...  78.6 us
    all_to_all x1, waiting for transfers between devices, shards(): received = lax.all_to_all(packed, 'seq', 0, 0, tiled=True)  41.1 us
    all_to_all x1, waiting for transfers between devices, shards(): lax.all_to_all(entering_each, 'seq', 0, 0, tiled=True)  40.3 us
    all_gather x1, waiting for transfers between devices, shards(): lax.all_gather(lax.dynamic_slice_in_dim(w_out, core * depth, depth, axis=...  20.1 us
    dot_general x1, matrix products, shards(): jnp.dot(jnp.concatenate([partner_rows, own_rows], axis=0), w_rows, prefer...  12.2 us
  transfers between devices with their start and end apart: 6, of which 6 were waited for; matrix products, arithmetic and copies ran while one was open for 15% of the time, Pallas kernels for 0%

profile of v11, /device:TPU:0, one launch (start us, length us, event | category | flops | bytes accessed | tf_op | source)
XLA Modules:
  0.0 409.5 jit_solution(18169038439958819513)
XLA Ops:
  6.5 2.5 constant_dynamic-slice_fusion
  9.1 0.0 all-gather.2.cloned.1.call-update
  9.1 0.7 exp.47
  9.8 1.0 multiply_bitcast_fusion
  10.7 0.6 reduce-window.16
  11.3 0.2 slice_reduce_fusion
  11.6 4.1 copy.98
  15.7 0.1 bitcast_bitcast_fusion
  15.7 0.2 slice_reduce_fusion.2
  15.9 0.1 broadcast_in_dim.119
  16.0 0.7 fusion.59
  16.8 4.6 %fusion.32 = f32[64,128,64]{1,2,0:T(8,128)S(1)} fusion(bf16[256,64,64]{0,2,1:T(8,128)(2,1)} %bitcast.100, f32[256,128]{1,0:T(8,128)S(1)} %convert_element_type.65, f32[256,64]{0,1:T(8,128)S(1)} %get-tuple-element.38, f32[64]{0:T(128)S(1)} %exponential_multiply_fusion.1), kind=kOutput, calls=%fused_computation.53 | convolution fusion | flops 273154048 | bytes 4391168 | tf_op jit(solution)/shard_map/while/body/eval_jaxpr/shn,shp->hpn/dot_general | solution.py:27
  21.4 0.1 broadcast_in_dim.120
  21.5 1.5 select_maximum_fusion
  22.9 7.2 %all-to-all-start = ((f32[16,264,128]{2,1,0:T(8,128)}), f32[16,264,128]{2,1,0:T(8,128)}, u32[]{:S(2)}, u32[]{:S(2)}) async-start(f32[16,264,128]{2,1,0:T(8,128)} %select_maximum_fusion), calls=%async_computation | async-start | bytes 4325376 | tf_op jit(solution)/shard_map/all_to_all | solution.py:78
  30.2 41.1 %all-to-all-done = f32[16,264,128]{2,1,0:T(8,128)} async-done(((f32[16,264,128]{2,1,0:T(8,128)}), f32[16,264,128]{2,1,0:T(8,128)}, u32[]{:S(2)}, u32[]{:S(2)}) %all-to-all-start) | async-done | bytes 2162720 | tf_op jit(solution)/shard_map/all_to_all | solution.py:78
  71.3 0.8 slice.79
  72.1 0.1 copy.99
  72.3 0.2 select_reduce_fusion
  72.5 0.2 copy.100
  72.7 1.7 slice.80
  74.5 5.5 %multiply_reduce_fusion = f32[16,4,64,128]{3,2,1,0:T(8,128)} fusion(f32[16,4,64,128]{3,2,1,0:T(8,128)S(1)} %bitcast.96, f32[16,16,4]{2,1,0:T(8,128)S(1)} %copy.100), kind=kLoop, calls=%fused_computation.1 | loop fusion | flops 16252928 | bytes 4198400 | tf_op jit(solution)/shard_map/reduce_sum | solution.py:86
  79.9 4.6 %all-to-all-start.1 = ((f32[16,256,128]{2,1,0:T(8,128)}), f32[16,256,128]{2,1,0:T(8,128)}, u32[]{:S(2)}, u32[]{:S(2)}) async-start(f32[16,256,128]{2,1,0:T(8,128)} %bitcast.95), calls=%async_computation.1 | async-start | bytes 4194304 | tf_op jit(solution)/shard_map/all_to_all | solution.py:89
  84.6 0.6 iota_compare_fusion.6
  85.2 0.2 fusion.64
  85.4 3.7 fusion.35
  89.2 40.3 %all-to-all-done.1 = f32[16,256,128]{2,1,0:T(8,128)} async-done(((f32[16,256,128]{2,1,0:T(8,128)}), f32[16,256,128]{2,1,0:T(8,128)}, u32[]{:S(2)}, u32[]{:S(2)}) %all-to-all-start.1) | async-done | bytes 2097184 | tf_op jit(solution)/shard_map/all_to_all | solution.py:89
  129.5 3.6 fusion.47
  133.2 0.2 copy-done.7
  133.3 7.5 %fusion.23 = f32[256,64,64]{0,2,1:T(8,128)} fusion(f32[64,64,256]{2,1,0:T(8,128)S(1)} %fusion.47, f32[64,64,256]{2,1,0:T(8,128)S(1)} %copy-done.6, bf16[256,64,64]{0,2,1:T(8,128)(2,1)S(1)} %bitcast.101, f32[256,64]{0,1:T(8,128)S(1)} %copy-done.11, f32[256,64]{0,1:T(8,128)} %copy-done.12, f32[256,256]{1,0:T(8,128)S(1)} %fusion.64, ...), kind=kOutput, calls=%fused_computation.38 | convolution fusion | flops 565182464 | bytes 15204608 | tf_op jit(solution)/shard_map/while/body/eval_jaxpr/tsh,shp->thp/dot_general | solution.py:18
  140.8 5.6 %copy.101 = f32[256,4096]{1,0:T(8,128)} copy(f32[256,4096]{0,1:T(8,128)} %bitcast.99) | data formatting | bytes 8388608 | tf_op jit(solution)/shard_map/reshape | solution.py:101
  146.5 4.5 %multiply_reduce_fusion.1 = f32[256]{0:T(256)S(1)} fusion(f32[256,4096]{1,0:T(8,128)} %copy.101, bf16[256,4096]{1,0:T(8,128)(2,1)} %param.18), kind=kLoop, calls=%fused_computation.43 | loop fusion | flops 8388352 | bytes 6292480 | tf_op jit(solution)/shard_map/reduce_sum | solution.py:104
  151.0 0.2 copy-done.5
  151.2 1.7 multiply_convert_fusion.4
  152.9 1.2 constant_dynamic-slice_fusion.2
  154.0 2.8 collective-permute-done
  156.8 20.1 %all-gather.2.cloned.1.call-done = bf16[2048,4096]{1,0:T(8,128)(2,1)} async-done(((bf16[2048,256]{1,0:T(8,128)(2,1)}), bf16[2048,4096]{1,0:T(8,128)(2,1)}) %all-gather.2.cloned.1.call-update) | async-done | bytes 16777232 | tf_op jit(solution)/shard_map/wgather/all_gather | solution.py:111
  176.9 12.2 %fusion.28 = f32[512,4096]{1,0:T(8,128)S(1)} fusion(bf16[2048,4096]{1,0:T(8,128)(2,1)} %all-gather.2.cloned.1.call-done, bf16[256,2048]{1,0:T(8,128)(2,1)} %get-tuple-element.36, bf16[256,2048]{1,0:T(8,128)(2,1)} %collective-permute-done), kind=kOutput, calls=%fused_computation.49 | convolution fusion | flops 8594128896 | bytes 27262976 | tf_op jit(solution)/shard_map/dot_general | solution.py:119
  189.2 2.8 slice.82
  191.9 1.7 copy-done.4
  193.6 0.1 copy.104
  193.7 0.1 eq.76
  193.9 0.1 eq.72
  194.1 1.2 reduce-window.24
  195.2 0.2 slice_reduce_fusion.1
  195.5 0.1 fusion.51
  195.6 0.1 sub.48
  195.7 0.1 copy.107
  195.8 5.3 %collective-permute-done.1 = f32[256,4096]{1,0:T(8,128)} collective-permute-done((f32[256,4096]{1,0:T(8,128)}, f32[256,4096]{1,0:T(8,128)}, u32[]{:S(2)}, u32[]{:S(2)}) %collective-permute-start.1) | collective-permute-done | bytes 4194336 | tf_op jit(solution)/shard_map/ppermute | solution.py:124
  201.1 5.0 %fusion.15 = (f32[256]{0:T(256)S(1)}, bf16[256,4096]{1,0:T(8,128)(2,1)S(1)}) fusion(f32[256,4096]{1,0:T(8,128)} %collective-permute-done.1, f32[512,4096]{1,0:T(8,128)} %copy-done.4, bf16[256,4096]{1,0:T(8,128)(2,1)} %param.27), kind=kLoop, calls=%fused_computation.26 | loop fusion | flops 9436928 | bytes 12583936 | tf_op jit(solution)/shard_map/reduce_sum | solution.py:130
  206.2 2.0 convolution_convert_fusion
  208.2 78.6 %all_to_all.20 = bf16[16,48,4096]{2,1,0:T(8,128)(2,1)S(1)} all-to-all(bf16[16,48,4096]{2,1,0:T(8,128)(2,1)S(1)} %bitcast.94), channel_id=1, replica_groups=mesh['seq'=16,'batch'=8] {'seq'}, dimensions={0} | all-to-all | bytes 12582912 | tf_op jit(solution)/shard_map/all_to_all | solution.py:158
  286.8 5.0 %fusion.7 = f32[768,768]{1,0:T(8,128)S(1)} fusion(bf16[768,4096]{1,0:T(8,128)(2,1)S(1)} %bitcast.98, bf16[4096,384]{1,0:T(8,128)(2,1)S(1)} %bitcast.111, bf16[4096,384]{1,0:T(8,128)(2,1)S(1)} %bitcast.112), kind=kOutput, calls=%fused_computation.13 | convolution fusion | flops 4844421120 | bytes 14942208 | tf_op jit(solution)/shard_map/dot_general | solution.py:161
  291.9 5.4 %convolution_convert_fusion.1 = bf16[768,4096]{1,0:T(8,128)(2,1)} fusion(bf16[1,384,4096]{2,1,0:T(8,128)(2,1)S(1)} %copy-done, f32[768,768]{1,0:T(8,128)S(1)} %fusion.7), kind=kOutput, calls=%fused_computation.12 | convolution fusion | flops 2420834304 | bytes 11796480 | tf_op jit(solution)/shard_map/dot_general | solution.py:169
  297.3 5.0 %all-to-all-start.3 = ((bf16[16,48,4096]{2,1,0:T(8,128)(2,1)}), bf16[16,48,4096]{2,1,0:T(8,128)(2,1)}, u32[]{:S(2)}, u32[]{:S(2)}) async-start(bf16[16,48,4096]{2,1,0:T(8,128)(2,1)} %bitcast.97), calls=%async_computation.3 | async-start | bytes 12582912 | tf_op jit(solution)/shard_map/all_to_all | solution.py:173
  302.3 0.1 copy.102
  302.5 0.1 reshape.202
  302.6 2.3 fusion.41
  304.9 4.6 %gather_fusion = f32[512]{0:T(512)S(1)} fusion(f32[256,16]{0,1:T(8,128)S(1)} %fusion.41, s32[512]{0:T(512)S(1)} %reshape.202), kind=kCustom, calls=%fused_computation | custom fusion | bytes 8192 | tf_op jit(solution)/shard_map/jit(take_along_axis)/gather | solution.py:134
  309.5 0.1 reshape.205
  309.6 0.1 copy.103
  309.8 84.4 %all-to-all-done.3 = bf16[16,48,4096]{2,1,0:T(8,128)(2,1)} async-done(((bf16[16,48,4096]{2,1,0:T(8,128)(2,1)}), bf16[16,48,4096]{2,1,0:T(8,128)(2,1)}, u32[]{:S(2)}, u32[]{:S(2)}) %all-to-all-start.3) | async-done | bytes 6291488 | tf_op jit(solution)/shard_map/all_to_all | solution.py:173
  394.2 5.7 %fusion.33 = f32[512,4096]{1,0:T(8,128)S(1)} fusion(bf16[768,4096]{1,0:T(8,128)(2,1)} %bitcast.26, s32[512]{0:T(512)S(1)} %bitcast.110), kind=kOutput, calls=%fused_computation.55 | convolution fusion | flops 3221618688 | bytes 14682112 | tf_op jit(solution)/shard_map/dot_general | solution.py:177
  400.0 2.6 fusion.19
  (62 shorter events, 0.3 us)
Async XLA Ops:
  6.5 285.3 %copy-start = (bf16[1,384,4096]{2,1,0:T(8,128)(2,1)S(1)}, bf16[1,384,4096]{2,1,0:T(8,128)(2,1)}, u32[]{:S(2)}) copy-start(bf16[1,384,4096]{2,1,0:T(8,128)(2,1)} %param.33) | copy-start | bytes 9437188
  6.5 9.1 %copy-start.9 = (bf16[256,128]{1,0:T(8,128)(2,1)S(1)}, bf16[256,128]{1,0:T(8,128)(2,1)}, u32[]{:S(2)}) copy-start(bf16[256,128]{1,0:T(8,128)(2,1)} %param.19) | copy-start | bytes 196612
  6.5 170.4 %all-gather.2.cloned.1.call-start = ((), (), s32[]{:S(2)}) async-start(), calls=%async_computation.4 | async-start | bytes 17825792 | tf_op jit(solution)/shard_map/wgather/all_gather | solution.py:111
  10.7 10.7 %copy-start.10 = (f32[256,64]{0,1:T(8,128)}, f32[256,64]{0,1:T(8,128)S(1)}, u32[]{:S(2)}) copy-start(f32[256,64]{0,1:T(8,128)S(1)} %get-tuple-element.32) | copy-start | bytes 196612
  15.7 7.2 %copy-start.12 = (f32[256,64]{0,1:T(8,128)}, f32[256,64]{0,1:T(8,128)S(1)}, u32[]{:S(2)}) copy-start(f32[256,64]{0,1:T(8,128)S(1)} %bitcast_bitcast_fusion) | copy-start | bytes 196612
  22.9 48.4 %all-to-all-start = ((f32[16,264,128]{2,1,0:T(8,128)}), f32[16,264,128]{2,1,0:T(8,128)}, u32[]{:S(2)}, u32[]{:S(2)}) async-start(f32[16,264,128]{2,1,0:T(8,128)} %select_maximum_fusion), calls=%async_computation | async-start | bytes 4325376 | tf_op jit(solution)/shard_map/all_to_all | solution.py:78
  74.4 10.8 %copy-start.8 = (bf16[256,128]{1,0:T(8,128)(2,1)S(1)}, bf16[256,128]{1,0:T(8,128)(2,1)}, u32[]{:S(2)}) copy-start(bf16[256,128]{1,0:T(8,128)(2,1)} %param.20) | copy-start | bytes 196612
  79.9 49.6 %all-to-all-start.1 = ((f32[16,256,128]{2,1,0:T(8,128)}), f32[16,256,128]{2,1,0:T(8,128)}, u32[]{:S(2)}, u32[]{:S(2)}) async-start(f32[16,256,128]{2,1,0:T(8,128)} %bitcast.95), calls=%async_computation.1 | async-start | bytes 4194304 | tf_op jit(solution)/shard_map/all_to_all | solution.py:89
  89.1 44.0 %copy-start.11 = (f32[256,64]{0,1:T(8,128)S(1)}, f32[256,64]{0,1:T(8,128)}, u32[]{:S(2)}) copy-start(f32[256,64]{0,1:T(8,128)} %copy-done.10) | copy-start | bytes 196612
  89.2 44.0 %copy-start.19 = (f32[64]{0:T(128)S(1)}, f32[64]{0:T(128)}, u32[]{:S(2)}) copy-start(f32[64]{0:T(128)} %param.24) | copy-start | bytes 772
  129.5 3.7 copy-start.6
  129.5 3.8 copy-start.7
  140.8 10.2 %copy-start.14 = (f32[4096]{0:T(1024)S(1)}, f32[4096]{0:T(1024)}, u32[]{:S(2)}) copy-start(f32[4096]{0:T(1024)} %param.25) | copy-start | bytes 49156
  146.5 4.5 %copy-start.1 = (f32[256,4096]{1,0:T(8,128)S(1)}, f32[256,4096]{1,0:T(8,128)}, u32[]{:S(2)}) copy-start(f32[256,4096]{1,0:T(8,128)} %copy.101) | copy-start | bytes 12582916
  146.5 4.7 %copy-start.5 = (bf16[256,4096]{1,0:T(8,128)(2,1)S(1)}, bf16[256,4096]{1,0:T(8,128)(2,1)}, u32[]{:S(2)}) copy-start(bf16[256,4096]{1,0:T(8,128)(2,1)} %param.18) | copy-start | bytes 6291460
  154.0 2.8 collective-permute-start
  189.1 4.5 %copy-start.4 = (f32[512,4096]{1,0:T(8,128)}, f32[512,4096]{1,0:T(8,128)S(1)}, u32[]{:S(2)}) copy-start(f32[512,4096]{1,0:T(8,128)S(1)} %fusion.28) | copy-start | bytes 25165828
  189.1 4.5 %copy-start.13 = (s32[256,2]{0,1:T(2,128)S(1)}, s32[256,2]{0,1:T(2,128)}, u32[]{:S(2)}) copy-start(s32[256,2]{0,1:T(2,128)} %param.30) | copy-start | bytes 6148
  193.6 7.5 %collective-permute-start.1 = (f32[256,4096]{1,0:T(8,128)}, f32[256,4096]{1,0:T(8,128)}, u32[]{:S(2)}, u32[]{:S(2)}) collective-permute-start(f32[256,4096]{1,0:T(8,128)} %slice.82), channel_id=1, source_target_pairs={{0,1},{1,0},{2,3},{3,2},{4,5},{5,4},{6,7},{7,6},{8,9},{9,8},{10,11... | collective-permute-start | bytes 12582920 | tf_op jit(solution)/shard_map/ppermute | solution.py:124
  195.8 10.3 %copy-start.15 = (f32[4096]{0:T(1024)S(1)}, f32[4096]{0:T(1024)}, u32[]{:S(2)}) copy-start(f32[4096]{0:T(1024)} %param.28) | copy-start | bytes 49156
  206.1 2.0 copy-start.2
  208.1 78.7 %copy-start.16 = (bf16[1,4096,384]{2,1,0:T(8,128)(2,1)S(1)}, bf16[1,4096,384]{2,1,0:T(8,128)(2,1)}, u32[]{:S(2)}) copy-start(bf16[1,4096,384]{2,1,0:T(8,128)(2,1)} %param.32) | copy-start | bytes 9437188
  208.2 78.7 %copy-start.17 = (bf16[1,4096,384]{2,1,0:T(8,128)(2,1)S(1)}, bf16[1,4096,384]{2,1,0:T(8,128)(2,1)}, u32[]{:S(2)}) copy-start(bf16[1,4096,384]{2,1,0:T(8,128)(2,1)} %param.31) | copy-start | bytes 9437188
  297.3 5.3 %copy-start.18 = (bf16[4096,16]{0,1:T(8,128)(2,1)S(1)}, bf16[4096,16]{0,1:T(8,128)(2,1)}, u32[]{:S(2)}) copy-start(bf16[4096,16]{0,1:T(8,128)(2,1)} %param.29) | copy-start | bytes 393220
  297.3 97.0 %all-to-all-start.3 = ((bf16[16,48,4096]{2,1,0:T(8,128)(2,1)}), bf16[16,48,4096]{2,1,0:T(8,128)(2,1)}, u32[]{:S(2)}, u32[]{:S(2)}) async-start(bf16[16,48,4096]{2,1,0:T(8,128)(2,1)} %bitcast.97), calls=%async_computation.3 | async-start | bytes 12582912 | tf_op jit(solution)/shard_map/all_to_all | solution.py:173
  394.2 5.8 %copy-start.3 = (bf16[256,4096]{1,0:T(8,128)(2,1)S(1)}, bf16[256,4096]{1,0:T(8,128)(2,1)}, u32[]{:S(2)}) copy-start(bf16[256,4096]{1,0:T(8,128)(2,1)} %copy-done.2) | copy-start | bytes 6291460
Sparse Core Ops, SparseCore 0:
  9.4 167.4 all-gather.1
